TPU v7x, 1024 devices: a whole 4x8x16 slice. The times are simulated.
1024 devices in a mesh: tm: 64 (over y, x, z_hi), tensor: 16 (over z_lo, core).
Axes of the slice: x: 4, y: 8, z: 16 (z_hi: 2, z_lo: 8; z = z_hi * 8 + z_lo), core: 2. Of those that a mesh axis runs over, the one named last changes fastest.
Arguments:
- normed: bfloat16 [16384, 1536], P('tm'), may hold values from -24 to 24
- grad_out: bfloat16 [16384, 1536], P('tm'), may hold values from -4 to 4
- w_query: bfloat16 [1536, 1024], P(None, 'tensor'), may hold values from -0.15625 to 0.15625
- w_key: bfloat16 [1536, 1024], P(None, 'tensor'), may hold values from -0.15625 to 0.15625
- w_value: bfloat16 [1536, 1024], P(None, 'tensor'), may hold values from -0.15625 to 0.15625
- w_out: bfloat16 [1024, 1536], P('tensor'), may hold values from -0.1875 to 0.1875
- key_span: int32 [128, 16], replicated, may hold values from 0 to 127, as said below
Outputs:
- dnormed: float32 [16384, 1536], P('tm')
Inputs may be any that keep to these rules, and one draw needn't show every extreme that they name: `key_span`: each reader span names distinct key spans. The key spans named by the 2 reader spans of one tm index lie on 32 distinct tm indices, one span on each, and the spans of each tm index are named by readers of exactly 32 tm indices.
All inputs are finite; a program needn't handle non-finite values.
Results may differ from a plain program's by a relative error of at most 0.014.
The roundings to bfloat16 on the way count: a program that leaves them out, or rounds other values in their place, can miss the bound.
Values may be sent and summed in bfloat16 or wider, within the bound.
No kernel may reach another device: no remote copies, remote signals or barrier semaphores. Data moves between devices by JAX's collectives and lax.ppermute only.
A program may use at most 32 MiB of HBM per device.

v0:
```python
import jax
import jax.numpy as jnp
from jax import lax
from jax.sharding import PartitionSpec as P

HD = 64
SPAN = 128


def attend_grad(query_t, key_t, value_t, dout_t):
    scaling = HD ** (-0.5)
    scores = (
        jnp.einsum("chdq,cjhdk->chqjk", query_t, key_t, preferred_element_type=jnp.float32)
        * scaling
    )
    probs = jax.nn.softmax(scores, axis=(-2, -1))
    probs_b = probs.astype(jnp.bfloat16)
    attn = jnp.einsum("chqjk,cjhdk->chdq", probs_b, value_t, preferred_element_type=jnp.float32)
    delta = jnp.sum(dout_t.astype(jnp.float32) * attn, axis=2)
    dprobs = jnp.einsum("chdq,cjhdk->chqjk", dout_t, value_t, preferred_element_type=jnp.float32)
    dscores_b = (probs * (dprobs - delta[:, :, :, None, None])).astype(jnp.bfloat16)
    grad_query = (
        jnp.einsum("chqjk,cjhdk->chdq", dscores_b, key_t, preferred_element_type=jnp.float32)
        * scaling
    ).astype(jnp.bfloat16)
    grad_key = (
        jnp.einsum("chqjk,chdq->cjhdk", dscores_b, query_t, preferred_element_type=jnp.float32)
        * scaling
    ).astype(jnp.bfloat16)
    grad_value = jnp.einsum(
        "chqjk,chdq->cjhdk", probs_b, dout_t, preferred_element_type=jnp.float32
    ).astype(jnp.bfloat16)
    return (grad_query, grad_key, grad_value)


def project_back(grads_t, weight):
    return lax.dot_general(
        grads_t, weight, (((0,), (1,)), ((), ())), preferred_element_type=jnp.float32
    )


def project_cols(weight, inputs):
    return lax.dot_general(
        weight, inputs, (((0,), (1,)), ((), ())), preferred_element_type=jnp.float32
    )


def local(normed, grad_out, w_query, w_key, w_value, w_out, key_span):
    device_count = lax.axis_size("tm")
    my_index = lax.axis_index("tm")
    row_count = normed.shape[0]
    col_count = w_query.shape[1]
    head_count = col_count // HD
    owned = row_count // SPAN
    per_reader = key_span.shape[1]
    queries_t = project_cols(w_query, normed).astype(jnp.bfloat16)
    keys_t = project_cols(w_key, normed).astype(jnp.bfloat16)
    values_t = project_cols(w_value, normed).astype(jnp.bfloat16)
    dout_t = lax.dot_general(
        w_out, grad_out, (((1,), (1,)), ((), ())), preferred_element_type=jnp.float32
    ).astype(jnp.bfloat16)
    paired_t = jnp.concatenate([keys_t, values_t], axis=0)
    paired_spans = jnp.transpose(paired_t.reshape(2 * col_count, owned, SPAN), (1, 0, 2))
    all_pairs = key_span.reshape(device_count, owned * per_reader)
    hits = all_pairs // owned == my_index
    slot_match = (all_pairs % owned)[:, :, None] == jnp.arange(owned, dtype=jnp.int32)[
        None, None, :
    ]
    picked = jnp.sum((hits[:, :, None] & slot_match).astype(jnp.int32), axis=1).astype(jnp.bfloat16)
    own_ids = lax.dynamic_slice_in_dim(key_span, my_index * owned, owned, 0)
    owner_ids = (own_ids // owned).reshape(-1)
    gathered = lax.all_gather(paired_spans, "tm", axis=0, tiled=True)
    fetched = gathered[own_ids.reshape(-1)]
    fetched = fetched.reshape(owned, per_reader, 2, head_count, HD, SPAN)
    query_rows = jnp.transpose(queries_t.reshape(head_count, HD, owned, SPAN), (2, 0, 1, 3))
    dout_rows = jnp.transpose(dout_t.reshape(head_count, HD, owned, SPAN), (2, 0, 1, 3))
    grad_query, grad_key, grad_value = attend_grad(
        query_rows, fetched[:, :, 0], fetched[:, :, 1], dout_rows
    )
    grad_query_t = jnp.transpose(grad_query, (1, 2, 0, 3)).reshape(col_count, row_count)
    query_term = project_back(grad_query_t, w_query)
    pair_grads = jnp.concatenate(
        [
            grad_key.reshape(owned * per_reader, col_count, SPAN),
            grad_value.reshape(owned * per_reader, col_count, SPAN),
        ],
        axis=1,
    )
    returned = (
        jnp.zeros((device_count, 2 * col_count, SPAN), jnp.bfloat16).at[owner_ids].set(pair_grads)
    )
    received = lax.all_to_all(returned, "tm", split_axis=0, concat_axis=0, tiled=True)
    summed = jnp.einsum("nc,nrh->crh", picked, received, preferred_element_type=jnp.float32).astype(
        jnp.bfloat16
    )
    summed_t = jnp.transpose(summed, (1, 0, 2)).reshape(2 * col_count, row_count)
    kv_term = project_back(summed_t[:col_count], w_key) + project_back(
        summed_t[col_count:], w_value
    )
    result = lax.psum(query_term + kv_term, "tensor")
    return result


def solution(mesh):
    return jax.shard_map(
        local,
        mesh=mesh,
        in_specs=(
            P("tm", None),
            P("tm", None),
            P(None, "tensor"),
            P(None, "tensor"),
            P(None, "tensor"),
            P("tensor", None),
            P(),
        ),
        out_specs=P("tm", None),
        check_vma=False,
    )
```

profile of v0, /device:TPU:1, one launch (start us, length us, event | category | flops | bytes accessed | tf_op | source)
XLA Modules:
  0.0 574.9 jit_solution(4536379292745500856)
XLA Ops:
  6.6 1.1 copy-done
  7.7 1.3 convolution_convert_fusion.4
  8.9 1.3 convolution_convert_fusion.3
  10.2 0.6 bitcast_bitcast_fusion
  12.2 223.3 %all-gather.2.cloned.1.call-done = bf16[128,128,128]{2,1,0:T(8,128)(2,1)} async-done(((bf16[2,128,128]{2,1,0:T(8,128)(2,1)}), bf16[128,128,128]{2,1,0:T(8,128)(2,1)}) %all-gather.2.cloned.1.call-update) | async-done | bytes 4194320 | tf_op jit(solution)/shard_map/all_gather | solution.py:72
  235.5 2.9 gather_fusion
  238.4 0.5 multiply_reduce_fusion
  239.0 0.4 fusion.3
  239.3 0.6 fusion.14
  240.0 0.6 convolution_convert_fusion
  240.6 0.8 multiply_convert_fusion
  241.4 1.0 copy-done.2
  242.4 0.5 fusion.4
  243.0 1.8 broadcast_in_dim.2
  244.8 4.6 scatter_fusion
  249.4 8.0 %all-to-all-start = ((bf16[64,128,128]{2,1,0:T(8,128)(2,1)}), bf16[64,128,128]{2,1,0:T(8,128)(2,1)S(1)}, u32[]{:S(2)}, u32[]{:S(2)}) async-start(bf16[64,128,128]{2,1,0:T(8,128)(2,1)} %scatter_fusion), calls=%async_computation | async-start | bytes 4194304 | tf_op jit(solution)/shard_map/all_to_all | solution.py:92
  257.8 1.7 fusion.15
  259.6 95.6 %all-to-all-done = bf16[64,128,128]{2,1,0:T(8,128)(2,1)S(1)} async-done(((bf16[64,128,128]{2,1,0:T(8,128)(2,1)}), bf16[64,128,128]{2,1,0:T(8,128)(2,1)S(1)}, u32[]{:S(2)}, u32[]{:S(2)}) %all-to-all-start) | async-done | bytes 2097184 | tf_op jit(solution)/shard_map/all_to_all | solution.py:92
  355.2 1.2 fusion.10
  356.5 0.4 fusion.21
  356.9 0.4 convolution_add_fusion
  357.2 1.5 convolution_add_fusion.1
  358.8 206.6 %all-reduce.2.cloned.1.call-done = f32[256,1536]{1,0:T(8,128)} async-done(((f32[256,1536]{1,0:T(8,128)}), f32[256,1536]{1,0:T(8,128)}) %all-reduce.2.cloned.1.call-update) | async-done | bytes 1572880 | tf_op jit(solution)/shard_map/psum | solution.py:100
  565.4 2.7 copy.140
  (41 shorter events, 1.8 us)
Async XLA Ops:
  6.5 1.1 copy-start
  6.5 4.4 copy-start.8
  6.5 4.8 copy-start.7
  6.5 4.8 copy-start.3
  6.5 5.2 copy-start.6
  6.5 228.9 %all-gather.2.cloned.1.call-start = ((), (), s32[]{:S(2)}) async-start(), calls=%async_computation.1 | async-start | bytes 4259840 | tf_op jit(solution)/shard_map/all_gather | solution.py:72
  238.4 2.2 copy-start.1
  241.4 1.0 copy-start.2
  249.4 105.8 %all-to-all-start = ((bf16[64,128,128]{2,1,0:T(8,128)(2,1)}), bf16[64,128,128]{2,1,0:T(8,128)(2,1)S(1)}, u32[]{:S(2)}, u32[]{:S(2)}) async-start(bf16[64,128,128]{2,1,0:T(8,128)(2,1)} %scatter_fusion), calls=%async_computation | async-start | bytes 4194304 | tf_op jit(solution)/shard_map/all_to_all | solution.py:92
  257.4 308.0 %all-reduce.2.cloned.1.call-start = ((), (), s32[]{:S(2)}) async-start(), calls=%async_computation.2 | async-start | bytes 3145728 | tf_op jit(solution)/shard_map/psum | solution.py:100
  257.6 98.9 %copy-start.4 = (bf16[1536,64]{0,1:T(8,128)(2,1)S(1)}, bf16[1536,64]{0,1:T(8,128)(2,1)}, u32[]{:S(2)}) copy-start(bf16[1536,64]{0,1:T(8,128)(2,1)} %param.10) | copy-start | bytes 589828
  259.5 97.3 %copy-start.5 = (bf16[1536,64]{0,1:T(8,128)(2,1)S(1)}, bf16[1536,64]{0,1:T(8,128)(2,1)}, u32[]{:S(2)}) copy-start(bf16[1536,64]{0,1:T(8,128)(2,1)} %param.11) | copy-start | bytes 589828
Sparse Core Ops, SparseCore 0:
  13.2 222.2 all-gather.1
  358.9 206.4 all-reduce.1
where the time goes:
time: 575 us
  waiting for transfers between devices  526 us (91%)
  local copies, waits for them, and re-layouts  14.8 us (3%)
  between operations  13.6 us (2%)
  matrix products  11.6 us (2%)
  starting transfers between devices  8.07 us (1%)
    all_gather x1, waiting for transfers between devices, local(): gathered = lax.all_gather(paired_spans, 'tm', axis=0, tiled=True)  223 us
    psum x1, waiting for transfers between devices, local(): result = lax.psum(query_term + kv_term, 'tensor')  207 us
    all_to_all x1, waiting for transfers between devices, local(): lax.all_to_all(returned, 'tm', split_axis=0, concat_axis=0, tiled=True)  95.6 us
  transfers between devices with their start and end apart: 3, of which 3 were waited for; matrix products, arithmetic and copies ran while one was open for 1% of the time, Pallas kernels for 0%

commit v1 on v0

--- a/solution.py
+++ b/solution.py
@@ -69,8 +69,10 @@
     picked = jnp.sum((hits[:, :, None] & slot_match).astype(jnp.int32), axis=1).astype(jnp.bfloat16)
     own_ids = lax.dynamic_slice_in_dim(key_span, my_index * owned, owned, 0)
     owner_ids = (own_ids // owned).reshape(-1)
-    gathered = lax.all_gather(paired_spans, "tm", axis=0, tiled=True)
-    fetched = gathered[own_ids.reshape(-1)]
+    asked = jnp.sum(jnp.where(hits, all_pairs % owned, 0), axis=1)
+    outgoing = paired_spans[asked]
+    incoming = lax.all_to_all(outgoing, "tm", split_axis=0, concat_axis=0, tiled=True)
+    fetched = incoming[owner_ids]
     fetched = fetched.reshape(owned, per_reader, 2, head_count, HD, SPAN)
     query_rows = jnp.transpose(queries_t.reshape(head_count, HD, owned, SPAN), (2, 0, 1, 3))
     dout_rows = jnp.transpose(dout_t.reshape(head_count, HD, owned, SPAN), (2, 0, 1, 3))

time: 575 us -> 506 us (0.88)
  waiting for transfers between devices: 526 us -> 416 us
  starting transfers between devices: 8.07 us -> 45.6 us
    all_gather x1 -> x0, waiting for transfers between devices: 223 us -> none  [local(): gathered = lax.all_gather(paired_spans, 'tm', axis=0, tiled=True)]
    psum x1, waiting for transfers between devices: 207 us -> 321 us  [local(): result = lax.psum(query_term + kv_term, 'tensor')]
    all_to_all x1, waiting for transfers between devices: 95.6 us -> 49.4 us  [local(): lax.all_to_all(returned, 'tm', split_axis=0, concat_axis=0, tiled=True)]
    all_to_all x0 -> x1, waiting for transfers between devices: none -> 45.9 us  [local(): lax.all_to_all(outgoing, 'tm', split_axis=0, concat_axis=0, tiled=True)]
    all_to_all x0 -> x1, starting transfers between devices: none -> 28.1 us  [local(): lax.all_to_all(outgoing, 'tm', split_axis=0, concat_axis=0, tiled=True)]
    all_to_all x1, starting transfers between devices: 7.99 us -> 17.5 us  [local(): lax.all_to_all(returned, 'tm', split_axis=0, concat_axis=0, tiled=True)]
where the time goes in v1:
time: 506 us
  waiting for transfers between devices  416 us (82%)
  starting transfers between devices  45.6 us (9%)
  local copies, waits for them, and re-layouts  14.7 us (3%)
  matrix products  13.9 us (3%)
  between operations  13.6 us (3%)
    psum x1, waiting for transfers between devices, local(): result = lax.psum(query_term + kv_term, 'tensor')  321 us
    all_to_all x1, waiting for transfers between devices, local(): lax.all_to_all(returned, 'tm', split_axis=0, concat_axis=0, tiled=True)  49.4 us
    all_to_all x1, waiting for transfers between devices, local(): lax.all_to_all(outgoing, 'tm', split_axis=0, concat_axis=0, tiled=True)  45.9 us
    all_to_all x1, starting transfers between devices, local(): lax.all_to_all(outgoing, 'tm', split_axis=0, concat_axis=0, tiled=True)  28.1 us
    all_to_all x1, starting transfers between devices, local(): lax.all_to_all(returned, 'tm', split_axis=0, concat_axis=0, tiled=True)  17.5 us
  transfers between devices with their start and end apart: 3, of which 3 were waited for; matrix products, arithmetic and copies ran while one was open for 1% of the time, Pallas kernels for 0%

profile of v1, /device:TPU:1, one launch (start us, length us, event | category | flops | bytes accessed | tf_op | source)
XLA Modules:
  0.0 505.7 jit_solution(12494802705793266062)
XLA Ops:
  6.5 0.8 fusion.40
  7.7 1.3 convolution_convert_fusion.4
  9.0 1.3 convolution_convert_fusion.3
  10.3 2.2 gather_fusion
  12.4 28.1 %all-to-all-start = ((bf16[64,128,128]{2,1,0:T(8,128)(2,1)}), bf16[64,128,128]{2,1,0:T(8,128)(2,1)S(1)}, u32[]{:S(2)}, u32[]{:S(2)}) async-start(bf16[64,128,128]{2,1,0:T(8,128)(2,1)} %gather_fusion), calls=%async_computation | async-start | bytes 4194304 | tf_op jit(solution)/shard_map/all_to_all | solution.py:74
  40.8 1.5 convolution_convert_fusion.1
  42.8 45.9 %all-to-all-done = bf16[64,128,128]{2,1,0:T(8,128)(2,1)S(1)} async-done(((bf16[64,128,128]{2,1,0:T(8,128)(2,1)}), bf16[64,128,128]{2,1,0:T(8,128)(2,1)S(1)}, u32[]{:S(2)}, u32[]{:S(2)}) %all-to-all-start) | async-done | bytes 2097184 | tf_op jit(solution)/shard_map/all_to_all | solution.py:74
  88.7 1.6 gather_fusion.1
  90.3 1.7 multiply_reduce_fusion
  92.4 0.6 fusion.14
  93.0 0.6 convolution_convert_fusion
  93.6 0.8 multiply_convert_fusion
  94.5 1.0 copy-done.2
  95.4 0.5 fusion.4
  96.0 1.9 broadcast_in_dim.3
  97.9 4.6 scatter_fusion
  102.5 17.5 %all-to-all-start.1 = ((bf16[64,128,128]{2,1,0:T(8,128)(2,1)}), bf16[64,128,128]{2,1,0:T(8,128)(2,1)S(1)}, u32[]{:S(2)}, u32[]{:S(2)}) async-start(bf16[64,128,128]{2,1,0:T(8,128)(2,1)} %scatter_fusion), calls=%async_computation.1 | async-start | bytes 4194304 | tf_op jit(solution)/shard_map/all_to_all | solution.py:94
  120.3 1.7 fusion.15
  122.1 49.4 %all-to-all-done.1 = bf16[64,128,128]{2,1,0:T(8,128)(2,1)S(1)} async-done(((bf16[64,128,128]{2,1,0:T(8,128)(2,1)}), bf16[64,128,128]{2,1,0:T(8,128)(2,1)S(1)}, u32[]{:S(2)}, u32[]{:S(2)}) %all-to-all-start.1) | async-done | bytes 2097184 | tf_op jit(solution)/shard_map/all_to_all | solution.py:94
  171.6 1.2 fusion.10
  173.2 0.4 convolution_add_fusion
  173.6 1.5 convolution_add_fusion.1
  175.2 321.0 %all-reduce.2.cloned.1.call-done = f32[256,1536]{1,0:T(8,128)} async-done(((f32[256,1536]{1,0:T(8,128)}), f32[256,1536]{1,0:T(8,128)}) %all-reduce.2.cloned.1.call-update) | async-done | bytes 1572880 | tf_op jit(solution)/shard_map/psum | solution.py:102
  496.2 2.7 copy.135
  (41 shorter events, 2.3 us)
Async XLA Ops:
  6.5 1.1 copy-start
  12.4 28.2 %copy-start.7 = (s32[128,16]{0,1:T(8,128)S(1)}, s32[128,16]{0,1:T(8,128)}, u32[]{:S(2)}) copy-start(s32[128,16]{0,1:T(8,128)} %param.13) | copy-start | bytes 24580
  12.4 28.4 %copy-start.6 = (bf16[64,1536]{1,0:T(8,128)(2,1)S(1)}, bf16[64,1536]{1,0:T(8,128)(2,1)}, u32[]{:S(2)}) copy-start(bf16[64,1536]{1,0:T(8,128)(2,1)} %param.12) | copy-start | bytes 589828
  12.4 29.9 %copy-start.5 = (bf16[1536,64]{0,1:T(8,128)(2,1)S(1)}, bf16[1536,64]{0,1:T(8,128)(2,1)}, u32[]{:S(2)}) copy-start(bf16[1536,64]{0,1:T(8,128)(2,1)} %param.9) | copy-start | bytes 589828
  12.4 76.2 %all-to-all-start = ((bf16[64,128,128]{2,1,0:T(8,128)(2,1)}), bf16[64,128,128]{2,1,0:T(8,128)(2,1)S(1)}, u32[]{:S(2)}, u32[]{:S(2)}) async-start(bf16[64,128,128]{2,1,0:T(8,128)(2,1)} %gather_fusion), calls=%async_computation | async-start | bytes 4194304 | tf_op jit(solution)/shard_map/all_to_all | solution.py:74
  90.3 2.0 copy-start.1
  94.5 1.0 copy-start.2
  102.5 69.1 %all-to-all-start.1 = ((bf16[64,128,128]{2,1,0:T(8,128)(2,1)}), bf16[64,128,128]{2,1,0:T(8,128)(2,1)S(1)}, u32[]{:S(2)}, u32[]{:S(2)}) async-start(bf16[64,128,128]{2,1,0:T(8,128)(2,1)} %scatter_fusion), calls=%async_computation.1 | async-start | bytes 4194304 | tf_op jit(solution)/shard_map/all_to_all | solution.py:94
  120.0 376.2 %all-reduce.2.cloned.1.call-start = ((), (), s32[]{:S(2)}) async-start(), calls=%async_computation.2 | async-start | bytes 3145728 | tf_op jit(solution)/shard_map/psum | solution.py:102
  120.1 52.7 %copy-start.3 = (bf16[1536,64]{0,1:T(8,128)(2,1)S(1)}, bf16[1536,64]{0,1:T(8,128)(2,1)}, u32[]{:S(2)}) copy-start(bf16[1536,64]{0,1:T(8,128)(2,1)} %param.10) | copy-start | bytes 589828
  122.1 51.2 %copy-start.4 = (bf16[1536,64]{0,1:T(8,128)(2,1)S(1)}, bf16[1536,64]{0,1:T(8,128)(2,1)}, u32[]{:S(2)}) copy-start(bf16[1536,64]{0,1:T(8,128)(2,1)} %param.11) | copy-start | bytes 589828
Sparse Core Ops, SparseCore 0:
  175.3 320.7 all-reduce.1

commit v2 on v1

--- a/solution.py
+++ b/solution.py
@@ -43,6 +43,28 @@
     return lax.dot_general(
         weight, inputs, (((0,), (1,)), ((), ())), preferred_element_type=jnp.float32
     )
+
+
+def head_sum(partial):
+    index = lax.axis_index("tensor")
+    count = lax.axis_size("tensor")
+    cur = partial
+    step = 1
+    while step < count:
+        upper = (index & step) != 0
+        half = cur.shape[0] // 2
+        low, high = cur[:half], cur[half:]
+        keep = jnp.where(upper, high, low)
+        send = jnp.where(upper, low, high)
+        got = lax.ppermute(send, "tensor", [(i, i ^ step) for i in range(count)])
+        cur = keep + got
+        step *= 2
+    while step > 1:
+        step //= 2
+        upper = (index & step) != 0
+        got = lax.ppermute(cur, "tensor", [(i, i ^ step) for i in range(count)])
+        cur = jnp.where(upper, jnp.concatenate([got, cur]), jnp.concatenate([cur, got]))
+    return cur
 
 
 def local(normed, grad_out, w_query, w_key, w_value, w_out, key_span):
@@ -99,7 +121,7 @@
     kv_term = project_back(summed_t[:col_count], w_key) + project_back(
         summed_t[col_count:], w_value
     )
-    result = lax.psum(query_term + kv_term, "tensor")
+    result = head_sum(query_term + kv_term)
     return result
 
 

time: 506 us -> 373 us (0.74)
  waiting for transfers between devices: 416 us -> 166 us
  starting transfers between devices: 45.6 us -> 176 us
  between operations: 13.6 us -> 0.4 us
    psum x1 -> x0, waiting for transfers between devices: 321 us -> none  [local(): result = lax.psum(query_term + kv_term, 'tensor')]
    ppermute x0 -> x8, starting transfers between devices: none -> 130 us  [the longest x4 121 us: head_sum(): got = lax.ppermute(send, 'tensor', [(i, i ^ step) for i in range(count)])]
    ppermute x0 -> x8, waiting for transfers between devices: none -> 71 us  [the longest x4 38 us: head_sum(): got = lax.ppermute(send, 'tensor', [(i, i ^ step) for i in range(count)])]
  transfers between devices with their start and end apart: 3 -> 10, of which waited for: 3 -> 10; matrix products, arithmetic and copies ran while one was open for 1% -> 1% of each run, Pallas kernels for 0% -> 0%
where the time goes in v2:
time: 373 us; the launch traced here: 372 us
  starting transfers between devices  176 us (47%)
  waiting for transfers between devices  166 us (45%)
  matrix products  12.7 us (3%)
  local copies, waits for them, and re-layouts  12.1 us (3%)
  other arithmetic  4.45 us (1%)
    ppermute x4, starting transfers between devices, head_sum(): got = lax.ppermute(send, 'tensor', [(i, i ^ step) for i in range(count)])  121 us
    all_to_all x1, waiting for transfers between devices, local(): lax.all_to_all(returned, 'tm', split_axis=0, concat_axis=0, tiled=True)  49.5 us
    all_to_all x1, waiting for transfers between devices, local(): lax.all_to_all(outgoing, 'tm', split_axis=0, concat_axis=0, tiled=True)  45.9 us
    ppermute x4, waiting for transfers between devices, head_sum(): got = lax.ppermute(send, 'tensor', [(i, i ^ step) for i in range(count)])  38 us
    ppermute x4, waiting for transfers between devices, head_sum(): got = lax.ppermute(cur, 'tensor', [(i, i ^ step) for i in range(count)])  33 us
    all_to_all x1, starting transfers between devices, local(): lax.all_to_all(outgoing, 'tm', split_axis=0, concat_axis=0, tiled=True)  28.1 us
    all_to_all x1, starting transfers between devices, local(): lax.all_to_all(returned, 'tm', split_axis=0, concat_axis=0, tiled=True)  17.4 us
    ppermute x4, starting transfers between devices, head_sum(): got = lax.ppermute(cur, 'tensor', [(i, i ^ step) for i in range(count)])  9.01 us
  transfers between devices with their start and end apart: 10, of which 10 were waited for; matrix products, arithmetic and copies ran while one was open for 1% of the time, Pallas kernels for 0%

profile of v2, /device:TPU:1, one launch (start us, length us, event | category | flops | bytes accessed | tf_op | source)
XLA Modules:
  0.0 371.8 jit_solution(4422121870618549961)
XLA Ops:
  3.7 2.2 gather_fusion
  5.9 28.1 %all-to-all-start = ((bf16[64,128,128]{2,1,0:T(8,128)(2,1)}), bf16[64,128,128]{2,1,0:T(8,128)(2,1)S(1)}, u32[]{:S(2)}, u32[]{:S(2)}) async-start(bf16[64,128,128]{2,1,0:T(8,128)(2,1)} %gather_fusion), calls=%async_computation | async-start | bytes 4194304 | tf_op jit(solution)/shard_map/all_to_all | solution.py:96
  36.2 45.9 %all-to-all-done = bf16[64,128,128]{2,1,0:T(8,128)(2,1)S(1)} async-done(((bf16[64,128,128]{2,1,0:T(8,128)(2,1)}), bf16[64,128,128]{2,1,0:T(8,128)(2,1)S(1)}, u32[]{:S(2)}, u32[]{:S(2)}) %all-to-all-start) | async-done | bytes 2097184 | tf_op jit(solution)/shard_map/all_to_all | solution.py:96
  89.5 1.8 broadcast_in_dim.3
  91.3 4.7 %scatter_fusion = bf16[64,128,128]{2,1,0:T(8,128)(2,1)} fusion(bf16[64,128,128]{2,1,0:T(8,128)(2,1)} %broadcast_in_dim.3, s32[32]{0:T(128)S(1)} %fusion.46, bf16[32,128,128]{2,1,0:T(8,128)(2,1)S(1)} %pad_maximum_fusion), kind=kCustom, calls=%fused_computation.2 | custom fusion | bytes 3145856 | tf_op jit(solution)/shard_map/scatter | solution.py:114
  96.0 17.4 %all-to-all-start.1 = ((bf16[64,128,128]{2,1,0:T(8,128)(2,1)}), bf16[64,128,128]{2,1,0:T(8,128)(2,1)S(1)}, u32[]{:S(2)}, u32[]{:S(2)}) async-start(bf16[64,128,128]{2,1,0:T(8,128)(2,1)} %scatter_fusion), calls=%async_computation.1 | async-start | bytes 4194304 | tf_op jit(solution)/shard_map/all_to_all | solution.py:116
  113.8 1.7 fusion.15
  115.6 49.5 %all-to-all-done.1 = bf16[64,128,128]{2,1,0:T(8,128)(2,1)S(1)} async-done(((bf16[64,128,128]{2,1,0:T(8,128)(2,1)}), bf16[64,128,128]{2,1,0:T(8,128)(2,1)S(1)}, u32[]{:S(2)}, u32[]{:S(2)}) %all-to-all-start.1) | async-done | bytes 2097184 | tf_op jit(solution)/shard_map/all_to_all | solution.py:116
  167.6 2.8 collective-permute-start
  170.5 2.0 collective-permute-done
  173.8 76.0 %collective-permute-start.1 = (f32[64,1536]{1,0:T(8,128)S(1)}, f32[64,1536]{1,0:T(8,128)S(1)}, u32[]{:S(2)}, u32[]{:S(2)}) collective-permute-start(f32[64,1536]{1,0:T(8,128)S(1)} %slice_select_fusion.1), channel_id=1, source_target_pairs={{0,2},{1,3},{2,0},{3,1},{4,6},{5,7},{6,4},{7,5},{8,10},{9,11},{10,... | collective-permute-start | bytes 1179656 | tf_op jit(solution)/shard_map/ppermute | solution.py:59
  249.8 19.0 %collective-permute-done.1 = f32[64,1536]{1,0:T(8,128)S(1)} collective-permute-done((f32[64,1536]{1,0:T(8,128)S(1)}, f32[64,1536]{1,0:T(8,128)S(1)}, u32[]{:S(2)}, u32[]{:S(2)}) %collective-permute-start.1) | collective-permute-done | bytes 393248 | tf_op jit(solution)/shard_map/ppermute | solution.py:59
  268.9 5.9 %collective-permute-start.2 = (f32[32,1536]{1,0:T(8,128)S(1)}, f32[32,1536]{1,0:T(8,128)S(1)}, u32[]{:S(2)}, u32[]{:S(2)}) collective-permute-start(f32[32,1536]{1,0:T(8,128)S(1)} %slice_select_fusion.2), channel_id=1, source_target_pairs={{0,4},{1,5},{2,6},{3,7},{4,0},{5,1},{6,2},{7,3},{8,12},{9,13},{10,... | collective-permute-start | bytes 589832 | tf_op jit(solution)/shard_map/ppermute | solution.py:59
  274.9 9.0 %collective-permute-done.2 = f32[32,1536]{1,0:T(8,128)S(1)} collective-permute-done((f32[32,1536]{1,0:T(8,128)S(1)}, f32[32,1536]{1,0:T(8,128)S(1)}, u32[]{:S(2)}, u32[]{:S(2)}) %collective-permute-start.2) | collective-permute-done | bytes 196640 | tf_op jit(solution)/shard_map/ppermute | solution.py:59
  283.9 36.4 %collective-permute-start.3 = (f32[16,1536]{1,0:T(8,128)S(1)}, f32[16,1536]{1,0:T(8,128)S(1)}, u32[]{:S(2)}, u32[]{:S(2)}) collective-permute-start(f32[16,1536]{1,0:T(8,128)S(1)} %slice_select_fusion.3), channel_id=1, source_target_pairs={{0,8},{1,9},{2,10},{3,11},{4,12},{5,13},{6,14},{7,15},{8,0},{9,1},... | collective-permute-start | bytes 294920 | tf_op jit(solution)/shard_map/ppermute | solution.py:59
  320.3 8.0 %collective-permute-done.3 = f32[16,1536]{1,0:T(8,128)S(1)} collective-permute-done((f32[16,1536]{1,0:T(8,128)S(1)}, f32[16,1536]{1,0:T(8,128)S(1)}, u32[]{:S(2)}, u32[]{:S(2)}) %collective-permute-start.3) | collective-permute-done | bytes 98336 | tf_op jit(solution)/shard_map/ppermute | solution.py:59
  328.3 1.9 collective-permute-start.4
  330.2 12.2 %collective-permute-done.4 = f32[16,1536]{1,0:T(8,128)S(1)} collective-permute-done((f32[16,1536]{1,0:T(8,128)S(1)}, f32[16,1536]{1,0:T(8,128)S(1)}, u32[]{:S(2)}, u32[]{:S(2)}) %collective-permute-start.4) | collective-permute-done | bytes 98336 | tf_op jit(solution)/shard_map/ppermute | solution.py:65
  342.4 1.9 collective-permute-start.5
  344.3 8.8 %collective-permute-done.5 = f32[32,1536]{1,0:T(8,128)S(1)} collective-permute-done((f32[32,1536]{1,0:T(8,128)S(1)}, f32[32,1536]{1,0:T(8,128)S(1)}, u32[]{:S(2)}, u32[]{:S(2)}) %collective-permute-start.5) | collective-permute-done | bytes 196640 | tf_op jit(solution)/shard_map/ppermute | solution.py:65
  353.2 1.9 collective-permute-start.6
  355.1 10.2 %collective-permute-done.6 = f32[64,1536]{1,0:T(8,128)S(1)} collective-permute-done((f32[64,1536]{1,0:T(8,128)S(1)}, f32[64,1536]{1,0:T(8,128)S(1)}, u32[]{:S(2)}, u32[]{:S(2)}) %collective-permute-start.6) | collective-permute-done | bytes 393248 | tf_op jit(solution)/shard_map/ppermute | solution.py:65
  365.3 3.3 collective-permute-start.7
  368.6 1.9 collective-permute-done.7
  (65 shorter events, 18.8 us)
Async XLA Ops:
  0.0 1.1 copy-start
  5.9 28.2 %copy-start.7 = (s32[128,16]{0,1:T(8,128)S(1)}, s32[128,16]{0,1:T(8,128)}, u32[]{:S(2)}) copy-start(s32[128,16]{0,1:T(8,128)} %param.13) | copy-start | bytes 24580
  5.9 28.4 %copy-start.6 = (bf16[64,1536]{1,0:T(8,128)(2,1)S(1)}, bf16[64,1536]{1,0:T(8,128)(2,1)}, u32[]{:S(2)}) copy-start(bf16[64,1536]{1,0:T(8,128)(2,1)} %param.12) | copy-start | bytes 589828
  5.9 29.9 %copy-start.5 = (bf16[1536,64]{0,1:T(8,128)(2,1)S(1)}, bf16[1536,64]{0,1:T(8,128)(2,1)}, u32[]{:S(2)}) copy-start(bf16[1536,64]{0,1:T(8,128)(2,1)} %param.9) | copy-start | bytes 589828
  5.9 76.2 %all-to-all-start = ((bf16[64,128,128]{2,1,0:T(8,128)(2,1)}), bf16[64,128,128]{2,1,0:T(8,128)(2,1)S(1)}, u32[]{:S(2)}, u32[]{:S(2)}) async-start(bf16[64,128,128]{2,1,0:T(8,128)(2,1)} %gather_fusion), calls=%async_computation | async-start | bytes 4194304 | tf_op jit(solution)/shard_map/all_to_all | solution.py:96
  83.8 2.0 copy-start.1
  87.9 1.0 copy-start.2
  96.0 69.0 %all-to-all-start.1 = ((bf16[64,128,128]{2,1,0:T(8,128)(2,1)}), bf16[64,128,128]{2,1,0:T(8,128)(2,1)S(1)}, u32[]{:S(2)}, u32[]{:S(2)}) async-start(bf16[64,128,128]{2,1,0:T(8,128)(2,1)} %scatter_fusion), calls=%async_computation.1 | async-start | bytes 4194304 | tf_op jit(solution)/shard_map/all_to_all | solution.py:116
  113.6 52.8 %copy-start.3 = (bf16[1536,64]{0,1:T(8,128)(2,1)S(1)}, bf16[1536,64]{0,1:T(8,128)(2,1)}, u32[]{:S(2)}) copy-start(bf16[1536,64]{0,1:T(8,128)(2,1)} %param.10) | copy-start | bytes 589828
  115.5 51.2 %copy-start.4 = (bf16[1536,64]{0,1:T(8,128)(2,1)S(1)}, bf16[1536,64]{0,1:T(8,128)(2,1)}, u32[]{:S(2)}) copy-start(bf16[1536,64]{0,1:T(8,128)(2,1)} %param.11) | copy-start | bytes 589828
  167.6 4.8 %collective-permute-start = (f32[128,1536]{1,0:T(8,128)S(1)}, f32[128,1536]{1,0:T(8,128)}, u32[]{:S(2)}, u32[]{:S(2)}) collective-permute-start(f32[128,1536]{1,0:T(8,128)S(1)} %slice_select_fusion), channel_id=1, source_target_pairs={{0,1},{1,0},{2,3},{3,2},{4,5},{5,4},{6,7},{7,6},{8,9},{9,8},{10,11... | collective-permute-start | bytes 2359304 | tf_op jit(solution)/shard_map/ppermute | solution.py:59
  173.8 95.0 %collective-permute-start.1 = (f32[64,1536]{1,0:T(8,128)S(1)}, f32[64,1536]{1,0:T(8,128)S(1)}, u32[]{:S(2)}, u32[]{:S(2)}) collective-permute-start(f32[64,1536]{1,0:T(8,128)S(1)} %slice_select_fusion.1), channel_id=1, source_target_pairs={{0,2},{1,3},{2,0},{3,1},{4,6},{5,7},{6,4},{7,5},{8,10},{9,11},{10,... | collective-permute-start | bytes 1179656 | tf_op jit(solution)/shard_map/ppermute | solution.py:59
  268.9 14.9 %collective-permute-start.2 = (f32[32,1536]{1,0:T(8,128)S(1)}, f32[32,1536]{1,0:T(8,128)S(1)}, u32[]{:S(2)}, u32[]{:S(2)}) collective-permute-start(f32[32,1536]{1,0:T(8,128)S(1)} %slice_select_fusion.2), channel_id=1, source_target_pairs={{0,4},{1,5},{2,6},{3,7},{4,0},{5,1},{6,2},{7,3},{8,12},{9,13},{10,... | collective-permute-start | bytes 589832 | tf_op jit(solution)/shard_map/ppermute | solution.py:59
  283.9 44.3 %collective-permute-start.3 = (f32[16,1536]{1,0:T(8,128)S(1)}, f32[16,1536]{1,0:T(8,128)S(1)}, u32[]{:S(2)}, u32[]{:S(2)}) collective-permute-start(f32[16,1536]{1,0:T(8,128)S(1)} %slice_select_fusion.3), channel_id=1, source_target_pairs={{0,8},{1,9},{2,10},{3,11},{4,12},{5,13},{6,14},{7,15},{8,0},{9,1},... | collective-permute-start | bytes 294920 | tf_op jit(solution)/shard_map/ppermute | solution.py:59
  328.3 14.1 %collective-permute-start.4 = (f32[16,1536]{1,0:T(8,128)S(1)}, f32[16,1536]{1,0:T(8,128)S(1)}, u32[]{:S(2)}, u32[]{:S(2)}) collective-permute-start(f32[16,1536]{1,0:T(8,128)S(1)} %select_add_fusion.3), channel_id=1, source_target_pairs={{0,8},{1,9},{2,10},{3,11},{4,12},{5,13},{6,14},{7,15},{8,0},{9,1},... | collective-permute-start | bytes 294920 | tf_op jit(solution)/shard_map/ppermute | solution.py:65
  342.4 10.7 %collective-permute-start.5 = (f32[32,1536]{1,0:T(8,128)S(1)}, f32[32,1536]{1,0:T(8,128)S(1)}, u32[]{:S(2)}, u32[]{:S(2)}) collective-permute-start(f32[32,1536]{1,0:T(8,128)S(1)} %maximum_select_fusion.3), channel_id=1, source_target_pairs={{0,4},{1,5},{2,6},{3,7},{4,0},{5,1},{6,2},{7,3},{8,12},{9,13},{10,... | collective-permute-start | bytes 589832 | tf_op jit(solution)/shard_map/ppermute | solution.py:65
  353.2 12.1 %collective-permute-start.6 = (f32[64,1536]{1,0:T(8,128)S(1)}, f32[64,1536]{1,0:T(8,128)S(1)}, u32[]{:S(2)}, u32[]{:S(2)}) collective-permute-start(f32[64,1536]{1,0:T(8,128)S(1)} %maximum_select_fusion.2), channel_id=1, source_target_pairs={{0,2},{1,3},{2,0},{3,1},{4,6},{5,7},{6,4},{7,5},{8,10},{9,11},{10,... | collective-permute-start | bytes 1179656 | tf_op jit(solution)/shard_map/ppermute | solution.py:65
  365.3 5.2 %collective-permute-start.7 = (f32[128,1536]{1,0:T(8,128)S(1)}, f32[128,1536]{1,0:T(8,128)S(1)}, u32[]{:S(2)}, u32[]{:S(2)}) collective-permute-start(f32[128,1536]{1,0:T(8,128)S(1)} %maximum_select_fusion.1), channel_id=1, source_target_pairs={{0,1},{1,0},{2,3},{3,2},{4,5},{5,4},{6,7},{7,6},{8,9},{9,8},{10,11... | collective-permute-start | bytes 2359304 | tf_op jit(solution)/shard_map/ppermute | solution.py:65

commit v3 on v2

--- a/solution.py
+++ b/solution.py
@@ -1,7 +1,7 @@
 import jax
 import jax.numpy as jnp
 from jax import lax
-from jax.sharding import PartitionSpec as P
+from jax.sharding import Mesh, PartitionSpec as P
 
 HD = 64
 SPAN = 128
@@ -68,8 +68,13 @@
 
 
 def local(normed, grad_out, w_query, w_key, w_value, w_out, key_span):
-    device_count = lax.axis_size("tm")
-    my_index = lax.axis_index("tm")
+    column_count = lax.axis_size("tq")
+    side_count = lax.axis_size("zh")
+    my_column = lax.axis_index("tq")
+    my_side = lax.axis_index("zh")
+    device_count = column_count * side_count
+    my_index = my_column * side_count + my_side
+    swap = [(0, 1), (1, 0)]
     row_count = normed.shape[0]
     col_count = w_query.shape[1]
     head_count = col_count // HD
@@ -83,17 +88,23 @@
     ).astype(jnp.bfloat16)
     paired_t = jnp.concatenate([keys_t, values_t], axis=0)
     paired_spans = jnp.transpose(paired_t.reshape(2 * col_count, owned, SPAN), (1, 0, 2))
-    all_pairs = key_span.reshape(device_count, owned * per_reader)
-    hits = all_pairs // owned == my_index
-    slot_match = (all_pairs % owned)[:, :, None] == jnp.arange(owned, dtype=jnp.int32)[
-        None, None, :
-    ]
-    picked = jnp.sum((hits[:, :, None] & slot_match).astype(jnp.int32), axis=1).astype(jnp.bfloat16)
+    mirror_spans = lax.ppermute(paired_spans, "zh", swap)
+    have = jnp.where(
+        my_side == 0,
+        jnp.concatenate([paired_spans, mirror_spans]),
+        jnp.concatenate([mirror_spans, paired_spans]),
+    )
+    all_pairs = key_span.reshape(column_count, side_count, owned * per_reader)
+    requests = lax.dynamic_index_in_dim(all_pairs, my_side, axis=1, keepdims=False)
+    sides = my_column * side_count + jnp.arange(side_count, dtype=jnp.int32)
+    hit = (requests // owned)[:, :, None] == sides[None, None, :]
+    slot = jnp.sum(jnp.where(hit, (requests % owned)[:, :, None], 0), axis=1)
+    exists = jnp.any(hit, axis=1)
+    which = jnp.arange(side_count, dtype=jnp.int32)[None, :] * owned + slot
+    outgoing = have[which.reshape(-1)]
+    incoming = lax.all_to_all(outgoing, "tq", split_axis=0, concat_axis=0, tiled=True)
     own_ids = lax.dynamic_slice_in_dim(key_span, my_index * owned, owned, 0)
     owner_ids = (own_ids // owned).reshape(-1)
-    asked = jnp.sum(jnp.where(hits, all_pairs % owned, 0), axis=1)
-    outgoing = paired_spans[asked]
-    incoming = lax.all_to_all(outgoing, "tm", split_axis=0, concat_axis=0, tiled=True)
     fetched = incoming[owner_ids]
     fetched = fetched.reshape(owned, per_reader, 2, head_count, HD, SPAN)
     query_rows = jnp.transpose(queries_t.reshape(head_count, HD, owned, SPAN), (2, 0, 1, 3))
@@ -113,10 +124,15 @@
     returned = (
         jnp.zeros((device_count, 2 * col_count, SPAN), jnp.bfloat16).at[owner_ids].set(pair_grads)
     )
-    received = lax.all_to_all(returned, "tm", split_axis=0, concat_axis=0, tiled=True)
-    summed = jnp.einsum("nc,nrh->crh", picked, received, preferred_element_type=jnp.float32).astype(
-        jnp.bfloat16
-    )
+    received = lax.all_to_all(returned, "tq", split_axis=0, concat_axis=0, tiled=True)
+    received = received.reshape(column_count, side_count, 2 * col_count, SPAN)
+    picked = (
+        exists[:, :, None] & (slot[:, :, None] == jnp.arange(owned, dtype=jnp.int32)[None, None, :])
+    ).astype(jnp.bfloat16)
+    partial = jnp.einsum("csk,csrh->skrh", picked, received, preferred_element_type=jnp.float32)
+    mine = lax.dynamic_index_in_dim(partial, my_side, axis=0, keepdims=False)
+    other = lax.dynamic_index_in_dim(partial, 1 - my_side, axis=0, keepdims=False)
+    summed = (mine + lax.ppermute(other, "zh", swap)).astype(jnp.bfloat16)
     summed_t = jnp.transpose(summed, (1, 0, 2)).reshape(2 * col_count, row_count)
     kv_term = project_back(summed_t[:col_count], w_key) + project_back(
         summed_t[col_count:], w_value
@@ -126,18 +142,22 @@
 
 
 def solution(mesh):
+    tm_size = mesh.shape["tm"]
+    tensor_size = mesh.shape["tensor"]
+    split = Mesh(mesh.devices.reshape(tm_size // 2, 2, tensor_size), ("tq", "zh", "tensor"))
+    rows = P(("tq", "zh"), None)
     return jax.shard_map(
         local,
-        mesh=mesh,
+        mesh=split,
         in_specs=(
-            P("tm", None),
-            P("tm", None),
+            rows,
+            rows,
             P(None, "tensor"),
             P(None, "tensor"),
             P(None, "tensor"),
             P("tensor", None),
             P(),
         ),
-        out_specs=P("tm", None),
+        out_specs=rows,
         check_vma=False,
     )

time: 373 us -> 271 us (0.73)
  starting transfers between devices: 176 us -> 87.2 us
  waiting for transfers between devices: 166 us -> 153 us
    ppermute x4, starting transfers between devices: 121 us -> 28.1 us  [head_sum(): got = lax.ppermute(send, 'tensor', [(i, i ^ step) for i in range(count)])]
    ppermute x0 -> x2, starting transfers between devices: none -> 32.1 us  [the longest x1 19.9 us: local(): mirror_spans = lax.ppermute(paired_spans, 'zh', swap)]
    all_to_all x2, starting transfers between devices: 45.5 us -> 17.9 us  [the longest x1 9.8 us: local(): lax.all_to_all(outgoing, 'tq', split_axis=0, concat_axis=0, tiled=True)]
    ppermute x4, waiting for transfers between devices: 38 us -> 28.6 us  [head_sum(): got = lax.ppermute(send, 'tensor', [(i, i ^ step) for i in range(count)])]
    all_to_all x2, waiting for transfers between devices: 95.4 us -> 88.4 us  [the longest x1 45.5 us: local(): lax.all_to_all(returned, 'tq', split_axis=0, concat_axis=0, tiled=True)]
  transfers between devices with their start and end apart: 10 -> 12, of which waited for: 10 -> 12; matrix products, arithmetic and copies ran while one was open for 1% -> 1% of each run, Pallas kernels for 0% -> 0%
where the time goes in v3:
time: 271 us; the launch traced here: 269 us
  waiting for transfers between devices  153 us (56%)
  starting transfers between devices  87.2 us (32%)
  local copies, waits for them, and re-layouts  13.1 us (5%)
  matrix products  11.3 us (4%)
  other arithmetic  4.02 us (1%)
    all_to_all x1, waiting for transfers between devices, local(): lax.all_to_all(returned, 'tq', split_axis=0, concat_axis=0, tiled=True)  45.5 us
    all_to_all x1, waiting for transfers between devices, local(): lax.all_to_all(outgoing, 'tq', split_axis=0, concat_axis=0, tiled=True)  42.9 us
    ppermute x4, waiting for transfers between devices, head_sum(): got = lax.ppermute(cur, 'tensor', [(i, i ^ step) for i in range(count)])  33 us
    ppermute x4, waiting for transfers between devices, head_sum(): got = lax.ppermute(send, 'tensor', [(i, i ^ step) for i in range(count)])  28.6 us
    ppermute x4, starting transfers between devices, head_sum(): got = lax.ppermute(send, 'tensor', [(i, i ^ step) for i in range(count)])  28.1 us
    ppermute x1, starting transfers between devices, local(): mirror_spans = lax.ppermute(paired_spans, 'zh', swap)  19.9 us
    ppermute x1, starting transfers between devices, local(): summed = (mine + lax.ppermute(other, 'zh', swap)).astype(jnp.bfloat16)  12.2 us
    all_to_all x1, starting transfers between devices, local(): lax.all_to_all(outgoing, 'tq', split_axis=0, concat_axis=0, tiled=True)  9.8 us
  transfers between devices with their start and end apart: 12, of which 12 were waited for; matrix products, arithmetic and copies ran while one was open for 1% of the time, Pallas kernels for 0%

profile of v3, /device:TPU:1, one launch (start us, length us, event | category | flops | bytes accessed | tf_op | source)
XLA Modules:
  0.0 269.1 jit_solution(11502755305615864888)
XLA Ops:
  3.7 19.9 %collective-permute-start = (bf16[2,128,128]{2,1,0:T(8,128)(2,1)S(1)}, bf16[2,128,128]{2,1,0:T(8,128)(2,1)S(1)}, u32[]{:S(2)}, u32[]{:S(2)}) collective-permute-start(bf16[2,128,128]{2,1,0:T(8,128)(2,1)S(1)} %bitcast_bitcast_fusion), channel_id=1, source_target_pairs={{0,16},{16,0},{1,17},{17,1},{2,18},{18,2},{3,19},{19,3},{4,20},{20... | collective-permute-start | bytes 196616 | tf_op jit(solution)/shard_map/ppermute | solution.py:91
  25.5 2.1 gather_fusion
  27.6 9.8 %all-to-all-start = ((bf16[64,128,128]{2,1,0:T(8,128)(2,1)}), bf16[64,128,128]{2,1,0:T(8,128)(2,1)S(1)}, u32[]{:S(2)}, u32[]{:S(2)}) async-start(bf16[64,128,128]{2,1,0:T(8,128)(2,1)} %gather_fusion), calls=%async_computation | async-start | bytes 4194304 | tf_op jit(solution)/shard_map/all_to_all | solution.py:105
  39.6 42.9 %all-to-all-done = bf16[64,128,128]{2,1,0:T(8,128)(2,1)S(1)} async-done(((bf16[64,128,128]{2,1,0:T(8,128)(2,1)}), bf16[64,128,128]{2,1,0:T(8,128)(2,1)S(1)}, u32[]{:S(2)}, u32[]{:S(2)}) %all-to-all-start) | async-done | bytes 2097184 | tf_op jit(solution)/shard_map/all_to_all | solution.py:105
  91.6 4.6 %scatter_fusion = bf16[64,128,128]{2,1,0:T(8,128)(2,1)} fusion(bf16[64,128,128]{2,1,0:T(8,128)(2,1)} %broadcast_in_dim.16, s32[32]{0:T(128)S(1)} %fusion.42, bf16[32,128,128]{2,1,0:T(8,128)(2,1)S(1)} %pad_maximum_fusion), kind=kCustom, calls=%fused_computation.2 | custom fusion | bytes 3145856 | tf_op jit(solution)/shard_map/scatter | solution.py:125
  96.3 8.1 %all-to-all-start.1 = ((bf16[64,128,128]{2,1,0:T(8,128)(2,1)}), bf16[64,128,128]{2,1,0:T(8,128)(2,1)S(1)}, u32[]{:S(2)}, u32[]{:S(2)}) async-start(bf16[64,128,128]{2,1,0:T(8,128)(2,1)} %scatter_fusion), calls=%async_computation.1 | async-start | bytes 4194304 | tf_op jit(solution)/shard_map/all_to_all | solution.py:127
  104.6 45.5 %all-to-all-done.1 = bf16[64,128,128]{2,1,0:T(8,128)(2,1)S(1)} async-done(((bf16[64,128,128]{2,1,0:T(8,128)(2,1)}), bf16[64,128,128]{2,1,0:T(8,128)(2,1)S(1)}, u32[]{:S(2)}, u32[]{:S(2)}) %all-to-all-start.1) | async-done | bytes 2097184 | tf_op jit(solution)/shard_map/all_to_all | solution.py:127
  151.4 12.2 %collective-permute-start.1 = (f32[2,128,128]{2,0,1:T(2,128)S(1)}, f32[2,128,128]{2,0,1:T(2,128)S(1)}, u32[]{:S(2)}, u32[]{:S(2)}) collective-permute-start(f32[2,128,128]{2,0,1:T(2,128)S(1)} %dynamic-slice_bitcast_fusion), channel_id=1, source_target_pairs={{0,16},{16,0},{1,17},{17,1},{2,18},{18,2},{3,19},{19,3},{4,20},{20... | collective-permute-start | bytes 393224 | tf_op jit(solution)/shard_map/ppermute | solution.py:135
  164.0 2.0 collective-permute-done.1
  167.4 8.7 %collective-permute-start.2 = (f32[128,1536]{1,0:T(8,128)S(1)}, f32[128,1536]{1,0:T(8,128)}, u32[]{:S(2)}, u32[]{:S(2)}) collective-permute-start(f32[128,1536]{1,0:T(8,128)S(1)} %slice_select_fusion), channel_id=1, source_target_pairs={{0,1},{1,0},{2,3},{3,2},{4,5},{5,4},{6,7},{7,6},{8,9},{9,8},{10,11... | collective-permute-start | bytes 2359304 | tf_op jit(solution)/shard_map/ppermute | solution.py:59
  176.1 2.0 collective-permute-done.2
  179.5 7.5 %collective-permute-start.3 = (f32[64,1536]{1,0:T(8,128)S(1)}, f32[64,1536]{1,0:T(8,128)S(1)}, u32[]{:S(2)}, u32[]{:S(2)}) collective-permute-start(f32[64,1536]{1,0:T(8,128)S(1)} %slice_select_fusion.1), channel_id=1, source_target_pairs={{0,2},{1,3},{2,0},{3,1},{4,6},{5,7},{6,4},{7,5},{8,10},{9,11},{10,... | collective-permute-start | bytes 1179656 | tf_op jit(solution)/shard_map/ppermute | solution.py:59
  187.0 9.1 %collective-permute-done.3 = f32[64,1536]{1,0:T(8,128)S(1)} collective-permute-done((f32[64,1536]{1,0:T(8,128)S(1)}, f32[64,1536]{1,0:T(8,128)S(1)}, u32[]{:S(2)}, u32[]{:S(2)}) %collective-permute-start.3) | collective-permute-done | bytes 393248 | tf_op jit(solution)/shard_map/ppermute | solution.py:59
  196.2 3.4 %collective-permute-start.4 = (f32[32,1536]{1,0:T(8,128)S(1)}, f32[32,1536]{1,0:T(8,128)S(1)}, u32[]{:S(2)}, u32[]{:S(2)}) collective-permute-start(f32[32,1536]{1,0:T(8,128)S(1)} %slice_select_fusion.2), channel_id=1, source_target_pairs={{0,4},{1,5},{2,6},{3,7},{4,0},{5,1},{6,2},{7,3},{8,12},{9,13},{10,... | collective-permute-start | bytes 589832 | tf_op jit(solution)/shard_map/ppermute | solution.py:59
  199.6 9.5 %collective-permute-done.4 = f32[32,1536]{1,0:T(8,128)S(1)} collective-permute-done((f32[32,1536]{1,0:T(8,128)S(1)}, f32[32,1536]{1,0:T(8,128)S(1)}, u32[]{:S(2)}, u32[]{:S(2)}) %collective-permute-start.4) | collective-permute-done | bytes 196640 | tf_op jit(solution)/shard_map/ppermute | solution.py:59
  209.2 8.5 %collective-permute-start.5 = (f32[16,1536]{1,0:T(8,128)S(1)}, f32[16,1536]{1,0:T(8,128)S(1)}, u32[]{:S(2)}, u32[]{:S(2)}) collective-permute-start(f32[16,1536]{1,0:T(8,128)S(1)} %slice_select_fusion.3), channel_id=1, source_target_pairs={{0,8},{1,9},{2,10},{3,11},{4,12},{5,13},{6,14},{7,15},{8,0},{9,1},... | collective-permute-start | bytes 294920 | tf_op jit(solution)/shard_map/ppermute | solution.py:59
  217.6 8.0 %collective-permute-done.5 = f32[16,1536]{1,0:T(8,128)S(1)} collective-permute-done((f32[16,1536]{1,0:T(8,128)S(1)}, f32[16,1536]{1,0:T(8,128)S(1)}, u32[]{:S(2)}, u32[]{:S(2)}) %collective-permute-start.5) | collective-permute-done | bytes 98336 | tf_op jit(solution)/shard_map/ppermute | solution.py:59
  225.6 1.9 collective-permute-start.6
  227.5 12.2 %collective-permute-done.6 = f32[16,1536]{1,0:T(8,128)S(1)} collective-permute-done((f32[16,1536]{1,0:T(8,128)S(1)}, f32[16,1536]{1,0:T(8,128)S(1)}, u32[]{:S(2)}, u32[]{:S(2)}) %collective-permute-start.6) | collective-permute-done | bytes 98336 | tf_op jit(solution)/shard_map/ppermute | solution.py:65
  239.8 1.9 collective-permute-start.7
  241.7 8.8 %collective-permute-done.7 = f32[32,1536]{1,0:T(8,128)S(1)} collective-permute-done((f32[32,1536]{1,0:T(8,128)S(1)}, f32[32,1536]{1,0:T(8,128)S(1)}, u32[]{:S(2)}, u32[]{:S(2)}) %collective-permute-start.7) | collective-permute-done | bytes 196640 | tf_op jit(solution)/shard_map/ppermute | solution.py:65
  250.5 1.9 collective-permute-start.8
  252.5 10.2 %collective-permute-done.8 = f32[64,1536]{1,0:T(8,128)S(1)} collective-permute-done((f32[64,1536]{1,0:T(8,128)S(1)}, f32[64,1536]{1,0:T(8,128)S(1)}, u32[]{:S(2)}, u32[]{:S(2)}) %collective-permute-start.8) | collective-permute-done | bytes 393248 | tf_op jit(solution)/shard_map/ppermute | solution.py:65
  262.7 3.3 %collective-permute-start.9 = (f32[128,1536]{1,0:T(8,128)S(1)}, f32[128,1536]{1,0:T(8,128)S(1)}, u32[]{:S(2)}, u32[]{:S(2)}) collective-permute-start(f32[128,1536]{1,0:T(8,128)S(1)} %maximum_select_fusion.1), channel_id=1, source_target_pairs={{0,1},{1,0},{2,3},{3,2},{4,5},{5,4},{6,7},{7,6},{8,9},{9,8},{10,11... | collective-permute-start | bytes 2359304 | tf_op jit(solution)/shard_map/ppermute | solution.py:65
  (78 shorter events, 24.6 us)
Async XLA Ops:
  0.0 1.1 copy-start
  0.0 23.7 %copy-start.9 = (s32[128,16]{0,1:T(8,128)S(1)}, s32[128,16]{0,1:T(8,128)}, u32[]{:S(2)}) copy-start(s32[128,16]{0,1:T(8,128)} %param.13) | copy-start | bytes 24580
  3.7 21.7 %collective-permute-start = (bf16[2,128,128]{2,1,0:T(8,128)(2,1)S(1)}, bf16[2,128,128]{2,1,0:T(8,128)(2,1)S(1)}, u32[]{:S(2)}, u32[]{:S(2)}) collective-permute-start(bf16[2,128,128]{2,1,0:T(8,128)(2,1)S(1)} %bitcast_bitcast_fusion), channel_id=1, source_target_pairs={{0,16},{16,0},{1,17},{17,1},{2,18},{18,2},{3,19},{19,3},{4,20},{20... | collective-permute-start | bytes 196616 | tf_op jit(solution)/shard_map/ppermute | solution.py:91
  27.6 10.1 %copy-start.8 = (bf16[64,1536]{1,0:T(8,128)(2,1)S(1)}, bf16[64,1536]{1,0:T(8,128)(2,1)}, u32[]{:S(2)}) copy-start(bf16[64,1536]{1,0:T(8,128)(2,1)} %param.12) | copy-start | bytes 589828
  27.6 11.6 %copy-start.7 = (bf16[1536,64]{0,1:T(8,128)(2,1)S(1)}, bf16[1536,64]{0,1:T(8,128)(2,1)}, u32[]{:S(2)}) copy-start(bf16[1536,64]{0,1:T(8,128)(2,1)} %param.9) | copy-start | bytes 589828
  27.6 54.8 %all-to-all-start = ((bf16[64,128,128]{2,1,0:T(8,128)(2,1)}), bf16[64,128,128]{2,1,0:T(8,128)(2,1)S(1)}, u32[]{:S(2)}, u32[]{:S(2)}) async-start(bf16[64,128,128]{2,1,0:T(8,128)(2,1)} %gather_fusion), calls=%async_computation | async-start | bytes 4194304 | tf_op jit(solution)/shard_map/all_to_all | solution.py:105
  84.1 2.0 copy-start.1
  88.2 1.0 copy-start.3
  96.3 53.9 %all-to-all-start.1 = ((bf16[64,128,128]{2,1,0:T(8,128)(2,1)}), bf16[64,128,128]{2,1,0:T(8,128)(2,1)S(1)}, u32[]{:S(2)}, u32[]{:S(2)}) async-start(bf16[64,128,128]{2,1,0:T(8,128)(2,1)} %scatter_fusion), calls=%async_computation.1 | async-start | bytes 4194304 | tf_op jit(solution)/shard_map/all_to_all | solution.py:127
  150.1 13.5 %copy-start.2 = (bf16[32,128,128]{2,1,0:T(8,128)(2,1)S(1)}, bf16[32,128,128]{2,1,0:T(8,128)(2,1)}, u32[]{:S(2)}) copy-start(bf16[32,128,128]{2,1,0:T(8,128)(2,1)} %gather_fusion.1) | copy-start | bytes 3145732
  150.1 13.5 %copy-start.4 = (bf16[2,128,16,128]{1,3,2,0:T(8,128)(2,1)S(1)}, bf16[2,128,16,128]{1,3,2,0:T(8,128)(2,1)}, u32[]{:S(2)}) copy-start(bf16[2,128,16,128]{1,3,2,0:T(8,128)(2,1)} %copy-done.3) | copy-start | bytes 3145732
  150.1 16.0 %copy-start.5 = (bf16[1536,64]{0,1:T(8,128)(2,1)S(1)}, bf16[1536,64]{0,1:T(8,128)(2,1)}, u32[]{:S(2)}) copy-start(bf16[1536,64]{0,1:T(8,128)(2,1)} %param.10) | copy-start | bytes 589828
  151.4 15.1 %copy-start.6 = (bf16[1536,64]{0,1:T(8,128)(2,1)S(1)}, bf16[1536,64]{0,1:T(8,128)(2,1)}, u32[]{:S(2)}) copy-start(bf16[1536,64]{0,1:T(8,128)(2,1)} %param.11) | copy-start | bytes 589828
  151.4 14.6 %collective-permute-start.1 = (f32[2,128,128]{2,0,1:T(2,128)S(1)}, f32[2,128,128]{2,0,1:T(2,128)S(1)}, u32[]{:S(2)}, u32[]{:S(2)}) collective-permute-start(f32[2,128,128]{2,0,1:T(2,128)S(1)} %dynamic-slice_bitcast_fusion), channel_id=1, source_target_pairs={{0,16},{16,0},{1,17},{17,1},{2,18},{18,2},{3,19},{19,3},{4,20},{20... | collective-permute-start | bytes 393224 | tf_op jit(solution)/shard_map/ppermute | solution.py:135
  167.4 10.8 %collective-permute-start.2 = (f32[128,1536]{1,0:T(8,128)S(1)}, f32[128,1536]{1,0:T(8,128)}, u32[]{:S(2)}, u32[]{:S(2)}) collective-permute-start(f32[128,1536]{1,0:T(8,128)S(1)} %slice_select_fusion), channel_id=1, source_target_pairs={{0,1},{1,0},{2,3},{3,2},{4,5},{5,4},{6,7},{7,6},{8,9},{9,8},{10,11... | collective-permute-start | bytes 2359304 | tf_op jit(solution)/shard_map/ppermute | solution.py:59
  179.5 16.6 %collective-permute-start.3 = (f32[64,1536]{1,0:T(8,128)S(1)}, f32[64,1536]{1,0:T(8,128)S(1)}, u32[]{:S(2)}, u32[]{:S(2)}) collective-permute-start(f32[64,1536]{1,0:T(8,128)S(1)} %slice_select_fusion.1), channel_id=1, source_target_pairs={{0,2},{1,3},{2,0},{3,1},{4,6},{5,7},{6,4},{7,5},{8,10},{9,11},{10,... | collective-permute-start | bytes 1179656 | tf_op jit(solution)/shard_map/ppermute | solution.py:59
  196.2 12.9 %collective-permute-start.4 = (f32[32,1536]{1,0:T(8,128)S(1)}, f32[32,1536]{1,0:T(8,128)S(1)}, u32[]{:S(2)}, u32[]{:S(2)}) collective-permute-start(f32[32,1536]{1,0:T(8,128)S(1)} %slice_select_fusion.2), channel_id=1, source_target_pairs={{0,4},{1,5},{2,6},{3,7},{4,0},{5,1},{6,2},{7,3},{8,12},{9,13},{10,... | collective-permute-start | bytes 589832 | tf_op jit(solution)/shard_map/ppermute | solution.py:59
  209.2 16.4 %collective-permute-start.5 = (f32[16,1536]{1,0:T(8,128)S(1)}, f32[16,1536]{1,0:T(8,128)S(1)}, u32[]{:S(2)}, u32[]{:S(2)}) collective-permute-start(f32[16,1536]{1,0:T(8,128)S(1)} %slice_select_fusion.3), channel_id=1, source_target_pairs={{0,8},{1,9},{2,10},{3,11},{4,12},{5,13},{6,14},{7,15},{8,0},{9,1},... | collective-permute-start | bytes 294920 | tf_op jit(solution)/shard_map/ppermute | solution.py:59
  225.6 14.1 %collective-permute-start.6 = (f32[16,1536]{1,0:T(8,128)S(1)}, f32[16,1536]{1,0:T(8,128)S(1)}, u32[]{:S(2)}, u32[]{:S(2)}) collective-permute-start(f32[16,1536]{1,0:T(8,128)S(1)} %select_add_fusion.3), channel_id=1, source_target_pairs={{0,8},{1,9},{2,10},{3,11},{4,12},{5,13},{6,14},{7,15},{8,0},{9,1},... | collective-permute-start | bytes 294920 | tf_op jit(solution)/shard_map/ppermute | solution.py:65
  239.8 10.7 %collective-permute-start.7 = (f32[32,1536]{1,0:T(8,128)S(1)}, f32[32,1536]{1,0:T(8,128)S(1)}, u32[]{:S(2)}, u32[]{:S(2)}) collective-permute-start(f32[32,1536]{1,0:T(8,128)S(1)} %maximum_select_fusion.3), channel_id=1, source_target_pairs={{0,4},{1,5},{2,6},{3,7},{4,0},{5,1},{6,2},{7,3},{8,12},{9,13},{10,... | collective-permute-start | bytes 589832 | tf_op jit(solution)/shard_map/ppermute | solution.py:65
  250.5 12.1 %collective-permute-start.8 = (f32[64,1536]{1,0:T(8,128)S(1)}, f32[64,1536]{1,0:T(8,128)S(1)}, u32[]{:S(2)}, u32[]{:S(2)}) collective-permute-start(f32[64,1536]{1,0:T(8,128)S(1)} %maximum_select_fusion.2), channel_id=1, source_target_pairs={{0,2},{1,3},{2,0},{3,1},{4,6},{5,7},{6,4},{7,5},{8,10},{9,11},{10,... | collective-permute-start | bytes 1179656 | tf_op jit(solution)/shard_map/ppermute | solution.py:65
  262.7 5.2 %collective-permute-start.9 = (f32[128,1536]{1,0:T(8,128)S(1)}, f32[128,1536]{1,0:T(8,128)S(1)}, u32[]{:S(2)}, u32[]{:S(2)}) collective-permute-start(f32[128,1536]{1,0:T(8,128)S(1)} %maximum_select_fusion.1), channel_id=1, source_target_pairs={{0,1},{1,0},{2,3},{3,2},{4,5},{5,4},{6,7},{7,6},{8,9},{9,8},{10,11... | collective-permute-start | bytes 2359304 | tf_op jit(solution)/shard_map/ppermute | solution.py:65

commit v4 on v3

--- a/solution.py
+++ b/solution.py
@@ -56,15 +56,16 @@
         low, high = cur[:half], cur[half:]
         keep = jnp.where(upper, high, low)
         send = jnp.where(upper, low, high)
-        got = lax.ppermute(send, "tensor", [(i, i ^ step) for i in range(count)])
-        cur = keep + got
+        got = lax.ppermute(send.astype(jnp.bfloat16), "tensor", [(i, i ^ step) for i in range(count)])
+        cur = keep + got.astype(jnp.float32)
         step *= 2
+    cur = cur.astype(jnp.bfloat16)
     while step > 1:
         step //= 2
         upper = (index & step) != 0
         got = lax.ppermute(cur, "tensor", [(i, i ^ step) for i in range(count)])
         cur = jnp.where(upper, jnp.concatenate([got, cur]), jnp.concatenate([cur, got]))
-    return cur
+    return cur.astype(jnp.float32)
 
 
 def local(normed, grad_out, w_query, w_key, w_value, w_out, key_span):

time: 271 us -> 245 us (0.904)
  waiting for transfers between devices: 153 us -> 119 us
  starting transfers between devices: 87.2 us -> 94.6 us
    ppermute x4, waiting for transfers between devices: 33 us -> 14 us  [head_sum(): got = lax.ppermute(cur, 'tensor', [(i, i ^ step) for i in range(count)])]
    ppermute x4, waiting for transfers between devices: 28.6 us -> 13.9 us  [head_sum(): lax.ppermute(send.astype(jnp.bfloat16), 'tensor', [(i, i ^ step) for i in...]
    ppermute x4, starting transfers between devices: 9.01 us -> 15.6 us  [head_sum(): got = lax.ppermute(cur, 'tensor', [(i, i ^ step) for i in range(count)])]
where the time goes in v4:
time: 245 us; the launch traced here: 242 us
  waiting for transfers between devices  119 us (49%)
  starting transfers between devices  94.6 us (39%)
  local copies, waits for them, and re-layouts  13.1 us (5%)
  matrix products  11.3 us (5%)
  other arithmetic  2.92 us (1%)
    all_to_all x1, waiting for transfers between devices, local(): lax.all_to_all(returned, 'tq', split_axis=0, concat_axis=0, tiled=True)  45.5 us
    all_to_all x1, waiting for transfers between devices, local(): lax.all_to_all(outgoing, 'tq', split_axis=0, concat_axis=0, tiled=True)  42.9 us
    ppermute x4, starting transfers between devices, head_sum(): lax.ppermute(send.astype(jnp.bfloat16), 'tensor', [(i, i ^ step) for i in...  28.9 us
    ppermute x1, starting transfers between devices, local(): mirror_spans = lax.ppermute(paired_spans, 'zh', swap)  19.9 us
    ppermute x4, starting transfers between devices, head_sum(): got = lax.ppermute(cur, 'tensor', [(i, i ^ step) for i in range(count)])  15.6 us
    ppermute x4, waiting for transfers between devices, head_sum(): got = lax.ppermute(cur, 'tensor', [(i, i ^ step) for i in range(count)])  14 us
    ppermute x4, waiting for transfers between devices, head_sum(): lax.ppermute(send.astype(jnp.bfloat16), 'tensor', [(i, i ^ step) for i in...  13.9 us
    ppermute x1, starting transfers between devices, local(): summed = (mine + lax.ppermute(other, 'zh', swap)).astype(jnp.bfloat16)  12.3 us
  transfers between devices with their start and end apart: 12, of which 12 were waited for; matrix products, arithmetic and copies ran while one was open for 1% of the time, Pallas kernels for 0%

profile of v4, /device:TPU:1, one launch (start us, length us, event | category | flops | bytes accessed | tf_op | source)
XLA Modules:
  0.0 241.7 jit_solution(6222367812721396407)
XLA Ops:
  3.7 19.9 %collective-permute-start = (bf16[2,128,128]{2,1,0:T(8,128)(2,1)S(1)}, bf16[2,128,128]{2,1,0:T(8,128)(2,1)S(1)}, u32[]{:S(2)}, u32[]{:S(2)}) collective-permute-start(bf16[2,128,128]{2,1,0:T(8,128)(2,1)S(1)} %bitcast_bitcast_fusion), channel_id=1, source_target_pairs={{0,16},{16,0},{1,17},{17,1},{2,18},{18,2},{3,19},{19,3},{4,20},{20... | collective-permute-start | bytes 196616 | tf_op jit(solution)/shard_map/ppermute | solution.py:92
  25.5 2.1 gather_fusion
  27.6 9.8 %all-to-all-start = ((bf16[64,128,128]{2,1,0:T(8,128)(2,1)}), bf16[64,128,128]{2,1,0:T(8,128)(2,1)S(1)}, u32[]{:S(2)}, u32[]{:S(2)}) async-start(bf16[64,128,128]{2,1,0:T(8,128)(2,1)} %gather_fusion), calls=%async_computation | async-start | bytes 4194304 | tf_op jit(solution)/shard_map/all_to_all | solution.py:106
  39.6 42.9 %all-to-all-done = bf16[64,128,128]{2,1,0:T(8,128)(2,1)S(1)} async-done(((bf16[64,128,128]{2,1,0:T(8,128)(2,1)}), bf16[64,128,128]{2,1,0:T(8,128)(2,1)S(1)}, u32[]{:S(2)}, u32[]{:S(2)}) %all-to-all-start) | async-done | bytes 2097184 | tf_op jit(solution)/shard_map/all_to_all | solution.py:106
  89.8 1.8 broadcast_in_dim.16
  91.6 4.6 %scatter_fusion = bf16[64,128,128]{2,1,0:T(8,128)(2,1)} fusion(bf16[64,128,128]{2,1,0:T(8,128)(2,1)} %broadcast_in_dim.16, s32[32]{0:T(128)S(1)} %fusion.43, bf16[32,128,128]{2,1,0:T(8,128)(2,1)S(1)} %pad_maximum_fusion), kind=kCustom, calls=%fused_computation.2 | custom fusion | bytes 3145856 | tf_op jit(solution)/shard_map/scatter | solution.py:126
  96.3 8.1 %all-to-all-start.1 = ((bf16[64,128,128]{2,1,0:T(8,128)(2,1)}), bf16[64,128,128]{2,1,0:T(8,128)(2,1)S(1)}, u32[]{:S(2)}, u32[]{:S(2)}) async-start(bf16[64,128,128]{2,1,0:T(8,128)(2,1)} %scatter_fusion), calls=%async_computation.1 | async-start | bytes 4194304 | tf_op jit(solution)/shard_map/all_to_all | solution.py:128
  104.6 45.5 %all-to-all-done.1 = bf16[64,128,128]{2,1,0:T(8,128)(2,1)S(1)} async-done(((bf16[64,128,128]{2,1,0:T(8,128)(2,1)}), bf16[64,128,128]{2,1,0:T(8,128)(2,1)S(1)}, u32[]{:S(2)}, u32[]{:S(2)}) %all-to-all-start.1) | async-done | bytes 2097184 | tf_op jit(solution)/shard_map/all_to_all | solution.py:128
  151.4 12.3 %collective-permute-start.1 = (f32[2,128,128]{2,0,1:T(2,128)S(1)}, f32[2,128,128]{2,0,1:T(2,128)S(1)}, u32[]{:S(2)}, u32[]{:S(2)}) collective-permute-start(f32[2,128,128]{2,0,1:T(2,128)S(1)} %dynamic-slice_bitcast_fusion), channel_id=1, source_target_pairs={{0,16},{16,0},{1,17},{17,1},{2,18},{18,2},{3,19},{19,3},{4,20},{20... | collective-permute-start | bytes 393224 | tf_op jit(solution)/shard_map/ppermute | solution.py:136
  164.1 1.9 collective-permute-done.1
  167.5 8.6 %collective-permute-start.2 = (bf16[128,1536]{1,0:T(8,128)(2,1)S(1)}, bf16[128,1536]{1,0:T(8,128)(2,1)S(1)}, u32[]{:S(2)}, u32[]{:S(2)}) collective-permute-start(bf16[128,1536]{1,0:T(8,128)(2,1)S(1)} %select_convert_fusion), channel_id=1, source_target_pairs={{0,1},{1,0},{2,3},{3,2},{4,5},{5,4},{6,7},{7,6},{8,9},{9,8},{10,11... | collective-permute-start | bytes 1179656 | tf_op jit(solution)/shard_map/ppermute | solution.py:59
  177.6 7.6 %collective-permute-start.3 = (bf16[64,1536]{1,0:T(8,128)(2,1)S(1)}, bf16[64,1536]{1,0:T(8,128)(2,1)S(1)}, u32[]{:S(2)}, u32[]{:S(2)}) collective-permute-start(bf16[64,1536]{1,0:T(8,128)(2,1)S(1)} %select_convert_fusion.1), channel_id=1, source_target_pairs={{0,2},{1,3},{2,0},{3,1},{4,6},{5,7},{6,4},{7,5},{8,10},{9,11},{10,... | collective-permute-start | bytes 589832 | tf_op jit(solution)/shard_map/ppermute | solution.py:59
  185.2 4.9 %collective-permute-done.3 = bf16[64,1536]{1,0:T(8,128)(2,1)S(1)} collective-permute-done((bf16[64,1536]{1,0:T(8,128)(2,1)S(1)}, bf16[64,1536]{1,0:T(8,128)(2,1)S(1)}, u32[]{:S(2)}, u32[]{:S(2)}) %collective-permute-start.3) | collective-permute-done | bytes 196640 | tf_op jit(solution)/shard_map/ppermute | solution.py:59
  190.1 3.4 %collective-permute-start.4 = (bf16[32,1536]{1,0:T(8,128)(2,1)S(1)}, bf16[32,1536]{1,0:T(8,128)(2,1)S(1)}, u32[]{:S(2)}, u32[]{:S(2)}) collective-permute-start(bf16[32,1536]{1,0:T(8,128)(2,1)S(1)} %select_convert_fusion.2), channel_id=1, source_target_pairs={{0,4},{1,5},{2,6},{3,7},{4,0},{5,1},{6,2},{7,3},{8,12},{9,13},{10,... | collective-permute-start | bytes 294920 | tf_op jit(solution)/shard_map/ppermute | solution.py:59
  193.5 4.3 %collective-permute-done.4 = bf16[32,1536]{1,0:T(8,128)(2,1)S(1)} collective-permute-done((bf16[32,1536]{1,0:T(8,128)(2,1)S(1)}, bf16[32,1536]{1,0:T(8,128)(2,1)S(1)}, u32[]{:S(2)}, u32[]{:S(2)}) %collective-permute-start.4) | collective-permute-done | bytes 98336 | tf_op jit(solution)/shard_map/ppermute | solution.py:59
  197.9 9.3 %collective-permute-start.5 = (bf16[16,1536]{1,0:T(8,128)(2,1)S(1)}, bf16[16,1536]{1,0:T(8,128)(2,1)S(1)}, u32[]{:S(2)}, u32[]{:S(2)}) collective-permute-start(bf16[16,1536]{1,0:T(8,128)(2,1)S(1)} %select_convert_fusion.3), channel_id=1, source_target_pairs={{0,8},{1,9},{2,10},{3,11},{4,12},{5,13},{6,14},{7,15},{8,0},{9,1},... | collective-permute-start | bytes 147464 | tf_op jit(solution)/shard_map/ppermute | solution.py:59
  207.1 3.4 %collective-permute-done.5 = bf16[16,1536]{1,0:T(8,128)(2,1)S(1)} collective-permute-done((bf16[16,1536]{1,0:T(8,128)(2,1)S(1)}, bf16[16,1536]{1,0:T(8,128)(2,1)S(1)}, u32[]{:S(2)}, u32[]{:S(2)}) %collective-permute-start.5) | collective-permute-done | bytes 49184 | tf_op jit(solution)/shard_map/ppermute | solution.py:59
  210.6 5.4 %collective-permute-start.6 = (bf16[16,1536]{1,0:T(8,128)(2,1)S(1)}, bf16[16,1536]{1,0:T(8,128)(2,1)S(1)}, u32[]{:S(2)}, u32[]{:S(2)}) collective-permute-start(bf16[16,1536]{1,0:T(8,128)(2,1)S(1)} %add_convert_fusion), channel_id=1, source_target_pairs={{0,8},{1,9},{2,10},{3,11},{4,12},{5,13},{6,14},{7,15},{8,0},{9,1},... | collective-permute-start | bytes 147464 | tf_op jit(solution)/shard_map/ppermute | solution.py:66
  216.0 3.8 %collective-permute-done.6 = bf16[16,1536]{1,0:T(8,128)(2,1)S(1)} collective-permute-done((bf16[16,1536]{1,0:T(8,128)(2,1)S(1)}, bf16[16,1536]{1,0:T(8,128)(2,1)S(1)}, u32[]{:S(2)}, u32[]{:S(2)}) %collective-permute-start.6) | collective-permute-done | bytes 49184 | tf_op jit(solution)/shard_map/ppermute | solution.py:66
  219.9 1.9 collective-permute-start.7
  221.8 4.3 %collective-permute-done.7 = bf16[32,1536]{1,0:T(8,128)(2,1)S(1)} collective-permute-done((bf16[32,1536]{1,0:T(8,128)(2,1)S(1)}, bf16[32,1536]{1,0:T(8,128)(2,1)S(1)}, u32[]{:S(2)}, u32[]{:S(2)}) %collective-permute-start.7) | collective-permute-done | bytes 98336 | tf_op jit(solution)/shard_map/ppermute | solution.py:66
  226.2 1.9 collective-permute-start.8
  228.1 4.5 %collective-permute-done.8 = bf16[64,1536]{1,0:T(8,128)(2,1)S(1)} collective-permute-done((bf16[64,1536]{1,0:T(8,128)(2,1)S(1)}, bf16[64,1536]{1,0:T(8,128)(2,1)S(1)}, u32[]{:S(2)}, u32[]{:S(2)}) %collective-permute-start.8) | collective-permute-done | bytes 196640 | tf_op jit(solution)/shard_map/ppermute | solution.py:66
  232.7 6.3 %collective-permute-start.9 = (bf16[128,1536]{1,0:T(8,128)(2,1)S(1)}, bf16[128,1536]{1,0:T(8,128)(2,1)S(1)}, u32[]{:S(2)}, u32[]{:S(2)}) collective-permute-start(bf16[128,1536]{1,0:T(8,128)(2,1)S(1)} %maximum_select_fusion.1), channel_id=1, source_target_pairs={{0,1},{1,0},{2,3},{3,2},{4,5},{5,4},{6,7},{7,6},{8,9},{9,8},{10,11... | collective-permute-start | bytes 1179656 | tf_op jit(solution)/shard_map/ppermute | solution.py:66
  (78 shorter events, 22.4 us)
Async XLA Ops:
  0.0 1.1 copy-start
  0.0 23.7 %copy-start.9 = (s32[128,16]{0,1:T(8,128)S(1)}, s32[128,16]{0,1:T(8,128)}, u32[]{:S(2)}) copy-start(s32[128,16]{0,1:T(8,128)} %param.13) | copy-start | bytes 24580
  3.7 21.7 %collective-permute-start = (bf16[2,128,128]{2,1,0:T(8,128)(2,1)S(1)}, bf16[2,128,128]{2,1,0:T(8,128)(2,1)S(1)}, u32[]{:S(2)}, u32[]{:S(2)}) collective-permute-start(bf16[2,128,128]{2,1,0:T(8,128)(2,1)S(1)} %bitcast_bitcast_fusion), channel_id=1, source_target_pairs={{0,16},{16,0},{1,17},{17,1},{2,18},{18,2},{3,19},{19,3},{4,20},{20... | collective-permute-start | bytes 196616 | tf_op jit(solution)/shard_map/ppermute | solution.py:92
  27.6 10.1 %copy-start.8 = (bf16[64,1536]{1,0:T(8,128)(2,1)S(1)}, bf16[64,1536]{1,0:T(8,128)(2,1)}, u32[]{:S(2)}) copy-start(bf16[64,1536]{1,0:T(8,128)(2,1)} %param.12) | copy-start | bytes 589828
  27.6 11.6 %copy-start.7 = (bf16[1536,64]{0,1:T(8,128)(2,1)S(1)}, bf16[1536,64]{0,1:T(8,128)(2,1)}, u32[]{:S(2)}) copy-start(bf16[1536,64]{0,1:T(8,128)(2,1)} %param.9) | copy-start | bytes 589828
  27.6 54.8 %all-to-all-start = ((bf16[64,128,128]{2,1,0:T(8,128)(2,1)}), bf16[64,128,128]{2,1,0:T(8,128)(2,1)S(1)}, u32[]{:S(2)}, u32[]{:S(2)}) async-start(bf16[64,128,128]{2,1,0:T(8,128)(2,1)} %gather_fusion), calls=%async_computation | async-start | bytes 4194304 | tf_op jit(solution)/shard_map/all_to_all | solution.py:106
  84.1 2.0 copy-start.1
  88.2 1.0 copy-start.3
  96.3 53.9 %all-to-all-start.1 = ((bf16[64,128,128]{2,1,0:T(8,128)(2,1)}), bf16[64,128,128]{2,1,0:T(8,128)(2,1)S(1)}, u32[]{:S(2)}, u32[]{:S(2)}) async-start(bf16[64,128,128]{2,1,0:T(8,128)(2,1)} %scatter_fusion), calls=%async_computation.1 | async-start | bytes 4194304 | tf_op jit(solution)/shard_map/all_to_all | solution.py:128
  150.2 13.6 %copy-start.2 = (bf16[32,128,128]{2,1,0:T(8,128)(2,1)S(1)}, bf16[32,128,128]{2,1,0:T(8,128)(2,1)}, u32[]{:S(2)}) copy-start(bf16[32,128,128]{2,1,0:T(8,128)(2,1)} %gather_fusion.1) | copy-start | bytes 3145732
  150.2 13.6 %copy-start.4 = (bf16[2,128,16,128]{1,3,2,0:T(8,128)(2,1)S(1)}, bf16[2,128,16,128]{1,3,2,0:T(8,128)(2,1)}, u32[]{:S(2)}) copy-start(bf16[2,128,16,128]{1,3,2,0:T(8,128)(2,1)} %copy-done.3) | copy-start | bytes 3145732
  150.2 16.0 %copy-start.5 = (bf16[1536,64]{0,1:T(8,128)(2,1)S(1)}, bf16[1536,64]{0,1:T(8,128)(2,1)}, u32[]{:S(2)}) copy-start(bf16[1536,64]{0,1:T(8,128)(2,1)} %param.10) | copy-start | bytes 589828
  151.4 15.2 %copy-start.6 = (bf16[1536,64]{0,1:T(8,128)(2,1)S(1)}, bf16[1536,64]{0,1:T(8,128)(2,1)}, u32[]{:S(2)}) copy-start(bf16[1536,64]{0,1:T(8,128)(2,1)} %param.11) | copy-start | bytes 589828
  151.4 14.6 %collective-permute-start.1 = (f32[2,128,128]{2,0,1:T(2,128)S(1)}, f32[2,128,128]{2,0,1:T(2,128)S(1)}, u32[]{:S(2)}, u32[]{:S(2)}) collective-permute-start(f32[2,128,128]{2,0,1:T(2,128)S(1)} %dynamic-slice_bitcast_fusion), channel_id=1, source_target_pairs={{0,16},{16,0},{1,17},{17,1},{2,18},{18,2},{3,19},{19,3},{4,20},{20... | collective-permute-start | bytes 393224 | tf_op jit(solution)/shard_map/ppermute | solution.py:136
  167.5 10.0 %collective-permute-start.2 = (bf16[128,1536]{1,0:T(8,128)(2,1)S(1)}, bf16[128,1536]{1,0:T(8,128)(2,1)S(1)}, u32[]{:S(2)}, u32[]{:S(2)}) collective-permute-start(bf16[128,1536]{1,0:T(8,128)(2,1)S(1)} %select_convert_fusion), channel_id=1, source_target_pairs={{0,1},{1,0},{2,3},{3,2},{4,5},{5,4},{6,7},{7,6},{8,9},{9,8},{10,11... | collective-permute-start | bytes 1179656 | tf_op jit(solution)/shard_map/ppermute | solution.py:59
  177.6 12.5 %collective-permute-start.3 = (bf16[64,1536]{1,0:T(8,128)(2,1)S(1)}, bf16[64,1536]{1,0:T(8,128)(2,1)S(1)}, u32[]{:S(2)}, u32[]{:S(2)}) collective-permute-start(bf16[64,1536]{1,0:T(8,128)(2,1)S(1)} %select_convert_fusion.1), channel_id=1, source_target_pairs={{0,2},{1,3},{2,0},{3,1},{4,6},{5,7},{6,4},{7,5},{8,10},{9,11},{10,... | collective-permute-start | bytes 589832 | tf_op jit(solution)/shard_map/ppermute | solution.py:59
  190.1 7.7 %collective-permute-start.4 = (bf16[32,1536]{1,0:T(8,128)(2,1)S(1)}, bf16[32,1536]{1,0:T(8,128)(2,1)S(1)}, u32[]{:S(2)}, u32[]{:S(2)}) collective-permute-start(bf16[32,1536]{1,0:T(8,128)(2,1)S(1)} %select_convert_fusion.2), channel_id=1, source_target_pairs={{0,4},{1,5},{2,6},{3,7},{4,0},{5,1},{6,2},{7,3},{8,12},{9,13},{10,... | collective-permute-start | bytes 294920 | tf_op jit(solution)/shard_map/ppermute | solution.py:59
  197.9 12.7 %collective-permute-start.5 = (bf16[16,1536]{1,0:T(8,128)(2,1)S(1)}, bf16[16,1536]{1,0:T(8,128)(2,1)S(1)}, u32[]{:S(2)}, u32[]{:S(2)}) collective-permute-start(bf16[16,1536]{1,0:T(8,128)(2,1)S(1)} %select_convert_fusion.3), channel_id=1, source_target_pairs={{0,8},{1,9},{2,10},{3,11},{4,12},{5,13},{6,14},{7,15},{8,0},{9,1},... | collective-permute-start | bytes 147464 | tf_op jit(solution)/shard_map/ppermute | solution.py:59
  210.6 9.3 %collective-permute-start.6 = (bf16[16,1536]{1,0:T(8,128)(2,1)S(1)}, bf16[16,1536]{1,0:T(8,128)(2,1)S(1)}, u32[]{:S(2)}, u32[]{:S(2)}) collective-permute-start(bf16[16,1536]{1,0:T(8,128)(2,1)S(1)} %add_convert_fusion), channel_id=1, source_target_pairs={{0,8},{1,9},{2,10},{3,11},{4,12},{5,13},{6,14},{7,15},{8,0},{9,1},... | collective-permute-start | bytes 147464 | tf_op jit(solution)/shard_map/ppermute | solution.py:66
  219.9 6.3 %collective-permute-start.7 = (bf16[32,1536]{1,0:T(8,128)(2,1)S(1)}, bf16[32,1536]{1,0:T(8,128)(2,1)S(1)}, u32[]{:S(2)}, u32[]{:S(2)}) collective-permute-start(bf16[32,1536]{1,0:T(8,128)(2,1)S(1)} %maximum_select_fusion.4), channel_id=1, source_target_pairs={{0,4},{1,5},{2,6},{3,7},{4,0},{5,1},{6,2},{7,3},{8,12},{9,13},{10,... | collective-permute-start | bytes 294920 | tf_op jit(solution)/shard_map/ppermute | solution.py:66
  226.2 6.4 %collective-permute-start.8 = (bf16[64,1536]{1,0:T(8,128)(2,1)S(1)}, bf16[64,1536]{1,0:T(8,128)(2,1)S(1)}, u32[]{:S(2)}, u32[]{:S(2)}) collective-permute-start(bf16[64,1536]{1,0:T(8,128)(2,1)S(1)} %maximum_select_fusion.2), channel_id=1, source_target_pairs={{0,2},{1,3},{2,0},{3,1},{4,6},{5,7},{6,4},{7,5},{8,10},{9,11},{10,... | collective-permute-start | bytes 589832 | tf_op jit(solution)/shard_map/ppermute | solution.py:66
  232.7 7.7 %collective-permute-start.9 = (bf16[128,1536]{1,0:T(8,128)(2,1)S(1)}, bf16[128,1536]{1,0:T(8,128)(2,1)S(1)}, u32[]{:S(2)}, u32[]{:S(2)}) collective-permute-start(bf16[128,1536]{1,0:T(8,128)(2,1)S(1)} %maximum_select_fusion.1), channel_id=1, source_target_pairs={{0,1},{1,0},{2,3},{3,2},{4,5},{5,4},{6,7},{7,6},{8,9},{9,8},{10,11... | collective-permute-start | bytes 1179656 | tf_op jit(solution)/shard_map/ppermute | solution.py:66

commit v5 on v4

--- a/solution.py
+++ b/solution.py
@@ -90,20 +90,19 @@
     paired_t = jnp.concatenate([keys_t, values_t], axis=0)
     paired_spans = jnp.transpose(paired_t.reshape(2 * col_count, owned, SPAN), (1, 0, 2))
     mirror_spans = lax.ppermute(paired_spans, "zh", swap)
-    have = jnp.where(
-        my_side == 0,
-        jnp.concatenate([paired_spans, mirror_spans]),
-        jnp.concatenate([mirror_spans, paired_spans]),
-    )
     all_pairs = key_span.reshape(column_count, side_count, owned * per_reader)
     requests = lax.dynamic_index_in_dim(all_pairs, my_side, axis=1, keepdims=False)
     sides = my_column * side_count + jnp.arange(side_count, dtype=jnp.int32)
     hit = (requests // owned)[:, :, None] == sides[None, None, :]
     slot = jnp.sum(jnp.where(hit, (requests % owned)[:, :, None], 0), axis=1)
     exists = jnp.any(hit, axis=1)
-    which = jnp.arange(side_count, dtype=jnp.int32)[None, :] * owned + slot
-    outgoing = have[which.reshape(-1)]
-    incoming = lax.all_to_all(outgoing, "tq", split_axis=0, concat_axis=0, tiled=True)
+    own_slot = lax.dynamic_index_in_dim(slot, my_side, axis=1, keepdims=False)
+    mirror_slot = lax.dynamic_index_in_dim(slot, 1 - my_side, axis=1, keepdims=False)
+    near = lax.all_to_all(paired_spans[own_slot], "tq", split_axis=0, concat_axis=0, tiled=True)
+    far = lax.all_to_all(mirror_spans[mirror_slot], "tq", split_axis=0, concat_axis=0, tiled=True)
+    incoming = jnp.where(
+        my_side == 0, jnp.stack([near, far], axis=1), jnp.stack([far, near], axis=1)
+    ).reshape(device_count, 2 * col_count, SPAN)
     own_ids = lax.dynamic_slice_in_dim(key_span, my_index * owned, owned, 0)
     owner_ids = (own_ids // owned).reshape(-1)
     fetched = incoming[owner_ids]
@@ -125,15 +124,32 @@
     returned = (
         jnp.zeros((device_count, 2 * col_count, SPAN), jnp.bfloat16).at[owner_ids].set(pair_grads)
     )
-    received = lax.all_to_all(returned, "tq", split_axis=0, concat_axis=0, tiled=True)
-    received = received.reshape(column_count, side_count, 2 * col_count, SPAN)
+    returned = returned.reshape(column_count, side_count, 2 * col_count, SPAN)
     picked = (
         exists[:, :, None] & (slot[:, :, None] == jnp.arange(owned, dtype=jnp.int32)[None, None, :])
     ).astype(jnp.bfloat16)
-    partial = jnp.einsum("csk,csrh->skrh", picked, received, preferred_element_type=jnp.float32)
-    mine = lax.dynamic_index_in_dim(partial, my_side, axis=0, keepdims=False)
-    other = lax.dynamic_index_in_dim(partial, 1 - my_side, axis=0, keepdims=False)
-    summed = (mine + lax.ppermute(other, "zh", swap)).astype(jnp.bfloat16)
+    far_back = lax.all_to_all(
+        lax.dynamic_index_in_dim(returned, 1 - my_side, axis=1, keepdims=False),
+        "tq", split_axis=0, concat_axis=0, tiled=True,
+    )
+    other = jnp.einsum(
+        "ck,crh->krh",
+        lax.dynamic_index_in_dim(picked, 1 - my_side, axis=1, keepdims=False),
+        far_back,
+        preferred_element_type=jnp.float32,
+    )
+    other_back = lax.ppermute(other, "zh", swap)
+    near_back = lax.all_to_all(
+        lax.dynamic_index_in_dim(returned, my_side, axis=1, keepdims=False),
+        "tq", split_axis=0, concat_axis=0, tiled=True,
+    )
+    mine = jnp.einsum(
+        "ck,crh->krh",
+        lax.dynamic_index_in_dim(picked, my_side, axis=1, keepdims=False),
+        near_back,
+        preferred_element_type=jnp.float32,
+    )
+    summed = (mine + other_back).astype(jnp.bfloat16)
     summed_t = jnp.transpose(summed, (1, 0, 2)).reshape(2 * col_count, row_count)
     kv_term = project_back(summed_t[:col_count], w_key) + project_back(
         summed_t[col_count:], w_value

time: 245 us -> 229 us (0.935)
  waiting for transfers between devices: 119 us -> 48.5 us
  blocking collectives: 0 us -> 30 us
  starting transfers between devices: 94.6 us -> 118 us
  matrix products: 11.3 us -> 14.6 us
    all_to_all x2 -> x3, waiting for transfers between devices: 88.4 us -> 21.9 us  [the longest x1 21.9 us: local(): lax.all_to_all(mirror_spans[mirror_slot], 'tq', split_axis=0, concat_axis...]
    all_to_all x0 -> x1, blocking collectives: none -> 30 us  [local(): lax.all_to_all(lax.dynamic_index_in_dim(returned, 1 - my_side, axis=1, ke...]
    ppermute x1, starting transfers between devices: 12.3 us -> 23.4 us  [local(): other_back = lax.ppermute(other, 'zh', swap)]
    all_to_all x2 -> x3, starting transfers between devices: 17.9 us -> 26.8 us  [the longest x1 10.5 us: local(): lax.all_to_all(paired_spans[own_slot], 'tq', split_axis=0, concat_axis=0,...]
    ppermute x4, starting transfers between devices: 15.6 us -> 23.4 us  [head_sum(): got = lax.ppermute(cur, 'tensor', [(i, i ^ step) for i in range(count)])]
    ppermute x4, waiting for transfers between devices: 14 us -> 9.7 us  [head_sum(): got = lax.ppermute(cur, 'tensor', [(i, i ^ step) for i in range(count)])]
    ppermute x4, starting transfers between devices: 28.9 us -> 25.2 us  [head_sum(): lax.ppermute(send.astype(jnp.bfloat16), 'tensor', [(i, i ^ step) for i in...]
    dot_general x1 -> x2, matrix products: 1.25 us -> 4.48 us  [the longest x1 2.58 us: local(): jnp.einsum('ck,crh->krh', lax.dynamic_index_in_dim(picked, 1 - my_side, a...]
  transfers between devices with their start and end apart: 12 -> 13, of which waited for: 12 -> 11; matrix products, arithmetic and copies ran while one was open for 1% -> 3% of each run, Pallas kernels for 0% -> 0%
where the time goes in v5:
time: 229 us; the launch traced here: 228 us
  starting transfers between devices  118 us (52%)
  waiting for transfers between devices  48.5 us (21%)
  blocking collectives  30 us (13%)
  matrix products  14.6 us (6%)
  local copies, waits for them, and re-layouts  11.7 us (5%)
  other arithmetic  4.82 us (2%)
    all_to_all x1, blocking collectives, local(): lax.all_to_all(lax.dynamic_index_in_dim(returned, 1 - my_side, axis=1, ke...  30 us
    ppermute x4, starting transfers between devices, head_sum(): lax.ppermute(send.astype(jnp.bfloat16), 'tensor', [(i, i ^ step) for i in...  25.2 us
    ppermute x4, starting transfers between devices, head_sum(): got = lax.ppermute(cur, 'tensor', [(i, i ^ step) for i in range(count)])  23.4 us
    ppermute x1, starting transfers between devices, local(): other_back = lax.ppermute(other, 'zh', swap)  23.4 us
    all_to_all x1, waiting for transfers between devices, local(): lax.all_to_all(mirror_spans[mirror_slot], 'tq', split_axis=0, concat_axis...  21.9 us
    ppermute x1, starting transfers between devices, local(): mirror_spans = lax.ppermute(paired_spans, 'zh', swap)  19.1 us
    ppermute x4, waiting for transfers between devices, head_sum(): lax.ppermute(send.astype(jnp.bfloat16), 'tensor', [(i, i ^ step) for i in...  12.6 us
    all_to_all x1, starting transfers between devices, local(): lax.all_to_all(paired_spans[own_slot], 'tq', split_axis=0, concat_axis=0,...  10.5 us
  transfers between devices with their start and end apart: 13, of which 11 were waited for; matrix products, arithmetic and copies ran while one was open for 3% of the time, Pallas kernels for 0%

profile of v5, /device:TPU:1, one launch (start us, length us, event | category | flops | bytes accessed | tf_op | source)
XLA Modules:
  0.0 228.1 jit_solution(1768248007953208599)
XLA Ops:
  6.4 10.5 %all-to-all-start = ((bf16[32,128,128]{2,1,0:T(8,128)(2,1)}), bf16[32,128,128]{2,1,0:T(8,128)(2,1)S(1)}, u32[]{:S(2)}, u32[]{:S(2)}) async-start(bf16[32,128,128]{2,1,0:T(8,128)(2,1)} %gather_fusion), calls=%async_computation | async-start | bytes 2097152 | tf_op jit(solution)/shard_map/all_to_all | solution.py:101
  16.9 19.1 %collective-permute-start = (bf16[2,128,128]{2,1,0:T(8,128)(2,1)S(1)}, bf16[2,128,128]{2,1,0:T(8,128)(2,1)S(1)}, u32[]{:S(2)}, u32[]{:S(2)}) collective-permute-start(bf16[2,128,128]{2,1,0:T(8,128)(2,1)S(1)} %bitcast_bitcast_fusion), channel_id=1, source_target_pairs={{0,16},{16,0},{1,17},{17,1},{2,18},{18,2},{3,19},{19,3},{4,20},{20... | collective-permute-start | bytes 196616 | tf_op jit(solution)/shard_map/ppermute | solution.py:92
  36.0 1.8 collective-permute-done
  39.5 9.5 %all-to-all-start.1 = ((bf16[32,128,128]{2,1,0:T(8,128)(2,1)}), bf16[32,128,128]{2,1,0:T(8,128)(2,1)S(1)}, u32[]{:S(2)}, u32[]{:S(2)}) async-start(bf16[32,128,128]{2,1,0:T(8,128)(2,1)} %gather_fusion.1), calls=%async_computation.1 | async-start | bytes 2097152 | tf_op jit(solution)/shard_map/all_to_all | solution.py:102
  50.9 21.9 %all-to-all-done.1 = bf16[32,128,128]{2,1,0:T(8,128)(2,1)S(1)} async-done(((bf16[32,128,128]{2,1,0:T(8,128)(2,1)}), bf16[32,128,128]{2,1,0:T(8,128)(2,1)S(1)}, u32[]{:S(2)}, u32[]{:S(2)}) %all-to-all-start.1) | async-done | bytes 1048608 | tf_op jit(solution)/shard_map/all_to_all | solution.py:102
  81.3 3.6 %scatter_fusion = bf16[64,128,128]{2,1,0:T(8,128)(2,1)S(1)} fusion(bf16[64,128,128]{2,1,0:T(8,128)(2,1)S(1)} %broadcast_in_dim.16, s32[32]{0:T(128)S(1)} %get-tuple-element.15, bf16[32,128,128]{2,1,0:T(8,128)(2,1)} %pad_maximum_fusion), kind=kCustom, calls=%fused_computation.3 | custom fusion | bytes 3145856 | tf_op jit(solution)/shard_map/scatter | solution.py:125
  86.0 30.0 %all_to_all.20 = bf16[32,128,128]{2,1,0:T(8,128)(2,1)} all-to-all(bf16[32,128,128]{2,1,0:T(8,128)(2,1)S(1)} %get-tuple-element.6), channel_id=1, replica_groups=mesh['tq'=32,'zh'=2,'tensor'=16] {'tq'}, dimensions={0} | all-to-all | bytes 2097152 | tf_op jit(solution)/shard_map/all_to_all | solution.py:131
  116.1 6.8 %all-to-all-start.2 = ((bf16[32,128,128]{2,1,0:T(8,128)(2,1)}), bf16[32,128,128]{2,1,0:T(8,128)(2,1)}, u32[]{:S(2)}, u32[]{:S(2)}) async-start(bf16[32,128,128]{2,1,0:T(8,128)(2,1)} %get-tuple-element.5), calls=%async_computation.2 | async-start | bytes 2097152 | tf_op jit(solution)/shard_map/all_to_all | solution.py:142
  123.1 2.6 %fusion.10 = f32[2,128,128]{2,0,1:T(2,128)} fusion(bf16[32,128,128]{2,1,0:T(8,128)(2,1)} %all_to_all.20, pred[32,2,2]{0,2,1:T(4,128)(4,1)S(1)} %compare_and_fusion, s32[]{:T(128)S(6)} %select_n.172), kind=kOutput, calls=%fused_computation.30 | convolution fusion | flops 2097152 | bytes 1180164 | tf_op jit(solution)/shard_map/ck,crh->krh/dot_general | solution.py:135
  125.7 23.4 %collective-permute-start.1 = (f32[2,128,128]{2,0,1:T(2,128)}, f32[2,128,128]{2,0,1:T(2,128)}, u32[]{:S(2)}, u32[]{:S(2)}) collective-permute-start(f32[2,128,128]{2,0,1:T(2,128)} %fusion.10), channel_id=1, source_target_pairs={{0,16},{16,0},{1,17},{17,1},{2,18},{18,2},{3,19},{19,3},{4,20},{20... | collective-permute-start | bytes 393224 | tf_op jit(solution)/shard_map/ppermute | solution.py:141
  149.5 2.6 %collective-permute-done.1 = f32[2,128,128]{2,0,1:T(2,128)} collective-permute-done((f32[2,128,128]{2,0,1:T(2,128)}, f32[2,128,128]{2,0,1:T(2,128)}, u32[]{:S(2)}, u32[]{:S(2)}) %collective-permute-start.1) | collective-permute-done | bytes 131104 | tf_op jit(solution)/shard_map/ppermute | solution.py:141
  152.1 1.9 fusion.6
  155.3 5.3 %collective-permute-start.2 = (bf16[128,1536]{1,0:T(8,128)(2,1)S(1)}, bf16[128,1536]{1,0:T(8,128)(2,1)S(1)}, u32[]{:S(2)}, u32[]{:S(2)}) collective-permute-start(bf16[128,1536]{1,0:T(8,128)(2,1)S(1)} %select_convert_fusion), channel_id=1, source_target_pairs={{0,1},{1,0},{2,3},{3,2},{4,5},{5,4},{6,7},{7,6},{8,9},{9,8},{10,11... | collective-permute-start | bytes 1179656 | tf_op jit(solution)/shard_map/ppermute | solution.py:59
  162.1 9.8 %collective-permute-start.3 = (bf16[64,1536]{1,0:T(8,128)(2,1)S(1)}, bf16[64,1536]{1,0:T(8,128)(2,1)S(1)}, u32[]{:S(2)}, u32[]{:S(2)}) collective-permute-start(bf16[64,1536]{1,0:T(8,128)(2,1)S(1)} %select_convert_fusion.1), channel_id=1, source_target_pairs={{0,2},{1,3},{2,0},{3,1},{4,6},{5,7},{6,4},{7,5},{8,10},{9,11},{10,... | collective-permute-start | bytes 589832 | tf_op jit(solution)/shard_map/ppermute | solution.py:59
  172.0 4.9 %collective-permute-done.3 = bf16[64,1536]{1,0:T(8,128)(2,1)S(1)} collective-permute-done((bf16[64,1536]{1,0:T(8,128)(2,1)S(1)}, bf16[64,1536]{1,0:T(8,128)(2,1)S(1)}, u32[]{:S(2)}, u32[]{:S(2)}) %collective-permute-start.3) | collective-permute-done | bytes 196640 | tf_op jit(solution)/shard_map/ppermute | solution.py:59
  176.9 3.1 %collective-permute-start.4 = (bf16[32,1536]{1,0:T(8,128)(2,1)S(1)}, bf16[32,1536]{1,0:T(8,128)(2,1)S(1)}, u32[]{:S(2)}, u32[]{:S(2)}) collective-permute-start(bf16[32,1536]{1,0:T(8,128)(2,1)S(1)} %select_convert_fusion.2), channel_id=1, source_target_pairs={{0,4},{1,5},{2,6},{3,7},{4,0},{5,1},{6,2},{7,3},{8,12},{9,13},{10,... | collective-permute-start | bytes 294920 | tf_op jit(solution)/shard_map/ppermute | solution.py:59
  180.0 4.6 %collective-permute-done.4 = bf16[32,1536]{1,0:T(8,128)(2,1)S(1)} collective-permute-done((bf16[32,1536]{1,0:T(8,128)(2,1)S(1)}, bf16[32,1536]{1,0:T(8,128)(2,1)S(1)}, u32[]{:S(2)}, u32[]{:S(2)}) %collective-permute-start.4) | collective-permute-done | bytes 98336 | tf_op jit(solution)/shard_map/ppermute | solution.py:59
  184.7 7.0 %collective-permute-start.5 = (bf16[16,1536]{1,0:T(8,128)(2,1)S(1)}, bf16[16,1536]{1,0:T(8,128)(2,1)S(1)}, u32[]{:S(2)}, u32[]{:S(2)}) collective-permute-start(bf16[16,1536]{1,0:T(8,128)(2,1)S(1)} %select_convert_fusion.3), channel_id=1, source_target_pairs={{0,8},{1,9},{2,10},{3,11},{4,12},{5,13},{6,14},{7,15},{8,0},{9,1},... | collective-permute-start | bytes 147464 | tf_op jit(solution)/shard_map/ppermute | solution.py:59
  193.4 7.0 %collective-permute-start.6 = (bf16[16,1536]{1,0:T(8,128)(2,1)S(1)}, bf16[16,1536]{1,0:T(8,128)(2,1)S(1)}, u32[]{:S(2)}, u32[]{:S(2)}) collective-permute-start(bf16[16,1536]{1,0:T(8,128)(2,1)S(1)} %add_convert_fusion), channel_id=1, source_target_pairs={{0,8},{1,9},{2,10},{3,11},{4,12},{5,13},{6,14},{7,15},{8,0},{9,1},... | collective-permute-start | bytes 147464 | tf_op jit(solution)/shard_map/ppermute | solution.py:66
  202.2 2.7 %collective-permute-start.7 = (bf16[32,1536]{1,0:T(8,128)(2,1)S(1)}, bf16[32,1536]{1,0:T(8,128)(2,1)S(1)}, u32[]{:S(2)}, u32[]{:S(2)}) collective-permute-start(bf16[32,1536]{1,0:T(8,128)(2,1)S(1)} %maximum_select_fusion.4), channel_id=1, source_target_pairs={{0,4},{1,5},{2,6},{3,7},{4,0},{5,1},{6,2},{7,3},{8,12},{9,13},{10,... | collective-permute-start | bytes 294920 | tf_op jit(solution)/shard_map/ppermute | solution.py:66
  204.9 3.5 %collective-permute-done.7 = bf16[32,1536]{1,0:T(8,128)(2,1)S(1)} collective-permute-done((bf16[32,1536]{1,0:T(8,128)(2,1)S(1)}, bf16[32,1536]{1,0:T(8,128)(2,1)S(1)}, u32[]{:S(2)}, u32[]{:S(2)}) %collective-permute-start.7) | collective-permute-done | bytes 98336 | tf_op jit(solution)/shard_map/ppermute | solution.py:66
  208.5 7.4 %collective-permute-start.8 = (bf16[64,1536]{1,0:T(8,128)(2,1)S(1)}, bf16[64,1536]{1,0:T(8,128)(2,1)S(1)}, u32[]{:S(2)}, u32[]{:S(2)}) collective-permute-start(bf16[64,1536]{1,0:T(8,128)(2,1)S(1)} %maximum_select_fusion.3), channel_id=1, source_target_pairs={{0,2},{1,3},{2,0},{3,1},{4,6},{5,7},{6,4},{7,5},{8,10},{9,11},{10,... | collective-permute-start | bytes 589832 | tf_op jit(solution)/shard_map/ppermute | solution.py:66
  215.9 3.0 %collective-permute-done.8 = bf16[64,1536]{1,0:T(8,128)(2,1)S(1)} collective-permute-done((bf16[64,1536]{1,0:T(8,128)(2,1)S(1)}, bf16[64,1536]{1,0:T(8,128)(2,1)S(1)}, u32[]{:S(2)}, u32[]{:S(2)}) %collective-permute-start.8) | collective-permute-done | bytes 196640 | tf_op jit(solution)/shard_map/ppermute | solution.py:66
  219.1 6.4 %collective-permute-start.9 = (bf16[128,1536]{1,0:T(8,128)(2,1)S(1)}, bf16[128,1536]{1,0:T(8,128)(2,1)S(1)}, u32[]{:S(2)}, u32[]{:S(2)}) collective-permute-start(bf16[128,1536]{1,0:T(8,128)(2,1)S(1)} %maximum_select_fusion.2), channel_id=1, source_target_pairs={{0,1},{1,0},{2,3},{3,2},{4,5},{5,4},{6,7},{7,6},{8,9},{9,8},{10,11... | collective-permute-start | bytes 1179656 | tf_op jit(solution)/shard_map/ppermute | solution.py:66
  (78 shorter events, 29.2 us)
Async XLA Ops:
  0.0 1.8 copy-start
  6.4 33.1 %all-to-all-start = ((bf16[32,128,128]{2,1,0:T(8,128)(2,1)}), bf16[32,128,128]{2,1,0:T(8,128)(2,1)S(1)}, u32[]{:S(2)}, u32[]{:S(2)}) async-start(bf16[32,128,128]{2,1,0:T(8,128)(2,1)} %gather_fusion), calls=%async_computation | async-start | bytes 2097152 | tf_op jit(solution)/shard_map/all_to_all | solution.py:101
  16.9 20.9 %collective-permute-start = (bf16[2,128,128]{2,1,0:T(8,128)(2,1)S(1)}, bf16[2,128,128]{2,1,0:T(8,128)(2,1)S(1)}, u32[]{:S(2)}, u32[]{:S(2)}) collective-permute-start(bf16[2,128,128]{2,1,0:T(8,128)(2,1)S(1)} %bitcast_bitcast_fusion), channel_id=1, source_target_pairs={{0,16},{16,0},{1,17},{17,1},{2,18},{18,2},{3,19},{19,3},{4,20},{20... | collective-permute-start | bytes 196616 | tf_op jit(solution)/shard_map/ppermute | solution.py:92
  36.0 13.0 %copy-start.8 = (bf16[64,1536]{1,0:T(8,128)(2,1)S(1)}, bf16[64,1536]{1,0:T(8,128)(2,1)}, u32[]{:S(2)}) copy-start(bf16[64,1536]{1,0:T(8,128)(2,1)} %param.12) | copy-start | bytes 589828
  39.5 11.0 %copy-start.7 = (bf16[1536,64]{0,1:T(8,128)(2,1)S(1)}, bf16[1536,64]{0,1:T(8,128)(2,1)}, u32[]{:S(2)}) copy-start(bf16[1536,64]{0,1:T(8,128)(2,1)} %param.9) | copy-start | bytes 589828
  39.5 33.4 %all-to-all-start.1 = ((bf16[32,128,128]{2,1,0:T(8,128)(2,1)}), bf16[32,128,128]{2,1,0:T(8,128)(2,1)S(1)}, u32[]{:S(2)}, u32[]{:S(2)}) async-start(bf16[32,128,128]{2,1,0:T(8,128)(2,1)} %gather_fusion.1), calls=%async_computation.1 | async-start | bytes 2097152 | tf_op jit(solution)/shard_map/all_to_all | solution.py:102
  75.1 2.0 copy-start.1
  79.2 1.6 copy-start.3
  116.1 33.0 %copy-start.2 = (bf16[32,128,128]{2,1,0:T(8,128)(2,1)S(1)}, bf16[32,128,128]{2,1,0:T(8,128)(2,1)}, u32[]{:S(2)}) copy-start(bf16[32,128,128]{2,1,0:T(8,128)(2,1)} %gather_fusion.2) | copy-start | bytes 3145732
  116.1 33.1 %copy-start.4 = (bf16[2,128,16,128]{1,3,2,0:T(8,128)(2,1)S(1)}, bf16[2,128,16,128]{1,3,2,0:T(8,128)(2,1)}, u32[]{:S(2)}) copy-start(bf16[2,128,16,128]{1,3,2,0:T(8,128)(2,1)} %copy-done.3) | copy-start | bytes 3145732
  116.1 33.4 %all-to-all-start.2 = ((bf16[32,128,128]{2,1,0:T(8,128)(2,1)}), bf16[32,128,128]{2,1,0:T(8,128)(2,1)}, u32[]{:S(2)}, u32[]{:S(2)}) async-start(bf16[32,128,128]{2,1,0:T(8,128)(2,1)} %get-tuple-element.5), calls=%async_computation.2 | async-start | bytes 2097152 | tf_op jit(solution)/shard_map/all_to_all | solution.py:142
  123.1 30.9 %copy-start.5 = (bf16[1536,64]{0,1:T(8,128)(2,1)S(1)}, bf16[1536,64]{0,1:T(8,128)(2,1)}, u32[]{:S(2)}) copy-start(bf16[1536,64]{0,1:T(8,128)(2,1)} %param.10) | copy-start | bytes 589828
  125.7 28.7 %copy-start.6 = (bf16[1536,64]{0,1:T(8,128)(2,1)S(1)}, bf16[1536,64]{0,1:T(8,128)(2,1)}, u32[]{:S(2)}) copy-start(bf16[1536,64]{0,1:T(8,128)(2,1)} %param.11) | copy-start | bytes 589828
  125.7 26.4 %collective-permute-start.1 = (f32[2,128,128]{2,0,1:T(2,128)}, f32[2,128,128]{2,0,1:T(2,128)}, u32[]{:S(2)}, u32[]{:S(2)}) collective-permute-start(f32[2,128,128]{2,0,1:T(2,128)} %fusion.10), channel_id=1, source_target_pairs={{0,16},{16,0},{1,17},{17,1},{2,18},{18,2},{3,19},{19,3},{4,20},{20... | collective-permute-start | bytes 393224 | tf_op jit(solution)/shard_map/ppermute | solution.py:141
  155.3 6.7 %collective-permute-start.2 = (bf16[128,1536]{1,0:T(8,128)(2,1)S(1)}, bf16[128,1536]{1,0:T(8,128)(2,1)S(1)}, u32[]{:S(2)}, u32[]{:S(2)}) collective-permute-start(bf16[128,1536]{1,0:T(8,128)(2,1)S(1)} %select_convert_fusion), channel_id=1, source_target_pairs={{0,1},{1,0},{2,3},{3,2},{4,5},{5,4},{6,7},{7,6},{8,9},{9,8},{10,11... | collective-permute-start | bytes 1179656 | tf_op jit(solution)/shard_map/ppermute | solution.py:59
  162.1 14.7 %collective-permute-start.3 = (bf16[64,1536]{1,0:T(8,128)(2,1)S(1)}, bf16[64,1536]{1,0:T(8,128)(2,1)S(1)}, u32[]{:S(2)}, u32[]{:S(2)}) collective-permute-start(bf16[64,1536]{1,0:T(8,128)(2,1)S(1)} %select_convert_fusion.1), channel_id=1, source_target_pairs={{0,2},{1,3},{2,0},{3,1},{4,6},{5,7},{6,4},{7,5},{8,10},{9,11},{10,... | collective-permute-start | bytes 589832 | tf_op jit(solution)/shard_map/ppermute | solution.py:59
  176.9 7.7 %collective-permute-start.4 = (bf16[32,1536]{1,0:T(8,128)(2,1)S(1)}, bf16[32,1536]{1,0:T(8,128)(2,1)S(1)}, u32[]{:S(2)}, u32[]{:S(2)}) collective-permute-start(bf16[32,1536]{1,0:T(8,128)(2,1)S(1)} %select_convert_fusion.2), channel_id=1, source_target_pairs={{0,4},{1,5},{2,6},{3,7},{4,0},{5,1},{6,2},{7,3},{8,12},{9,13},{10,... | collective-permute-start | bytes 294920 | tf_op jit(solution)/shard_map/ppermute | solution.py:59
  184.7 8.8 %collective-permute-start.5 = (bf16[16,1536]{1,0:T(8,128)(2,1)S(1)}, bf16[16,1536]{1,0:T(8,128)(2,1)S(1)}, u32[]{:S(2)}, u32[]{:S(2)}) collective-permute-start(bf16[16,1536]{1,0:T(8,128)(2,1)S(1)} %select_convert_fusion.3), channel_id=1, source_target_pairs={{0,8},{1,9},{2,10},{3,11},{4,12},{5,13},{6,14},{7,15},{8,0},{9,1},... | collective-permute-start | bytes 147464 | tf_op jit(solution)/shard_map/ppermute | solution.py:59
  193.4 8.8 %collective-permute-start.6 = (bf16[16,1536]{1,0:T(8,128)(2,1)S(1)}, bf16[16,1536]{1,0:T(8,128)(2,1)S(1)}, u32[]{:S(2)}, u32[]{:S(2)}) collective-permute-start(bf16[16,1536]{1,0:T(8,128)(2,1)S(1)} %add_convert_fusion), channel_id=1, source_target_pairs={{0,8},{1,9},{2,10},{3,11},{4,12},{5,13},{6,14},{7,15},{8,0},{9,1},... | collective-permute-start | bytes 147464 | tf_op jit(solution)/shard_map/ppermute | solution.py:66
  202.2 6.3 %collective-permute-start.7 = (bf16[32,1536]{1,0:T(8,128)(2,1)S(1)}, bf16[32,1536]{1,0:T(8,128)(2,1)S(1)}, u32[]{:S(2)}, u32[]{:S(2)}) collective-permute-start(bf16[32,1536]{1,0:T(8,128)(2,1)S(1)} %maximum_select_fusion.4), channel_id=1, source_target_pairs={{0,4},{1,5},{2,6},{3,7},{4,0},{5,1},{6,2},{7,3},{8,12},{9,13},{10,... | collective-permute-start | bytes 294920 | tf_op jit(solution)/shard_map/ppermute | solution.py:66
  208.5 10.5 %collective-permute-start.8 = (bf16[64,1536]{1,0:T(8,128)(2,1)S(1)}, bf16[64,1536]{1,0:T(8,128)(2,1)S(1)}, u32[]{:S(2)}, u32[]{:S(2)}) collective-permute-start(bf16[64,1536]{1,0:T(8,128)(2,1)S(1)} %maximum_select_fusion.3), channel_id=1, source_target_pairs={{0,2},{1,3},{2,0},{3,1},{4,6},{5,7},{6,4},{7,5},{8,10},{9,11},{10,... | collective-permute-start | bytes 589832 | tf_op jit(solution)/shard_map/ppermute | solution.py:66
  219.1 7.7 %collective-permute-start.9 = (bf16[128,1536]{1,0:T(8,128)(2,1)S(1)}, bf16[128,1536]{1,0:T(8,128)(2,1)S(1)}, u32[]{:S(2)}, u32[]{:S(2)}) collective-permute-start(bf16[128,1536]{1,0:T(8,128)(2,1)S(1)} %maximum_select_fusion.2), channel_id=1, source_target_pairs={{0,1},{1,0},{2,3},{3,2},{4,5},{5,4},{6,7},{7,6},{8,9},{9,8},{10,11... | collective-permute-start | bytes 1179656 | tf_op jit(solution)/shard_map/ppermute | solution.py:66

commit v6 on v5

--- a/solution.py
+++ b/solution.py
@@ -45,27 +45,35 @@
     )
 
 
-def head_sum(partial):
+def head_sum(partial, chains=2):
     index = lax.axis_index("tensor")
     count = lax.axis_size("tensor")
-    cur = partial
+    curs = jnp.split(partial, chains, axis=1)
     step = 1
     while step < count:
         upper = (index & step) != 0
-        half = cur.shape[0] // 2
-        low, high = cur[:half], cur[half:]
-        keep = jnp.where(upper, high, low)
-        send = jnp.where(upper, low, high)
-        got = lax.ppermute(send.astype(jnp.bfloat16), "tensor", [(i, i ^ step) for i in range(count)])
-        cur = keep + got.astype(jnp.float32)
+        pairs = [(i, i ^ step) for i in range(count)]
+        nxt = []
+        for cur in curs:
+            half = cur.shape[0] // 2
+            low, high = cur[:half], cur[half:]
+            keep = jnp.where(upper, high, low)
+            send = jnp.where(upper, low, high)
+            got = lax.ppermute(send.astype(jnp.bfloat16), "tensor", pairs)
+            nxt.append(keep + got.astype(jnp.float32))
+        curs = nxt
         step *= 2
-    cur = cur.astype(jnp.bfloat16)
+    curs = [cur.astype(jnp.bfloat16) for cur in curs]
     while step > 1:
         step //= 2
         upper = (index & step) != 0
-        got = lax.ppermute(cur, "tensor", [(i, i ^ step) for i in range(count)])
-        cur = jnp.where(upper, jnp.concatenate([got, cur]), jnp.concatenate([cur, got]))
-    return cur.astype(jnp.float32)
+        pairs = [(i, i ^ step) for i in range(count)]
+        nxt = []
+        for cur in curs:
+            got = lax.ppermute(cur, "tensor", pairs)
+            nxt.append(jnp.where(upper, jnp.concatenate([got, cur]), jnp.concatenate([cur, got])))
+        curs = nxt
+    return jnp.concatenate(curs, axis=1).astype(jnp.float32)
 
 
 def local(normed, grad_out, w_query, w_key, w_value, w_out, key_span):

time: 229 us -> 233 us (1.017)
  starting transfers between devices: 118 us -> 137 us
  waiting for transfers between devices: 48.5 us -> 32.6 us
    ppermute x8 -> x16, starting transfers between devices: 48.6 us -> 67.4 us  [the longest x8 35.8 us: head_sum(): got = lax.ppermute(send.astype(jnp.bfloat16), 'tensor', pairs)]
    ppermute x8 -> x16, waiting for transfers between devices: 22.3 us -> 6.33 us  [the longest x8 3.87 us: head_sum(): got = lax.ppermute(cur, 'tensor', pairs)]
  transfers between devices with their start and end apart: 13 -> 21, of which waited for: 11 -> 7; matrix products, arithmetic and copies ran while one was open for 3% -> 3% of each run, Pallas kernels for 0% -> 0%
where the time goes in v6:
time: 233 us; the launch traced here: 231 us
  starting transfers between devices  137 us (59%)
  waiting for transfers between devices  32.6 us (14%)
  blocking collectives  30.1 us (13%)
  matrix products  14.6 us (6%)
  local copies, waits for them, and re-layouts  11.7 us (5%)
  other arithmetic  4.99 us (2%)
    ppermute x8, starting transfers between devices, head_sum(): got = lax.ppermute(send.astype(jnp.bfloat16), 'tensor', pairs)  35.8 us
    ppermute x8, starting transfers between devices, head_sum(): got = lax.ppermute(cur, 'tensor', pairs)  31.5 us
    all_to_all x1, blocking collectives, local(): lax.all_to_all(lax.dynamic_index_in_dim(returned, 1 - my_side, axis=1, ke...  30.1 us
    ppermute x1, starting transfers between devices, local(): other_back = lax.ppermute(other, 'zh', swap)  23.4 us
    all_to_all x1, waiting for transfers between devices, local(): lax.all_to_all(mirror_spans[mirror_slot], 'tq', split_axis=0, concat_axis...  21.9 us
    ppermute x1, starting transfers between devices, local(): mirror_spans = lax.ppermute(paired_spans, 'zh', swap)  19.1 us
    all_to_all x1, starting transfers between devices, local(): lax.all_to_all(paired_spans[own_slot], 'tq', split_axis=0, concat_axis=0,...  10.5 us
    all_to_all x1, starting transfers between devices, local(): lax.all_to_all(mirror_spans[mirror_slot], 'tq', split_axis=0, concat_axis...  9.5 us
  transfers between devices with their start and end apart: 21, of which 7 were waited for; matrix products, arithmetic and copies ran while one was open for 3% of the time, Pallas kernels for 0%

profile of v6, /device:TPU:1, one launch (start us, length us, event | category | flops | bytes accessed | tf_op | source)
XLA Modules:
  0.0 231.4 jit_solution(8578903769500199108)
XLA Ops:
  6.5 10.5 %all-to-all-start = ((bf16[32,128,128]{2,1,0:T(8,128)(2,1)}), bf16[32,128,128]{2,1,0:T(8,128)(2,1)S(1)}, u32[]{:S(2)}, u32[]{:S(2)}) async-start(bf16[32,128,128]{2,1,0:T(8,128)(2,1)} %gather_fusion), calls=%async_computation | async-start | bytes 2097152 | tf_op jit(solution)/shard_map/all_to_all | solution.py:109
  17.0 19.1 %collective-permute-start = (bf16[2,128,128]{2,1,0:T(8,128)(2,1)S(1)}, bf16[2,128,128]{2,1,0:T(8,128)(2,1)S(1)}, u32[]{:S(2)}, u32[]{:S(2)}) collective-permute-start(bf16[2,128,128]{2,1,0:T(8,128)(2,1)S(1)} %bitcast_bitcast_fusion), channel_id=1, source_target_pairs={{0,16},{16,0},{1,17},{17,1},{2,18},{18,2},{3,19},{19,3},{4,20},{20... | collective-permute-start | bytes 196616 | tf_op jit(solution)/shard_map/ppermute | solution.py:100
  39.5 9.5 %all-to-all-start.1 = ((bf16[32,128,128]{2,1,0:T(8,128)(2,1)}), bf16[32,128,128]{2,1,0:T(8,128)(2,1)S(1)}, u32[]{:S(2)}, u32[]{:S(2)}) async-start(bf16[32,128,128]{2,1,0:T(8,128)(2,1)} %gather_fusion.1), calls=%async_computation.1 | async-start | bytes 2097152 | tf_op jit(solution)/shard_map/all_to_all | solution.py:110
  51.0 21.9 %all-to-all-done.1 = bf16[32,128,128]{2,1,0:T(8,128)(2,1)S(1)} async-done(((bf16[32,128,128]{2,1,0:T(8,128)(2,1)}), bf16[32,128,128]{2,1,0:T(8,128)(2,1)S(1)}, u32[]{:S(2)}, u32[]{:S(2)}) %all-to-all-start.1) | async-done | bytes 1048608 | tf_op jit(solution)/shard_map/all_to_all | solution.py:110
  81.3 3.6 %scatter_fusion = bf16[64,128,128]{2,1,0:T(8,128)(2,1)S(1)} fusion(bf16[64,128,128]{2,1,0:T(8,128)(2,1)S(1)} %broadcast_in_dim.16, s32[32]{0:T(128)S(1)} %get-tuple-element.19, bf16[32,128,128]{2,1,0:T(8,128)(2,1)} %pad_maximum_fusion), kind=kCustom, calls=%fused_computation.3 | custom fusion | bytes 3145856 | tf_op jit(solution)/shard_map/scatter | solution.py:133
  86.0 30.1 %all_to_all.20 = bf16[32,128,128]{2,1,0:T(8,128)(2,1)} all-to-all(bf16[32,128,128]{2,1,0:T(8,128)(2,1)S(1)} %get-tuple-element.6), channel_id=1, replica_groups=mesh['tq'=32,'zh'=2,'tensor'=16] {'tq'}, dimensions={0} | all-to-all | bytes 2097152 | tf_op jit(solution)/shard_map/all_to_all | solution.py:139
  116.1 6.8 %all-to-all-start.2 = ((bf16[32,128,128]{2,1,0:T(8,128)(2,1)}), bf16[32,128,128]{2,1,0:T(8,128)(2,1)}, u32[]{:S(2)}, u32[]{:S(2)}) async-start(bf16[32,128,128]{2,1,0:T(8,128)(2,1)} %get-tuple-element.5), calls=%async_computation.2 | async-start | bytes 2097152 | tf_op jit(solution)/shard_map/all_to_all | solution.py:150
  123.1 2.6 %fusion.10 = f32[2,128,128]{2,0,1:T(2,128)} fusion(bf16[32,128,128]{2,1,0:T(8,128)(2,1)} %all_to_all.20, pred[32,2,2]{0,2,1:T(4,128)(4,1)S(1)} %compare_and_fusion, s32[]{:T(128)S(6)} %select_n.220), kind=kOutput, calls=%fused_computation.30 | convolution fusion | flops 2097152 | bytes 1180164 | tf_op jit(solution)/shard_map/ck,crh->krh/dot_general | solution.py:143
  125.7 23.4 %collective-permute-start.1 = (f32[2,128,128]{2,0,1:T(2,128)}, f32[2,128,128]{2,0,1:T(2,128)}, u32[]{:S(2)}, u32[]{:S(2)}) collective-permute-start(f32[2,128,128]{2,0,1:T(2,128)} %fusion.10), channel_id=1, source_target_pairs={{0,16},{16,0},{1,17},{17,1},{2,18},{18,2},{3,19},{19,3},{4,20},{20... | collective-permute-start | bytes 393224 | tf_op jit(solution)/shard_map/ppermute | solution.py:149
  149.5 2.6 %collective-permute-done.1 = f32[2,128,128]{2,0,1:T(2,128)} collective-permute-done((f32[2,128,128]{2,0,1:T(2,128)}, f32[2,128,128]{2,0,1:T(2,128)}, u32[]{:S(2)}, u32[]{:S(2)}) %collective-permute-start.1) | collective-permute-done | bytes 131104 | tf_op jit(solution)/shard_map/ppermute | solution.py:149
  155.3 5.3 %collective-permute-start.2 = (bf16[128,768]{1,0:T(8,128)(2,1)S(1)}, bf16[128,768]{1,0:T(8,128)(2,1)S(1)}, u32[]{:S(2)}, u32[]{:S(2)}) collective-permute-start(bf16[128,768]{1,0:T(8,128)(2,1)S(1)} %get-tuple-element.9), channel_id=1, source_target_pairs={{0,1},{1,0},{2,3},{3,2},{4,5},{5,4},{6,7},{7,6},{8,9},{9,8},{10,11... | collective-permute-start | bytes 589832 | tf_op jit(solution)/shard_map/ppermute | solution.py:62
  164.1 9.8 %collective-permute-start.3 = (bf16[64,768]{1,0:T(8,128)(2,1)S(1)}, bf16[64,768]{1,0:T(8,128)(2,1)S(1)}, u32[]{:S(2)}, u32[]{:S(2)}) collective-permute-start(bf16[64,768]{1,0:T(8,128)(2,1)S(1)} %select_convert_fusion.3), channel_id=1, source_target_pairs={{0,2},{1,3},{2,0},{3,1},{4,6},{5,7},{6,4},{7,5},{8,10},{9,11},{10,... | collective-permute-start | bytes 294920 | tf_op jit(solution)/shard_map/ppermute | solution.py:62
  177.0 3.0 %collective-permute-start.4 = (bf16[32,768]{1,0:T(8,128)(2,1)S(1)}, bf16[32,768]{1,0:T(8,128)(2,1)S(1)}, u32[]{:S(2)}, u32[]{:S(2)}) collective-permute-start(bf16[32,768]{1,0:T(8,128)(2,1)S(1)} %select_convert_fusion.5), channel_id=1, source_target_pairs={{0,4},{1,5},{2,6},{3,7},{4,0},{5,1},{6,2},{7,3},{8,12},{9,13},{10,... | collective-permute-start | bytes 147464 | tf_op jit(solution)/shard_map/ppermute | solution.py:62
  180.2 3.1 %collective-permute-start.12 = (bf16[32,768]{1,0:T(8,128)(2,1)S(1)}, bf16[32,768]{1,0:T(8,128)(2,1)S(1)}, u32[]{:S(2)}, u32[]{:S(2)}) collective-permute-start(bf16[32,768]{1,0:T(8,128)(2,1)S(1)} %select_convert_fusion.4), channel_id=1, source_target_pairs={{0,4},{1,5},{2,6},{3,7},{4,0},{5,1},{6,2},{7,3},{8,12},{9,13},{10,... | collective-permute-start | bytes 147464 | tf_op jit(solution)/shard_map/ppermute | solution.py:62
  183.4 7.8 %collective-permute-start.5 = (bf16[16,768]{1,0:T(8,128)(2,1)S(1)}, bf16[16,768]{1,0:T(8,128)(2,1)S(1)}, u32[]{:S(2)}, u32[]{:S(2)}) collective-permute-start(bf16[16,768]{1,0:T(8,128)(2,1)S(1)} %select_convert_fusion.7), channel_id=1, source_target_pairs={{0,8},{1,9},{2,10},{3,11},{4,12},{5,13},{6,14},{7,15},{8,0},{9,1},... | collective-permute-start | bytes 73736 | tf_op jit(solution)/shard_map/ppermute | solution.py:62
  191.2 2.9 %collective-permute-start.13 = (bf16[16,768]{1,0:T(8,128)(2,1)S(1)}, bf16[16,768]{1,0:T(8,128)(2,1)S(1)}, u32[]{:S(2)}, u32[]{:S(2)}) collective-permute-start(bf16[16,768]{1,0:T(8,128)(2,1)S(1)} %select_convert_fusion.6), channel_id=1, source_target_pairs={{0,8},{1,9},{2,10},{3,11},{4,12},{5,13},{6,14},{7,15},{8,0},{9,1},... | collective-permute-start | bytes 73736 | tf_op jit(solution)/shard_map/ppermute | solution.py:62
  194.1 6.3 %collective-permute-start.6 = (bf16[16,768]{1,0:T(8,128)(2,1)S(1)}, bf16[16,768]{1,0:T(8,128)(2,1)S(1)}, u32[]{:S(2)}, u32[]{:S(2)}) collective-permute-start(bf16[16,768]{1,0:T(8,128)(2,1)S(1)} %add_convert_fusion.1), channel_id=1, source_target_pairs={{0,8},{1,9},{2,10},{3,11},{4,12},{5,13},{6,14},{7,15},{8,0},{9,1},... | collective-permute-start | bytes 73736 | tf_op jit(solution)/shard_map/ppermute | solution.py:73
  200.5 2.9 %collective-permute-start.14 = (bf16[16,768]{1,0:T(8,128)(2,1)S(1)}, bf16[16,768]{1,0:T(8,128)(2,1)S(1)}, u32[]{:S(2)}, u32[]{:S(2)}) collective-permute-start(bf16[16,768]{1,0:T(8,128)(2,1)S(1)} %add_convert_fusion), channel_id=1, source_target_pairs={{0,8},{1,9},{2,10},{3,11},{4,12},{5,13},{6,14},{7,15},{8,0},{9,1},... | collective-permute-start | bytes 73736 | tf_op jit(solution)/shard_map/ppermute | solution.py:73
  203.4 2.8 %collective-permute-start.7 = (bf16[32,768]{1,0:T(8,128)(2,1)S(1)}, bf16[32,768]{1,0:T(8,128)(2,1)S(1)}, u32[]{:S(2)}, u32[]{:S(2)}) collective-permute-start(bf16[32,768]{1,0:T(8,128)(2,1)S(1)} %maximum_select_fusion.7), channel_id=1, source_target_pairs={{0,4},{1,5},{2,6},{3,7},{4,0},{5,1},{6,2},{7,3},{8,12},{9,13},{10,... | collective-permute-start | bytes 147464 | tf_op jit(solution)/shard_map/ppermute | solution.py:73
  206.2 2.9 %collective-permute-done.14 = bf16[16,768]{1,0:T(8,128)(2,1)S(1)} collective-permute-done((bf16[16,768]{1,0:T(8,128)(2,1)S(1)}, bf16[16,768]{1,0:T(8,128)(2,1)S(1)}, u32[]{:S(2)}, u32[]{:S(2)}) %collective-permute-start.14) | collective-permute-done | bytes 24608 | tf_op jit(solution)/shard_map/ppermute | solution.py:73
  209.1 3.4 %collective-permute-start.15 = (bf16[32,768]{1,0:T(8,128)(2,1)S(1)}, bf16[32,768]{1,0:T(8,128)(2,1)S(1)}, u32[]{:S(2)}, u32[]{:S(2)}) collective-permute-start(bf16[32,768]{1,0:T(8,128)(2,1)S(1)} %maximum_select_fusion.8), channel_id=1, source_target_pairs={{0,4},{1,5},{2,6},{3,7},{4,0},{5,1},{6,2},{7,3},{8,12},{9,13},{10,... | collective-permute-start | bytes 147464 | tf_op jit(solution)/shard_map/ppermute | solution.py:73
  212.5 3.0 %collective-permute-start.8 = (bf16[64,768]{1,0:T(8,128)(2,1)S(1)}, bf16[64,768]{1,0:T(8,128)(2,1)S(1)}, u32[]{:S(2)}, u32[]{:S(2)}) collective-permute-start(bf16[64,768]{1,0:T(8,128)(2,1)S(1)} %maximum_select_fusion.5), channel_id=1, source_target_pairs={{0,2},{1,3},{2,0},{3,1},{4,6},{5,7},{6,4},{7,5},{8,10},{9,11},{10,... | collective-permute-start | bytes 294920 | tf_op jit(solution)/shard_map/ppermute | solution.py:73
  217.9 7.0 %collective-permute-start.9 = (bf16[128,768]{1,0:T(8,128)(2,1)S(1)}, bf16[128,768]{1,0:T(8,128)(2,1)S(1)}, u32[]{:S(2)}, u32[]{:S(2)}) collective-permute-start(bf16[128,768]{1,0:T(8,128)(2,1)S(1)} %maximum_select_fusion.3), channel_id=1, source_target_pairs={{0,1},{1,0},{2,3},{3,2},{4,5},{5,4},{6,7},{7,6},{8,9},{9,8},{10,11... | collective-permute-start | bytes 589832 | tf_op jit(solution)/shard_map/ppermute | solution.py:73
  225.0 3.9 %collective-permute-start.17 = (bf16[128,768]{1,0:T(8,128)(2,1)S(1)}, bf16[128,768]{1,0:T(8,128)(2,1)S(1)}, u32[]{:S(2)}, u32[]{:S(2)}) collective-permute-start(bf16[128,768]{1,0:T(8,128)(2,1)S(1)} %maximum_select_fusion.4), channel_id=1, source_target_pairs={{0,1},{1,0},{2,3},{3,2},{4,5},{5,4},{6,7},{7,6},{8,9},{9,8},{10,11... | collective-permute-start | bytes 589832 | tf_op jit(solution)/shard_map/ppermute | solution.py:73
  (105 shorter events, 36.5 us)
Async XLA Ops:
  6.5 33.1 %all-to-all-start = ((bf16[32,128,128]{2,1,0:T(8,128)(2,1)}), bf16[32,128,128]{2,1,0:T(8,128)(2,1)S(1)}, u32[]{:S(2)}, u32[]{:S(2)}) async-start(bf16[32,128,128]{2,1,0:T(8,128)(2,1)} %gather_fusion), calls=%async_computation | async-start | bytes 2097152 | tf_op jit(solution)/shard_map/all_to_all | solution.py:109
  17.0 20.9 %collective-permute-start = (bf16[2,128,128]{2,1,0:T(8,128)(2,1)S(1)}, bf16[2,128,128]{2,1,0:T(8,128)(2,1)S(1)}, u32[]{:S(2)}, u32[]{:S(2)}) collective-permute-start(bf16[2,128,128]{2,1,0:T(8,128)(2,1)S(1)} %bitcast_bitcast_fusion), channel_id=1, source_target_pairs={{0,16},{16,0},{1,17},{17,1},{2,18},{18,2},{3,19},{19,3},{4,20},{20... | collective-permute-start | bytes 196616 | tf_op jit(solution)/shard_map/ppermute | solution.py:100
  39.5 33.4 %all-to-all-start.1 = ((bf16[32,128,128]{2,1,0:T(8,128)(2,1)}), bf16[32,128,128]{2,1,0:T(8,128)(2,1)S(1)}, u32[]{:S(2)}, u32[]{:S(2)}) async-start(bf16[32,128,128]{2,1,0:T(8,128)(2,1)} %gather_fusion.1), calls=%async_computation.1 | async-start | bytes 2097152 | tf_op jit(solution)/shard_map/all_to_all | solution.py:110
  116.1 33.0 %copy-start.2 = (bf16[32,128,128]{2,1,0:T(8,128)(2,1)S(1)}, bf16[32,128,128]{2,1,0:T(8,128)(2,1)}, u32[]{:S(2)}) copy-start(bf16[32,128,128]{2,1,0:T(8,128)(2,1)} %gather_fusion.2) | copy-start | bytes 3145732
  116.1 33.1 %copy-start.4 = (bf16[2,128,16,128]{1,3,2,0:T(8,128)(2,1)S(1)}, bf16[2,128,16,128]{1,3,2,0:T(8,128)(2,1)}, u32[]{:S(2)}) copy-start(bf16[2,128,16,128]{1,3,2,0:T(8,128)(2,1)} %copy-done.3) | copy-start | bytes 3145732
  116.1 33.4 %all-to-all-start.2 = ((bf16[32,128,128]{2,1,0:T(8,128)(2,1)}), bf16[32,128,128]{2,1,0:T(8,128)(2,1)}, u32[]{:S(2)}, u32[]{:S(2)}) async-start(bf16[32,128,128]{2,1,0:T(8,128)(2,1)} %get-tuple-element.5), calls=%async_computation.2 | async-start | bytes 2097152 | tf_op jit(solution)/shard_map/all_to_all | solution.py:150
  123.1 31.0 %copy-start.5 = (bf16[1536,64]{0,1:T(8,128)(2,1)S(1)}, bf16[1536,64]{0,1:T(8,128)(2,1)}, u32[]{:S(2)}) copy-start(bf16[1536,64]{0,1:T(8,128)(2,1)} %param.10) | copy-start | bytes 589828
  125.7 26.4 %collective-permute-start.1 = (f32[2,128,128]{2,0,1:T(2,128)}, f32[2,128,128]{2,0,1:T(2,128)}, u32[]{:S(2)}, u32[]{:S(2)}) collective-permute-start(f32[2,128,128]{2,0,1:T(2,128)} %fusion.10), channel_id=1, source_target_pairs={{0,16},{16,0},{1,17},{17,1},{2,18},{18,2},{3,19},{19,3},{4,20},{20... | collective-permute-start | bytes 393224 | tf_op jit(solution)/shard_map/ppermute | solution.py:149
  155.3 7.3 %collective-permute-start.2 = (bf16[128,768]{1,0:T(8,128)(2,1)S(1)}, bf16[128,768]{1,0:T(8,128)(2,1)S(1)}, u32[]{:S(2)}, u32[]{:S(2)}) collective-permute-start(bf16[128,768]{1,0:T(8,128)(2,1)S(1)} %get-tuple-element.9), channel_id=1, source_target_pairs={{0,1},{1,0},{2,3},{3,2},{4,5},{5,4},{6,7},{7,6},{8,9},{9,8},{10,11... | collective-permute-start | bytes 589832 | tf_op jit(solution)/shard_map/ppermute | solution.py:62
  160.7 3.3 %collective-permute-start.10 = (bf16[128,768]{1,0:T(8,128)(2,1)S(1)}, bf16[128,768]{1,0:T(8,128)(2,1)S(1)}, u32[]{:S(2)}, u32[]{:S(2)}) collective-permute-start(bf16[128,768]{1,0:T(8,128)(2,1)S(1)} %get-tuple-element.10), channel_id=1, source_target_pairs={{0,1},{1,0},{2,3},{3,2},{4,5},{5,4},{6,7},{7,6},{8,9},{9,8},{10,11... | collective-permute-start | bytes 589832 | tf_op jit(solution)/shard_map/ppermute | solution.py:62
  164.1 12.8 %collective-permute-start.3 = (bf16[64,768]{1,0:T(8,128)(2,1)S(1)}, bf16[64,768]{1,0:T(8,128)(2,1)S(1)}, u32[]{:S(2)}, u32[]{:S(2)}) collective-permute-start(bf16[64,768]{1,0:T(8,128)(2,1)S(1)} %select_convert_fusion.3), channel_id=1, source_target_pairs={{0,2},{1,3},{2,0},{3,1},{4,6},{5,7},{6,4},{7,5},{8,10},{9,11},{10,... | collective-permute-start | bytes 294920 | tf_op jit(solution)/shard_map/ppermute | solution.py:62
  174.0 6.1 %collective-permute-start.11 = (bf16[64,768]{1,0:T(8,128)(2,1)S(1)}, bf16[64,768]{1,0:T(8,128)(2,1)S(1)}, u32[]{:S(2)}, u32[]{:S(2)}) collective-permute-start(bf16[64,768]{1,0:T(8,128)(2,1)S(1)} %select_convert_fusion.2), channel_id=1, source_target_pairs={{0,2},{1,3},{2,0},{3,1},{4,6},{5,7},{6,4},{7,5},{8,10},{9,11},{10,... | collective-permute-start | bytes 294920 | tf_op jit(solution)/shard_map/ppermute | solution.py:62
  177.0 6.3 %collective-permute-start.4 = (bf16[32,768]{1,0:T(8,128)(2,1)S(1)}, bf16[32,768]{1,0:T(8,128)(2,1)S(1)}, u32[]{:S(2)}, u32[]{:S(2)}) collective-permute-start(bf16[32,768]{1,0:T(8,128)(2,1)S(1)} %select_convert_fusion.5), channel_id=1, source_target_pairs={{0,4},{1,5},{2,6},{3,7},{4,0},{5,1},{6,2},{7,3},{8,12},{9,13},{10,... | collective-permute-start | bytes 147464 | tf_op jit(solution)/shard_map/ppermute | solution.py:62
  180.2 11.0 %collective-permute-start.12 = (bf16[32,768]{1,0:T(8,128)(2,1)S(1)}, bf16[32,768]{1,0:T(8,128)(2,1)S(1)}, u32[]{:S(2)}, u32[]{:S(2)}) collective-permute-start(bf16[32,768]{1,0:T(8,128)(2,1)S(1)} %select_convert_fusion.4), channel_id=1, source_target_pairs={{0,4},{1,5},{2,6},{3,7},{4,0},{5,1},{6,2},{7,3},{8,12},{9,13},{10,... | collective-permute-start | bytes 147464 | tf_op jit(solution)/shard_map/ppermute | solution.py:62
  183.4 10.8 %collective-permute-start.5 = (bf16[16,768]{1,0:T(8,128)(2,1)S(1)}, bf16[16,768]{1,0:T(8,128)(2,1)S(1)}, u32[]{:S(2)}, u32[]{:S(2)}) collective-permute-start(bf16[16,768]{1,0:T(8,128)(2,1)S(1)} %select_convert_fusion.7), channel_id=1, source_target_pairs={{0,8},{1,9},{2,10},{3,11},{4,12},{5,13},{6,14},{7,15},{8,0},{9,1},... | collective-permute-start | bytes 73736 | tf_op jit(solution)/shard_map/ppermute | solution.py:62
  191.2 9.2 %collective-permute-start.13 = (bf16[16,768]{1,0:T(8,128)(2,1)S(1)}, bf16[16,768]{1,0:T(8,128)(2,1)S(1)}, u32[]{:S(2)}, u32[]{:S(2)}) collective-permute-start(bf16[16,768]{1,0:T(8,128)(2,1)S(1)} %select_convert_fusion.6), channel_id=1, source_target_pairs={{0,8},{1,9},{2,10},{3,11},{4,12},{5,13},{6,14},{7,15},{8,0},{9,1},... | collective-permute-start | bytes 73736 | tf_op jit(solution)/shard_map/ppermute | solution.py:62
  194.1 9.2 %collective-permute-start.6 = (bf16[16,768]{1,0:T(8,128)(2,1)S(1)}, bf16[16,768]{1,0:T(8,128)(2,1)S(1)}, u32[]{:S(2)}, u32[]{:S(2)}) collective-permute-start(bf16[16,768]{1,0:T(8,128)(2,1)S(1)} %add_convert_fusion.1), channel_id=1, source_target_pairs={{0,8},{1,9},{2,10},{3,11},{4,12},{5,13},{6,14},{7,15},{8,0},{9,1},... | collective-permute-start | bytes 73736 | tf_op jit(solution)/shard_map/ppermute | solution.py:73
  200.5 8.6 %collective-permute-start.14 = (bf16[16,768]{1,0:T(8,128)(2,1)S(1)}, bf16[16,768]{1,0:T(8,128)(2,1)S(1)}, u32[]{:S(2)}, u32[]{:S(2)}) collective-permute-start(bf16[16,768]{1,0:T(8,128)(2,1)S(1)} %add_convert_fusion), channel_id=1, source_target_pairs={{0,8},{1,9},{2,10},{3,11},{4,12},{5,13},{6,14},{7,15},{8,0},{9,1},... | collective-permute-start | bytes 73736 | tf_op jit(solution)/shard_map/ppermute | solution.py:73
  203.4 9.1 %collective-permute-start.7 = (bf16[32,768]{1,0:T(8,128)(2,1)S(1)}, bf16[32,768]{1,0:T(8,128)(2,1)S(1)}, u32[]{:S(2)}, u32[]{:S(2)}) collective-permute-start(bf16[32,768]{1,0:T(8,128)(2,1)S(1)} %maximum_select_fusion.7), channel_id=1, source_target_pairs={{0,4},{1,5},{2,6},{3,7},{4,0},{5,1},{6,2},{7,3},{8,12},{9,13},{10,... | collective-permute-start | bytes 147464 | tf_op jit(solution)/shard_map/ppermute | solution.py:73
  209.1 6.5 %collective-permute-start.15 = (bf16[32,768]{1,0:T(8,128)(2,1)S(1)}, bf16[32,768]{1,0:T(8,128)(2,1)S(1)}, u32[]{:S(2)}, u32[]{:S(2)}) collective-permute-start(bf16[32,768]{1,0:T(8,128)(2,1)S(1)} %maximum_select_fusion.8), channel_id=1, source_target_pairs={{0,4},{1,5},{2,6},{3,7},{4,0},{5,1},{6,2},{7,3},{8,12},{9,13},{10,... | collective-permute-start | bytes 147464 | tf_op jit(solution)/shard_map/ppermute | solution.py:73
  212.5 5.4 %collective-permute-start.8 = (bf16[64,768]{1,0:T(8,128)(2,1)S(1)}, bf16[64,768]{1,0:T(8,128)(2,1)S(1)}, u32[]{:S(2)}, u32[]{:S(2)}) collective-permute-start(bf16[64,768]{1,0:T(8,128)(2,1)S(1)} %maximum_select_fusion.5), channel_id=1, source_target_pairs={{0,2},{1,3},{2,0},{3,1},{4,6},{5,7},{6,4},{7,5},{8,10},{9,11},{10,... | collective-permute-start | bytes 294920 | tf_op jit(solution)/shard_map/ppermute | solution.py:73
  215.6 9.4 %collective-permute-start.16 = (bf16[64,768]{1,0:T(8,128)(2,1)S(1)}, bf16[64,768]{1,0:T(8,128)(2,1)S(1)}, u32[]{:S(2)}, u32[]{:S(2)}) collective-permute-start(bf16[64,768]{1,0:T(8,128)(2,1)S(1)} %maximum_select_fusion.6), channel_id=1, source_target_pairs={{0,2},{1,3},{2,0},{3,1},{4,6},{5,7},{6,4},{7,5},{8,10},{9,11},{10,... | collective-permute-start | bytes 294920 | tf_op jit(solution)/shard_map/ppermute | solution.py:73
  217.9 11.0 %collective-permute-start.9 = (bf16[128,768]{1,0:T(8,128)(2,1)S(1)}, bf16[128,768]{1,0:T(8,128)(2,1)S(1)}, u32[]{:S(2)}, u32[]{:S(2)}) collective-permute-start(bf16[128,768]{1,0:T(8,128)(2,1)S(1)} %maximum_select_fusion.3), channel_id=1, source_target_pairs={{0,1},{1,0},{2,3},{3,2},{4,5},{5,4},{6,7},{7,6},{8,9},{9,8},{10,11... | collective-permute-start | bytes 589832 | tf_op jit(solution)/shard_map/ppermute | solution.py:73
  225.0 5.0 %collective-permute-start.17 = (bf16[128,768]{1,0:T(8,128)(2,1)S(1)}, bf16[128,768]{1,0:T(8,128)(2,1)S(1)}, u32[]{:S(2)}, u32[]{:S(2)}) collective-permute-start(bf16[128,768]{1,0:T(8,128)(2,1)S(1)} %maximum_select_fusion.4), channel_id=1, source_target_pairs={{0,1},{1,0},{2,3},{3,2},{4,5},{5,4},{6,7},{7,6},{8,9},{9,8},{10,11... | collective-permute-start | bytes 589832 | tf_op jit(solution)/shard_map/ppermute | solution.py:73
  (6 other events, 58.2 us)

commit v7 on v5

--- a/solution.py
+++ b/solution.py
@@ -45,26 +45,35 @@
     )
 
 
-def head_sum(partial):
+def head_sum(partial, radix=4):
     index = lax.axis_index("tensor")
     count = lax.axis_size("tensor")
+    width = partial.shape[1]
+    strides = []
+    stride = 1
+    while stride < count:
+        strides.append(stride)
+        stride *= radix
+
+    def pairs(stride, flip):
+        return [(i, i + ((((i // stride) % radix) ^ flip) - (i // stride) % radix) * stride) for i in range(count)]
+
     cur = partial
-    step = 1
-    while step < count:
-        upper = (index & step) != 0
-        half = cur.shape[0] // 2
-        low, high = cur[:half], cur[half:]
-        keep = jnp.where(upper, high, low)
-        send = jnp.where(upper, low, high)
-        got = lax.ppermute(send.astype(jnp.bfloat16), "tensor", [(i, i ^ step) for i in range(count)])
-        cur = keep + got.astype(jnp.float32)
-        step *= 2
+    for stride in strides:
+        digit = (index // stride) % radix
+        blocks = cur.reshape(radix, cur.shape[0] // radix, width)
+        total = lax.dynamic_index_in_dim(blocks, digit, axis=0, keepdims=False)
+        for flip in range(1, radix):
+            send = lax.dynamic_index_in_dim(blocks, digit ^ flip, axis=0, keepdims=False)
+            got = lax.ppermute(send.astype(jnp.bfloat16), "tensor", pairs(stride, flip))
+            total = total + got.astype(jnp.float32)
+        cur = total
     cur = cur.astype(jnp.bfloat16)
-    while step > 1:
-        step //= 2
-        upper = (index & step) != 0
-        got = lax.ppermute(cur, "tensor", [(i, i ^ step) for i in range(count)])
-        cur = jnp.where(upper, jnp.concatenate([got, cur]), jnp.concatenate([cur, got]))
+    for stride in reversed(strides):
+        digit = (index // stride) % radix
+        gots = [cur] + [lax.ppermute(cur, "tensor", pairs(stride, flip)) for flip in range(1, radix)]
+        order = digit ^ jnp.arange(radix, dtype=digit.dtype)
+        cur = jnp.take(jnp.stack(gots), order, axis=0).reshape(-1, width)
     return cur.astype(jnp.float32)
 
 

time: 229 us -> 238 us (1.039)
  waiting for transfers between devices: 48.5 us -> 53.1 us
    ppermute x8 -> x12, waiting for transfers between devices: 22.3 us -> 26.9 us  [the longest x6 17.6 us: head_sum(): got = lax.ppermute(send.astype(jnp.bfloat16), 'tensor', pairs(stride, flip))]
    ppermute x8 -> x12, starting transfers between devices: 48.6 us -> 51.2 us  [the longest x6 30.1 us: head_sum(): got = lax.ppermute(send.astype(jnp.bfloat16), 'tensor', pairs(stride, flip))]
  transfers between devices with their start and end apart: 13 -> 17, of which waited for: 11 -> 11; matrix products, arithmetic and copies ran while one was open for 3% -> 3% of each run, Pallas kernels for 0% -> 0%
where the time goes in v7:
time: 238 us; the launch traced here: 237 us
  starting transfers between devices  120 us (50%)
  waiting for transfers between devices  53.1 us (22%)
  blocking collectives  30.1 us (13%)
  matrix products  14.6 us (6%)
  local copies, waits for them, and re-layouts  13.3 us (6%)
  other arithmetic  4.81 us (2%)
    ppermute x6, starting transfers between devices, head_sum(): got = lax.ppermute(send.astype(jnp.bfloat16), 'tensor', pairs(stride, flip))  30.1 us
    all_to_all x1, blocking collectives, local(): lax.all_to_all(lax.dynamic_index_in_dim(returned, 1 - my_side, axis=1, ke...  30.1 us
    ppermute x1, starting transfers between devices, local(): other_back = lax.ppermute(other, 'zh', swap)  23.4 us
    all_to_all x1, waiting for transfers between devices, local(): lax.all_to_all(mirror_spans[mirror_slot], 'tq', split_axis=0, concat_axis...  21.9 us
    ppermute x6, starting transfers between devices, head_sum(): lax.ppermute(cur, 'tensor', pairs(stride, flip))  21 us
    ppermute x1, starting transfers between devices, local(): mirror_spans = lax.ppermute(paired_spans, 'zh', swap)  19.1 us
    ppermute x6, waiting for transfers between devices, head_sum(): got = lax.ppermute(send.astype(jnp.bfloat16), 'tensor', pairs(stride, flip))  17.6 us
    all_to_all x1, starting transfers between devices, local(): lax.all_to_all(paired_spans[own_slot], 'tq', split_axis=0, concat_axis=0,...  10.5 us
  transfers between devices with their start and end apart: 17, of which 11 were waited for; matrix products, arithmetic and copies ran while one was open for 3% of the time, Pallas kernels for 0%

profile of v7, /device:TPU:1, one launch (start us, length us, event | category | flops | bytes accessed | tf_op | source)
XLA Modules:
  0.0 237.0 jit_solution(13330110683970785954)
XLA Ops:
  6.4 10.5 %all-to-all-start = ((bf16[32,128,128]{2,1,0:T(8,128)(2,1)}), bf16[32,128,128]{2,1,0:T(8,128)(2,1)S(1)}, u32[]{:S(2)}, u32[]{:S(2)}) async-start(bf16[32,128,128]{2,1,0:T(8,128)(2,1)} %gather_fusion), calls=%async_computation | async-start | bytes 2097152 | tf_op jit(solution)/shard_map/all_to_all | solution.py:110
  16.9 19.1 %collective-permute-start = (bf16[2,128,128]{2,1,0:T(8,128)(2,1)S(1)}, bf16[2,128,128]{2,1,0:T(8,128)(2,1)S(1)}, u32[]{:S(2)}, u32[]{:S(2)}) collective-permute-start(bf16[2,128,128]{2,1,0:T(8,128)(2,1)S(1)} %bitcast_bitcast_fusion), channel_id=1, source_target_pairs={{0,16},{16,0},{1,17},{17,1},{2,18},{18,2},{3,19},{19,3},{4,20},{20... | collective-permute-start | bytes 196616 | tf_op jit(solution)/shard_map/ppermute | solution.py:101
  39.5 9.5 %all-to-all-start.1 = ((bf16[32,128,128]{2,1,0:T(8,128)(2,1)}), bf16[32,128,128]{2,1,0:T(8,128)(2,1)S(1)}, u32[]{:S(2)}, u32[]{:S(2)}) async-start(bf16[32,128,128]{2,1,0:T(8,128)(2,1)} %gather_fusion.1), calls=%async_computation.1 | async-start | bytes 2097152 | tf_op jit(solution)/shard_map/all_to_all | solution.py:111
  50.9 21.9 %all-to-all-done.1 = bf16[32,128,128]{2,1,0:T(8,128)(2,1)S(1)} async-done(((bf16[32,128,128]{2,1,0:T(8,128)(2,1)}), bf16[32,128,128]{2,1,0:T(8,128)(2,1)S(1)}, u32[]{:S(2)}, u32[]{:S(2)}) %all-to-all-start.1) | async-done | bytes 1048608 | tf_op jit(solution)/shard_map/all_to_all | solution.py:111
  81.3 3.6 %scatter_fusion = bf16[64,128,128]{2,1,0:T(8,128)(2,1)S(1)} fusion(bf16[64,128,128]{2,1,0:T(8,128)(2,1)S(1)} %broadcast_in_dim.68, s32[32]{0:T(128)S(1)} %get-tuple-element.21, bf16[32,128,128]{2,1,0:T(8,128)(2,1)} %pad_maximum_fusion), kind=kCustom, calls=%fused_computation.5 | custom fusion | bytes 3145856 | tf_op jit(solution)/shard_map/scatter | solution.py:134
  86.0 30.1 %all_to_all.20 = bf16[32,128,128]{2,1,0:T(8,128)(2,1)} all-to-all(bf16[32,128,128]{2,1,0:T(8,128)(2,1)S(1)} %get-tuple-element.6), channel_id=1, replica_groups=mesh['tq'=32,'zh'=2,'tensor'=16] {'tq'}, dimensions={0} | all-to-all | bytes 2097152 | tf_op jit(solution)/shard_map/all_to_all | solution.py:140
  116.1 6.8 %all-to-all-start.2 = ((bf16[32,128,128]{2,1,0:T(8,128)(2,1)}), bf16[32,128,128]{2,1,0:T(8,128)(2,1)}, u32[]{:S(2)}, u32[]{:S(2)}) async-start(bf16[32,128,128]{2,1,0:T(8,128)(2,1)} %get-tuple-element.5), calls=%async_computation.2 | async-start | bytes 2097152 | tf_op jit(solution)/shard_map/all_to_all | solution.py:151
  123.2 2.6 %fusion.10 = f32[2,128,128]{2,0,1:T(2,128)} fusion(bf16[32,128,128]{2,1,0:T(8,128)(2,1)} %all_to_all.20, pred[32,2,2]{0,2,1:T(4,128)(4,1)S(1)} %compare_and_fusion, s32[]{:T(128)S(6)} %select_n.186), kind=kOutput, calls=%fused_computation.32 | convolution fusion | flops 2097152 | bytes 1180164 | tf_op jit(solution)/shard_map/ck,crh->krh/dot_general | solution.py:144
  125.8 23.4 %collective-permute-start.1 = (f32[2,128,128]{2,0,1:T(2,128)}, f32[2,128,128]{2,0,1:T(2,128)}, u32[]{:S(2)}, u32[]{:S(2)}) collective-permute-start(f32[2,128,128]{2,0,1:T(2,128)} %fusion.10), channel_id=1, source_target_pairs={{0,16},{16,0},{1,17},{17,1},{2,18},{18,2},{3,19},{19,3},{4,20},{20... | collective-permute-start | bytes 393224 | tf_op jit(solution)/shard_map/ppermute | solution.py:150
  149.6 2.6 %collective-permute-done.1 = f32[2,128,128]{2,0,1:T(2,128)} collective-permute-done((f32[2,128,128]{2,0,1:T(2,128)}, f32[2,128,128]{2,0,1:T(2,128)}, u32[]{:S(2)}, u32[]{:S(2)}) %collective-permute-start.1) | collective-permute-done | bytes 131104 | tf_op jit(solution)/shard_map/ppermute | solution.py:150
  155.4 5.3 %collective-permute-start.2 = (bf16[64,1536]{1,0:T(8,128)(2,1)S(1)}, bf16[64,1536]{1,0:T(8,128)(2,1)S(1)}, u32[]{:S(2)}, u32[]{:S(2)}) collective-permute-start(bf16[64,1536]{1,0:T(8,128)(2,1)S(1)} %get-tuple-element.7), channel_id=1, source_target_pairs={{0,1},{1,0},{2,3},{3,2},{4,5},{5,4},{6,7},{7,6},{8,9},{9,8},{10,11... | collective-permute-start | bytes 589832 | tf_op jit(solution)/shard_map/ppermute | solution.py:68
  160.7 9.7 %collective-permute-start.4 = (bf16[64,1536]{1,0:T(8,128)(2,1)S(1)}, bf16[64,1536]{1,0:T(8,128)(2,1)S(1)}, u32[]{:S(2)}, u32[]{:S(2)}) collective-permute-start(bf16[64,1536]{1,0:T(8,128)(2,1)S(1)} %get-tuple-element.8), channel_id=1, source_target_pairs={{0,3},{1,2},{2,1},{3,0},{4,7},{5,6},{6,5},{7,4},{8,11},{9,10},{10,... | collective-permute-start | bytes 589832 | tf_op jit(solution)/shard_map/ppermute | solution.py:68
  172.5 3.4 %collective-permute-done.4 = bf16[64,1536]{1,0:T(8,128)(2,1)S(1)} collective-permute-done((bf16[64,1536]{1,0:T(8,128)(2,1)S(1)}, bf16[64,1536]{1,0:T(8,128)(2,1)S(1)}, u32[]{:S(2)}, u32[]{:S(2)}) %collective-permute-start.4) | collective-permute-done | bytes 196640 | tf_op jit(solution)/shard_map/ppermute | solution.py:68
  175.9 4.1 %collective-permute-done.3 = bf16[64,1536]{1,0:T(8,128)(2,1)S(1)} collective-permute-done((bf16[64,1536]{1,0:T(8,128)(2,1)S(1)}, bf16[64,1536]{1,0:T(8,128)(2,1)S(1)}, u32[]{:S(2)}, u32[]{:S(2)}) %collective-permute-start.3) | collective-permute-done | bytes 196640 | tf_op jit(solution)/shard_map/ppermute | solution.py:68
  180.2 3.0 %collective-permute-start.5 = (bf16[16,1536]{1,0:T(8,128)(2,1)S(1)}, bf16[16,1536]{1,0:T(8,128)(2,1)S(1)}, u32[]{:S(2)}, u32[]{:S(2)}) collective-permute-start(bf16[16,1536]{1,0:T(8,128)(2,1)S(1)} %get-tuple-element.10), channel_id=1, source_target_pairs={{0,4},{1,5},{2,6},{3,7},{4,0},{5,1},{6,2},{7,3},{8,12},{9,13},{10,... | collective-permute-start | bytes 147464 | tf_op jit(solution)/shard_map/ppermute | solution.py:68
  183.2 7.8 %collective-permute-start.7 = (bf16[16,1536]{1,0:T(8,128)(2,1)S(1)}, bf16[16,1536]{1,0:T(8,128)(2,1)S(1)}, u32[]{:S(2)}, u32[]{:S(2)}) collective-permute-start(bf16[16,1536]{1,0:T(8,128)(2,1)S(1)} %get-tuple-element.11), channel_id=1, source_target_pairs={{0,12},{1,13},{2,14},{3,15},{4,8},{5,9},{6,10},{7,11},{8,4},{9,5},... | collective-permute-start | bytes 147464 | tf_op jit(solution)/shard_map/ppermute | solution.py:68
  191.0 2.2 collective-permute-start.6
  193.9 9.5 %collective-permute-done.6 = bf16[16,1536]{1,0:T(8,128)(2,1)S(1)} collective-permute-done((bf16[16,1536]{1,0:T(8,128)(2,1)S(1)}, bf16[16,1536]{1,0:T(8,128)(2,1)S(1)}, u32[]{:S(2)}, u32[]{:S(2)}) %collective-permute-start.6) | collective-permute-done | bytes 49184 | tf_op jit(solution)/shard_map/ppermute | solution.py:68
  203.4 3.2 %collective-permute-start.10 = (bf16[16,1536]{1,0:T(8,128)(2,1)S(1)}, bf16[16,1536]{1,0:T(8,128)(2,1)S(1)}, u32[]{:S(2)}, u32[]{:S(2)}) collective-permute-start(bf16[16,1536]{1,0:T(8,128)(2,1)S(1)} %fusion.24), channel_id=1, source_target_pairs={{0,12},{1,13},{2,14},{3,15},{4,8},{5,9},{6,10},{7,11},{8,4},{9,5},... | collective-permute-start | bytes 147464 | tf_op jit(solution)/shard_map/ppermute | solution.py:74
  208.6 8.0 %collective-permute-start.8 = (bf16[16,1536]{1,0:T(8,128)(2,1)S(1)}, bf16[16,1536]{1,0:T(8,128)(2,1)S(1)}, u32[]{:S(2)}, u32[]{:S(2)}) collective-permute-start(bf16[16,1536]{1,0:T(8,128)(2,1)S(1)} %fusion.24), channel_id=1, source_target_pairs={{0,4},{1,5},{2,6},{3,7},{4,0},{5,1},{6,2},{7,3},{8,12},{9,13},{10,... | collective-permute-start | bytes 147464 | tf_op jit(solution)/shard_map/ppermute | solution.py:74
  218.9 2.1 collective-permute-done.8
  223.6 3.7 %collective-permute-start.12 = (bf16[64,1536]{1,0:T(8,128)(2,1)S(1)}, bf16[64,1536]{1,0:T(8,128)(2,1)S(1)}, u32[]{:S(2)}, u32[]{:S(2)}) collective-permute-start(bf16[64,1536]{1,0:T(8,128)(2,1)S(1)} %bitcast_select_fusion.1), channel_id=1, source_target_pairs={{0,2},{1,3},{2,0},{3,1},{4,6},{5,7},{6,4},{7,5},{8,10},{9,11},{10,... | collective-permute-start | bytes 589832 | tf_op jit(solution)/shard_map/ppermute | solution.py:74
  227.4 2.2 collective-permute-start.11
  230.8 4.1 %collective-permute-done.12 = bf16[64,1536]{1,0:T(8,128)(2,1)S(1)} collective-permute-done((bf16[64,1536]{1,0:T(8,128)(2,1)S(1)}, bf16[64,1536]{1,0:T(8,128)(2,1)S(1)}, u32[]{:S(2)}, u32[]{:S(2)}) %collective-permute-start.12) | collective-permute-done | bytes 196640 | tf_op jit(solution)/shard_map/ppermute | solution.py:74
  (95 shorter events, 37.8 us)
Async XLA Ops:
  6.4 33.1 %all-to-all-start = ((bf16[32,128,128]{2,1,0:T(8,128)(2,1)}), bf16[32,128,128]{2,1,0:T(8,128)(2,1)S(1)}, u32[]{:S(2)}, u32[]{:S(2)}) async-start(bf16[32,128,128]{2,1,0:T(8,128)(2,1)} %gather_fusion), calls=%async_computation | async-start | bytes 2097152 | tf_op jit(solution)/shard_map/all_to_all | solution.py:110
  16.9 20.9 %collective-permute-start = (bf16[2,128,128]{2,1,0:T(8,128)(2,1)S(1)}, bf16[2,128,128]{2,1,0:T(8,128)(2,1)S(1)}, u32[]{:S(2)}, u32[]{:S(2)}) collective-permute-start(bf16[2,128,128]{2,1,0:T(8,128)(2,1)S(1)} %bitcast_bitcast_fusion), channel_id=1, source_target_pairs={{0,16},{16,0},{1,17},{17,1},{2,18},{18,2},{3,19},{19,3},{4,20},{20... | collective-permute-start | bytes 196616 | tf_op jit(solution)/shard_map/ppermute | solution.py:101
  36.0 13.0 %copy-start.8 = (bf16[64,1536]{1,0:T(8,128)(2,1)S(1)}, bf16[64,1536]{1,0:T(8,128)(2,1)}, u32[]{:S(2)}) copy-start(bf16[64,1536]{1,0:T(8,128)(2,1)} %param.12) | copy-start | bytes 589828
  39.5 11.0 %copy-start.7 = (bf16[1536,64]{0,1:T(8,128)(2,1)S(1)}, bf16[1536,64]{0,1:T(8,128)(2,1)}, u32[]{:S(2)}) copy-start(bf16[1536,64]{0,1:T(8,128)(2,1)} %param.9) | copy-start | bytes 589828
  39.5 33.4 %all-to-all-start.1 = ((bf16[32,128,128]{2,1,0:T(8,128)(2,1)}), bf16[32,128,128]{2,1,0:T(8,128)(2,1)S(1)}, u32[]{:S(2)}, u32[]{:S(2)}) async-start(bf16[32,128,128]{2,1,0:T(8,128)(2,1)} %gather_fusion.1), calls=%async_computation.1 | async-start | bytes 2097152 | tf_op jit(solution)/shard_map/all_to_all | solution.py:111
  75.1 2.0 copy-start.1
  116.1 33.1 %copy-start.2 = (bf16[32,128,128]{2,1,0:T(8,128)(2,1)S(1)}, bf16[32,128,128]{2,1,0:T(8,128)(2,1)}, u32[]{:S(2)}) copy-start(bf16[32,128,128]{2,1,0:T(8,128)(2,1)} %gather_fusion.2) | copy-start | bytes 3145732
  116.1 33.2 %copy-start.4 = (bf16[2,128,16,128]{1,3,2,0:T(8,128)(2,1)S(1)}, bf16[2,128,16,128]{1,3,2,0:T(8,128)(2,1)}, u32[]{:S(2)}) copy-start(bf16[2,128,16,128]{1,3,2,0:T(8,128)(2,1)} %copy-done.3) | copy-start | bytes 3145732
  116.1 33.5 %all-to-all-start.2 = ((bf16[32,128,128]{2,1,0:T(8,128)(2,1)}), bf16[32,128,128]{2,1,0:T(8,128)(2,1)}, u32[]{:S(2)}, u32[]{:S(2)}) async-start(bf16[32,128,128]{2,1,0:T(8,128)(2,1)} %get-tuple-element.5), calls=%async_computation.2 | async-start | bytes 2097152 | tf_op jit(solution)/shard_map/all_to_all | solution.py:151
  123.2 31.0 %copy-start.5 = (bf16[1536,64]{0,1:T(8,128)(2,1)S(1)}, bf16[1536,64]{0,1:T(8,128)(2,1)}, u32[]{:S(2)}) copy-start(bf16[1536,64]{0,1:T(8,128)(2,1)} %param.10) | copy-start | bytes 589828
  125.8 28.8 %copy-start.6 = (bf16[1536,64]{0,1:T(8,128)(2,1)S(1)}, bf16[1536,64]{0,1:T(8,128)(2,1)}, u32[]{:S(2)}) copy-start(bf16[1536,64]{0,1:T(8,128)(2,1)} %param.11) | copy-start | bytes 589828
  125.8 26.4 %collective-permute-start.1 = (f32[2,128,128]{2,0,1:T(2,128)}, f32[2,128,128]{2,0,1:T(2,128)}, u32[]{:S(2)}, u32[]{:S(2)}) collective-permute-start(f32[2,128,128]{2,0,1:T(2,128)} %fusion.10), channel_id=1, source_target_pairs={{0,16},{16,0},{1,17},{17,1},{2,18},{18,2},{3,19},{19,3},{4,20},{20... | collective-permute-start | bytes 393224 | tf_op jit(solution)/shard_map/ppermute | solution.py:150
  155.4 17.1 %collective-permute-start.2 = (bf16[64,1536]{1,0:T(8,128)(2,1)S(1)}, bf16[64,1536]{1,0:T(8,128)(2,1)S(1)}, u32[]{:S(2)}, u32[]{:S(2)}) collective-permute-start(bf16[64,1536]{1,0:T(8,128)(2,1)S(1)} %get-tuple-element.7), channel_id=1, source_target_pairs={{0,1},{1,0},{2,3},{3,2},{4,5},{5,4},{6,7},{7,6},{8,9},{9,8},{10,11... | collective-permute-start | bytes 589832 | tf_op jit(solution)/shard_map/ppermute | solution.py:68
  160.7 15.2 %collective-permute-start.4 = (bf16[64,1536]{1,0:T(8,128)(2,1)S(1)}, bf16[64,1536]{1,0:T(8,128)(2,1)S(1)}, u32[]{:S(2)}, u32[]{:S(2)}) collective-permute-start(bf16[64,1536]{1,0:T(8,128)(2,1)S(1)} %get-tuple-element.8), channel_id=1, source_target_pairs={{0,3},{1,2},{2,1},{3,0},{4,7},{5,6},{6,5},{7,4},{8,11},{9,10},{10,... | collective-permute-start | bytes 589832 | tf_op jit(solution)/shard_map/ppermute | solution.py:68
  170.5 9.6 %collective-permute-start.3 = (bf16[64,1536]{1,0:T(8,128)(2,1)S(1)}, bf16[64,1536]{1,0:T(8,128)(2,1)S(1)}, u32[]{:S(2)}, u32[]{:S(2)}) collective-permute-start(bf16[64,1536]{1,0:T(8,128)(2,1)S(1)} %get-tuple-element.9), channel_id=1, source_target_pairs={{0,2},{1,3},{2,0},{3,1},{4,6},{5,7},{6,4},{7,5},{8,10},{9,11},{10,... | collective-permute-start | bytes 589832 | tf_op jit(solution)/shard_map/ppermute | solution.py:68
  180.2 13.1 %collective-permute-start.5 = (bf16[16,1536]{1,0:T(8,128)(2,1)S(1)}, bf16[16,1536]{1,0:T(8,128)(2,1)S(1)}, u32[]{:S(2)}, u32[]{:S(2)}) collective-permute-start(bf16[16,1536]{1,0:T(8,128)(2,1)S(1)} %get-tuple-element.10), channel_id=1, source_target_pairs={{0,4},{1,5},{2,6},{3,7},{4,0},{5,1},{6,2},{7,3},{8,12},{9,13},{10,... | collective-permute-start | bytes 147464 | tf_op jit(solution)/shard_map/ppermute | solution.py:68
  183.2 10.7 %collective-permute-start.7 = (bf16[16,1536]{1,0:T(8,128)(2,1)S(1)}, bf16[16,1536]{1,0:T(8,128)(2,1)S(1)}, u32[]{:S(2)}, u32[]{:S(2)}) collective-permute-start(bf16[16,1536]{1,0:T(8,128)(2,1)S(1)} %get-tuple-element.11), channel_id=1, source_target_pairs={{0,12},{1,13},{2,14},{3,15},{4,8},{5,9},{6,10},{7,11},{8,4},{9,5},... | collective-permute-start | bytes 147464 | tf_op jit(solution)/shard_map/ppermute | solution.py:68
  191.0 12.3 %collective-permute-start.6 = (bf16[16,1536]{1,0:T(8,128)(2,1)S(1)}, bf16[16,1536]{1,0:T(8,128)(2,1)S(1)}, u32[]{:S(2)}, u32[]{:S(2)}) collective-permute-start(bf16[16,1536]{1,0:T(8,128)(2,1)S(1)} %get-tuple-element.12), channel_id=1, source_target_pairs={{0,8},{1,9},{2,10},{3,11},{4,12},{5,13},{6,14},{7,15},{8,0},{9,1},... | collective-permute-start | bytes 147464 | tf_op jit(solution)/shard_map/ppermute | solution.py:68
  203.4 13.5 %collective-permute-start.10 = (bf16[16,1536]{1,0:T(8,128)(2,1)S(1)}, bf16[16,1536]{1,0:T(8,128)(2,1)S(1)}, u32[]{:S(2)}, u32[]{:S(2)}) collective-permute-start(bf16[16,1536]{1,0:T(8,128)(2,1)S(1)} %fusion.24), channel_id=1, source_target_pairs={{0,12},{1,13},{2,14},{3,15},{4,8},{5,9},{6,10},{7,11},{8,4},{9,5},... | collective-permute-start | bytes 147464 | tf_op jit(solution)/shard_map/ppermute | solution.py:74
  206.6 12.2 %collective-permute-start.9 = (bf16[16,1536]{1,0:T(8,128)(2,1)S(1)}, bf16[16,1536]{1,0:T(8,128)(2,1)S(1)}, u32[]{:S(2)}, u32[]{:S(2)}) collective-permute-start(bf16[16,1536]{1,0:T(8,128)(2,1)S(1)} %fusion.24), channel_id=1, source_target_pairs={{0,8},{1,9},{2,10},{3,11},{4,12},{5,13},{6,14},{7,15},{8,0},{9,1},... | collective-permute-start | bytes 147464 | tf_op jit(solution)/shard_map/ppermute | solution.py:74
  208.6 12.4 %collective-permute-start.8 = (bf16[16,1536]{1,0:T(8,128)(2,1)S(1)}, bf16[16,1536]{1,0:T(8,128)(2,1)S(1)}, u32[]{:S(2)}, u32[]{:S(2)}) collective-permute-start(bf16[16,1536]{1,0:T(8,128)(2,1)S(1)} %fusion.24), channel_id=1, source_target_pairs={{0,4},{1,5},{2,6},{3,7},{4,0},{5,1},{6,2},{7,3},{8,12},{9,13},{10,... | collective-permute-start | bytes 147464 | tf_op jit(solution)/shard_map/ppermute | solution.py:74
  221.7 9.1 %collective-permute-start.13 = (bf16[64,1536]{1,0:T(8,128)(2,1)S(1)}, bf16[64,1536]{1,0:T(8,128)(2,1)S(1)}, u32[]{:S(2)}, u32[]{:S(2)}) collective-permute-start(bf16[64,1536]{1,0:T(8,128)(2,1)S(1)} %bitcast_select_fusion.1), channel_id=1, source_target_pairs={{0,3},{1,2},{2,1},{3,0},{4,7},{5,6},{6,5},{7,4},{8,11},{9,10},{10,... | collective-permute-start | bytes 589832 | tf_op jit(solution)/shard_map/ppermute | solution.py:74
  223.6 11.3 %collective-permute-start.12 = (bf16[64,1536]{1,0:T(8,128)(2,1)S(1)}, bf16[64,1536]{1,0:T(8,128)(2,1)S(1)}, u32[]{:S(2)}, u32[]{:S(2)}) collective-permute-start(bf16[64,1536]{1,0:T(8,128)(2,1)S(1)} %bitcast_select_fusion.1), channel_id=1, source_target_pairs={{0,2},{1,3},{2,0},{3,1},{4,6},{5,7},{6,4},{7,5},{8,10},{9,11},{10,... | collective-permute-start | bytes 589832 | tf_op jit(solution)/shard_map/ppermute | solution.py:74
  227.4 7.5 %collective-permute-start.11 = (bf16[64,1536]{1,0:T(8,128)(2,1)S(1)}, bf16[64,1536]{1,0:T(8,128)(2,1)S(1)}, u32[]{:S(2)}, u32[]{:S(2)}) collective-permute-start(bf16[64,1536]{1,0:T(8,128)(2,1)S(1)} %bitcast_select_fusion.1), channel_id=1, source_target_pairs={{0,1},{1,0},{2,3},{3,2},{4,5},{5,4},{6,7},{7,6},{8,9},{9,8},{10,11... | collective-permute-start | bytes 589832 | tf_op jit(solution)/shard_map/ppermute | solution.py:74
  (2 other events, 3.4 us)

commit v8 on v5

--- a/solution.py
+++ b/solution.py
@@ -100,12 +100,11 @@
     mirror_slot = lax.dynamic_index_in_dim(slot, 1 - my_side, axis=1, keepdims=False)
     near = lax.all_to_all(paired_spans[own_slot], "tq", split_axis=0, concat_axis=0, tiled=True)
     far = lax.all_to_all(mirror_spans[mirror_slot], "tq", split_axis=0, concat_axis=0, tiled=True)
-    incoming = jnp.where(
-        my_side == 0, jnp.stack([near, far], axis=1), jnp.stack([far, near], axis=1)
-    ).reshape(device_count, 2 * col_count, SPAN)
     own_ids = lax.dynamic_slice_in_dim(key_span, my_index * owned, owned, 0)
     owner_ids = (own_ids // owned).reshape(-1)
-    fetched = incoming[owner_ids]
+    owner_column = owner_ids // side_count
+    from_near = owner_ids % side_count == my_side
+    fetched = jnp.where(from_near[:, None, None], near[owner_column], far[owner_column])
     fetched = fetched.reshape(owned, per_reader, 2, head_count, HD, SPAN)
     query_rows = jnp.transpose(queries_t.reshape(head_count, HD, owned, SPAN), (2, 0, 1, 3))
     dout_rows = jnp.transpose(dout_t.reshape(head_count, HD, owned, SPAN), (2, 0, 1, 3))
@@ -121,15 +120,16 @@
         ],
         axis=1,
     )
-    returned = (
-        jnp.zeros((device_count, 2 * col_count, SPAN), jnp.bfloat16).at[owner_ids].set(pair_grads)
-    )
-    returned = returned.reshape(column_count, side_count, 2 * col_count, SPAN)
+    pair_count = owned * per_reader
+    pair_index = jnp.arange(pair_count, dtype=jnp.int32)
+    unused = jnp.full((column_count,), pair_count, jnp.int32)
+    near_pair = unused.at[jnp.where(from_near, owner_column, column_count)].set(pair_index, mode="drop")
+    far_pair = unused.at[jnp.where(from_near, column_count, owner_column)].set(pair_index, mode="drop")
     picked = (
         exists[:, :, None] & (slot[:, :, None] == jnp.arange(owned, dtype=jnp.int32)[None, None, :])
     ).astype(jnp.bfloat16)
     far_back = lax.all_to_all(
-        lax.dynamic_index_in_dim(returned, 1 - my_side, axis=1, keepdims=False),
+        jnp.take(pair_grads, far_pair, axis=0, mode="fill", fill_value=0),
         "tq", split_axis=0, concat_axis=0, tiled=True,
     )
     other = jnp.einsum(
@@ -140,7 +140,7 @@
     )
     other_back = lax.ppermute(other, "zh", swap)
     near_back = lax.all_to_all(
-        lax.dynamic_index_in_dim(returned, my_side, axis=1, keepdims=False),
+        jnp.take(pair_grads, near_pair, axis=0, mode="fill", fill_value=0),
         "tq", split_axis=0, concat_axis=0, tiled=True,
     )
     mine = jnp.einsum(

time: 229 us -> 228 us (level)
  blocking collectives: 30 us -> 0 us
  waiting for transfers between devices: 48.5 us -> 64.9 us
  starting transfers between devices: 118 us -> 124 us
  other arithmetic: 4.82 us -> 9.17 us
  local copies, waits for them, and re-layouts: 11.7 us -> 14 us
    all_to_all x1 -> x0, blocking collectives: 30 us -> none  [local(): lax.all_to_all(lax.dynamic_index_in_dim(returned, 1 - my_side, axis=1, ke...]
    all_to_all x1 -> x2, waiting for transfers between devices: 0.01 us -> 18.8 us  [the longest x1 18.8 us: local(): lax.all_to_all(jnp.take(pair_grads, far_pair, axis=0, mode='fill', fill_v...]
    all_to_all x1 -> x2, starting transfers between devices: 6.81 us -> 13.4 us  [the longest x1 6.71 us: local(): lax.all_to_all(jnp.take(pair_grads, far_pair, axis=0, mode='fill', fill_v...]
    select_n x2 -> x6, other arithmetic: 1.12 us -> 6.43 us  [the longest x2 2.37 us: local(): jnp.take(pair_grads, near_pair, axis=0, mode='fill', fill_value=0)]
    gather x1 -> x4, local copies, waits for them, and re-layouts: 1.66 us -> 6.63 us  [the longest x1 1.68 us: local(): jnp.take(pair_grads, near_pair, axis=0, mode='fill', fill_value=0)]
    all_to_all x1, waiting for transfers between devices: 21.9 us -> 19.5 us  [local(): lax.all_to_all(mirror_spans[mirror_slot], 'tq', split_axis=0, concat_axis...]
  transfers between devices with their start and end apart: 13 -> 14, of which waited for: 11 -> 12; matrix products, arithmetic and copies ran while one was open for 3% -> 6% of each run, Pallas kernels for 0% -> 0%
where the time goes in v8:
time: 228 us; the launch traced here: 227 us
  starting transfers between devices  124 us (54%)
  waiting for transfers between devices  64.9 us (28%)
  local copies, waits for them, and re-layouts  14 us (6%)
  matrix products  13.4 us (6%)
  other arithmetic  9.17 us (4%)
    ppermute x4, starting transfers between devices, head_sum(): lax.ppermute(send.astype(jnp.bfloat16), 'tensor', [(i, i ^ step) for i in...  25.2 us
    ppermute x4, starting transfers between devices, head_sum(): got = lax.ppermute(cur, 'tensor', [(i, i ^ step) for i in range(count)])  23.4 us
    ppermute x1, starting transfers between devices, local(): other_back = lax.ppermute(other, 'zh', swap)  23.4 us
    all_to_all x1, waiting for transfers between devices, local(): lax.all_to_all(mirror_spans[mirror_slot], 'tq', split_axis=0, concat_axis...  19.5 us
    ppermute x1, starting transfers between devices, local(): mirror_spans = lax.ppermute(paired_spans, 'zh', swap)  19.1 us
    all_to_all x1, waiting for transfers between devices, local(): lax.all_to_all(jnp.take(pair_grads, far_pair, axis=0, mode='fill', fill_v...  18.8 us
    ppermute x4, waiting for transfers between devices, head_sum(): lax.ppermute(send.astype(jnp.bfloat16), 'tensor', [(i, i ^ step) for i in...  12.5 us
    all_to_all x1, starting transfers between devices, local(): lax.all_to_all(paired_spans[own_slot], 'tq', split_axis=0, concat_axis=0,...  10.5 us
  transfers between devices with their start and end apart: 14, of which 12 were waited for; matrix products, arithmetic and copies ran while one was open for 6% of the time, Pallas kernels for 0%

profile of v8, /device:TPU:1, one launch (start us, length us, event | category | flops | bytes accessed | tf_op | source)
XLA Modules:
  0.0 226.5 jit_solution(16184616282719231161)
XLA Ops:
  6.7 10.5 %all-to-all-start = ((bf16[32,128,128]{2,1,0:T(8,128)(2,1)}), bf16[32,128,128]{2,1,0:T(8,128)(2,1)S(1)}, u32[]{:S(2)}, u32[]{:S(2)}) async-start(bf16[32,128,128]{2,1,0:T(8,128)(2,1)} %gather_fusion), calls=%async_computation | async-start | bytes 2097152 | tf_op jit(solution)/shard_map/all_to_all | solution.py:101
  17.2 19.1 %collective-permute-start = (bf16[2,128,128]{2,1,0:T(8,128)(2,1)S(1)}, bf16[2,128,128]{2,1,0:T(8,128)(2,1)S(1)}, u32[]{:S(2)}, u32[]{:S(2)}) collective-permute-start(bf16[2,128,128]{2,1,0:T(8,128)(2,1)S(1)} %bitcast_bitcast_fusion), channel_id=1, source_target_pairs={{0,16},{16,0},{1,17},{17,1},{2,18},{18,2},{3,19},{19,3},{4,20},{20... | collective-permute-start | bytes 196616 | tf_op jit(solution)/shard_map/ppermute | solution.py:92
  39.7 9.5 %all-to-all-start.1 = ((bf16[32,128,128]{2,1,0:T(8,128)(2,1)}), bf16[32,128,128]{2,1,0:T(8,128)(2,1)S(1)}, u32[]{:S(2)}, u32[]{:S(2)}) async-start(bf16[32,128,128]{2,1,0:T(8,128)(2,1)} %gather_fusion.2), calls=%async_computation.1 | async-start | bytes 2097152 | tf_op jit(solution)/shard_map/all_to_all | solution.py:102
  53.5 19.5 %all-to-all-done.1 = bf16[32,128,128]{2,1,0:T(8,128)(2,1)S(1)} async-done(((bf16[32,128,128]{2,1,0:T(8,128)(2,1)}), bf16[32,128,128]{2,1,0:T(8,128)(2,1)S(1)}, u32[]{:S(2)}, u32[]{:S(2)}) %all-to-all-start.1) | async-done | bytes 1048608 | tf_op jit(solution)/shard_map/all_to_all | solution.py:102
  82.1 2.3 %broadcast_select_fusion = bf16[32,128,128]{2,1,0:T(8,128)(2,1)} fusion(bf16[32,128,128]{2,1,0:T(8,128)(2,1)} %gather_fusion.5, pred[32]{0:T(512)(128)(4,1)S(1)} %compare_and_fusion.1), kind=kLoop, calls=%fused_computation.37 | loop fusion | flops 524288 | bytes 2097184 | tf_op jit(solution)/shard_map/jit(_take)/select_n | solution.py:132
  84.5 6.7 %all-to-all-start.3 = ((bf16[32,128,128]{2,1,0:T(8,128)(2,1)}), bf16[32,128,128]{2,1,0:T(8,128)(2,1)}, u32[]{:S(2)}, u32[]{:S(2)}) async-start(bf16[32,128,128]{2,1,0:T(8,128)(2,1)} %broadcast_select_fusion), calls=%async_computation.3 | async-start | bytes 2097152 | tf_op jit(solution)/shard_map/all_to_all | solution.py:131
  93.6 2.4 %broadcast_select_fusion.1 = bf16[32,128,128]{2,1,0:T(8,128)(2,1)} fusion(bf16[32,128,128]{2,1,0:T(8,128)(2,1)} %gather_fusion.4, pred[32]{0:T(512)(128)(4,1)S(1)} %compare_and_fusion.2), kind=kLoop, calls=%fused_computation.38 | loop fusion | flops 524288 | bytes 2097184 | tf_op jit(solution)/shard_map/jit(_take)/select_n | solution.py:143
  96.0 18.8 %all-to-all-done.3 = bf16[32,128,128]{2,1,0:T(8,128)(2,1)} async-done(((bf16[32,128,128]{2,1,0:T(8,128)(2,1)}), bf16[32,128,128]{2,1,0:T(8,128)(2,1)}, u32[]{:S(2)}, u32[]{:S(2)}) %all-to-all-start.3) | async-done | bytes 1048608 | tf_op jit(solution)/shard_map/all_to_all | solution.py:131
  114.8 6.6 %all-to-all-start.2 = ((bf16[32,128,128]{2,1,0:T(8,128)(2,1)}), bf16[32,128,128]{2,1,0:T(8,128)(2,1)}, u32[]{:S(2)}, u32[]{:S(2)}) async-start(bf16[32,128,128]{2,1,0:T(8,128)(2,1)} %broadcast_select_fusion.1), calls=%async_computation.2 | async-start | bytes 2097152 | tf_op jit(solution)/shard_map/all_to_all | solution.py:142
  121.6 2.6 %fusion.10 = f32[2,128,128]{2,0,1:T(2,128)} fusion(bf16[32,128,128]{2,1,0:T(8,128)(2,1)} %all-to-all-done.3, pred[32,2,2]{0,2,1:T(4,128)(4,1)S(1)} %compare_and_fusion, s32[]{:T(128)S(6)} %select_n.263), kind=kOutput, calls=%fused_computation.33 | convolution fusion | flops 2097152 | bytes 1180164 | tf_op jit(solution)/shard_map/ck,crh->krh/dot_general | solution.py:135
  124.2 23.4 %collective-permute-start.1 = (f32[2,128,128]{2,0,1:T(2,128)}, f32[2,128,128]{2,0,1:T(2,128)}, u32[]{:S(2)}, u32[]{:S(2)}) collective-permute-start(f32[2,128,128]{2,0,1:T(2,128)} %fusion.10), channel_id=1, source_target_pairs={{0,16},{16,0},{1,17},{17,1},{2,18},{18,2},{3,19},{19,3},{4,20},{20... | collective-permute-start | bytes 393224 | tf_op jit(solution)/shard_map/ppermute | solution.py:141
  148.1 2.6 %collective-permute-done.1 = f32[2,128,128]{2,0,1:T(2,128)} collective-permute-done((f32[2,128,128]{2,0,1:T(2,128)}, f32[2,128,128]{2,0,1:T(2,128)}, u32[]{:S(2)}, u32[]{:S(2)}) %collective-permute-start.1) | collective-permute-done | bytes 131104 | tf_op jit(solution)/shard_map/ppermute | solution.py:141
  153.8 5.3 %collective-permute-start.2 = (bf16[128,1536]{1,0:T(8,128)(2,1)S(1)}, bf16[128,1536]{1,0:T(8,128)(2,1)S(1)}, u32[]{:S(2)}, u32[]{:S(2)}) collective-permute-start(bf16[128,1536]{1,0:T(8,128)(2,1)S(1)} %select_convert_fusion), channel_id=1, source_target_pairs={{0,1},{1,0},{2,3},{3,2},{4,5},{5,4},{6,7},{7,6},{8,9},{9,8},{10,11... | collective-permute-start | bytes 1179656 | tf_op jit(solution)/shard_map/ppermute | solution.py:59
  160.7 9.8 %collective-permute-start.3 = (bf16[64,1536]{1,0:T(8,128)(2,1)S(1)}, bf16[64,1536]{1,0:T(8,128)(2,1)S(1)}, u32[]{:S(2)}, u32[]{:S(2)}) collective-permute-start(bf16[64,1536]{1,0:T(8,128)(2,1)S(1)} %select_convert_fusion.1), channel_id=1, source_target_pairs={{0,2},{1,3},{2,0},{3,1},{4,6},{5,7},{6,4},{7,5},{8,10},{9,11},{10,... | collective-permute-start | bytes 589832 | tf_op jit(solution)/shard_map/ppermute | solution.py:59
  170.4 4.9 %collective-permute-done.3 = bf16[64,1536]{1,0:T(8,128)(2,1)S(1)} collective-permute-done((bf16[64,1536]{1,0:T(8,128)(2,1)S(1)}, bf16[64,1536]{1,0:T(8,128)(2,1)S(1)}, u32[]{:S(2)}, u32[]{:S(2)}) %collective-permute-start.3) | collective-permute-done | bytes 196640 | tf_op jit(solution)/shard_map/ppermute | solution.py:59
  175.4 3.2 %collective-permute-start.4 = (bf16[32,1536]{1,0:T(8,128)(2,1)S(1)}, bf16[32,1536]{1,0:T(8,128)(2,1)S(1)}, u32[]{:S(2)}, u32[]{:S(2)}) collective-permute-start(bf16[32,1536]{1,0:T(8,128)(2,1)S(1)} %select_convert_fusion.2), channel_id=1, source_target_pairs={{0,4},{1,5},{2,6},{3,7},{4,0},{5,1},{6,2},{7,3},{8,12},{9,13},{10,... | collective-permute-start | bytes 294920 | tf_op jit(solution)/shard_map/ppermute | solution.py:59
  178.6 4.5 %collective-permute-done.4 = bf16[32,1536]{1,0:T(8,128)(2,1)S(1)} collective-permute-done((bf16[32,1536]{1,0:T(8,128)(2,1)S(1)}, bf16[32,1536]{1,0:T(8,128)(2,1)S(1)}, u32[]{:S(2)}, u32[]{:S(2)}) %collective-permute-start.4) | collective-permute-done | bytes 98336 | tf_op jit(solution)/shard_map/ppermute | solution.py:59
  183.1 7.0 %collective-permute-start.5 = (bf16[16,1536]{1,0:T(8,128)(2,1)S(1)}, bf16[16,1536]{1,0:T(8,128)(2,1)S(1)}, u32[]{:S(2)}, u32[]{:S(2)}) collective-permute-start(bf16[16,1536]{1,0:T(8,128)(2,1)S(1)} %select_convert_fusion.3), channel_id=1, source_target_pairs={{0,8},{1,9},{2,10},{3,11},{4,12},{5,13},{6,14},{7,15},{8,0},{9,1},... | collective-permute-start | bytes 147464 | tf_op jit(solution)/shard_map/ppermute | solution.py:59
  191.9 7.0 %collective-permute-start.6 = (bf16[16,1536]{1,0:T(8,128)(2,1)S(1)}, bf16[16,1536]{1,0:T(8,128)(2,1)S(1)}, u32[]{:S(2)}, u32[]{:S(2)}) collective-permute-start(bf16[16,1536]{1,0:T(8,128)(2,1)S(1)} %add_convert_fusion), channel_id=1, source_target_pairs={{0,8},{1,9},{2,10},{3,11},{4,12},{5,13},{6,14},{7,15},{8,0},{9,1},... | collective-permute-start | bytes 147464 | tf_op jit(solution)/shard_map/ppermute | solution.py:66
  200.7 2.7 %collective-permute-start.7 = (bf16[32,1536]{1,0:T(8,128)(2,1)S(1)}, bf16[32,1536]{1,0:T(8,128)(2,1)S(1)}, u32[]{:S(2)}, u32[]{:S(2)}) collective-permute-start(bf16[32,1536]{1,0:T(8,128)(2,1)S(1)} %maximum_select_fusion.3), channel_id=1, source_target_pairs={{0,4},{1,5},{2,6},{3,7},{4,0},{5,1},{6,2},{7,3},{8,12},{9,13},{10,... | collective-permute-start | bytes 294920 | tf_op jit(solution)/shard_map/ppermute | solution.py:66
  203.4 3.5 %collective-permute-done.7 = bf16[32,1536]{1,0:T(8,128)(2,1)S(1)} collective-permute-done((bf16[32,1536]{1,0:T(8,128)(2,1)S(1)}, bf16[32,1536]{1,0:T(8,128)(2,1)S(1)}, u32[]{:S(2)}, u32[]{:S(2)}) %collective-permute-start.7) | collective-permute-done | bytes 98336 | tf_op jit(solution)/shard_map/ppermute | solution.py:66
  207.0 7.4 %collective-permute-start.8 = (bf16[64,1536]{1,0:T(8,128)(2,1)S(1)}, bf16[64,1536]{1,0:T(8,128)(2,1)S(1)}, u32[]{:S(2)}, u32[]{:S(2)}) collective-permute-start(bf16[64,1536]{1,0:T(8,128)(2,1)S(1)} %maximum_select_fusion.2), channel_id=1, source_target_pairs={{0,2},{1,3},{2,0},{3,1},{4,6},{5,7},{6,4},{7,5},{8,10},{9,11},{10,... | collective-permute-start | bytes 589832 | tf_op jit(solution)/shard_map/ppermute | solution.py:66
  214.4 3.0 %collective-permute-done.8 = bf16[64,1536]{1,0:T(8,128)(2,1)S(1)} collective-permute-done((bf16[64,1536]{1,0:T(8,128)(2,1)S(1)}, bf16[64,1536]{1,0:T(8,128)(2,1)S(1)}, u32[]{:S(2)}, u32[]{:S(2)}) %collective-permute-start.8) | collective-permute-done | bytes 196640 | tf_op jit(solution)/shard_map/ppermute | solution.py:66
  217.5 6.3 %collective-permute-start.9 = (bf16[128,1536]{1,0:T(8,128)(2,1)S(1)}, bf16[128,1536]{1,0:T(8,128)(2,1)S(1)}, u32[]{:S(2)}, u32[]{:S(2)}) collective-permute-start(bf16[128,1536]{1,0:T(8,128)(2,1)S(1)} %maximum_select_fusion.1), channel_id=1, source_target_pairs={{0,1},{1,0},{2,3},{3,2},{4,5},{5,4},{6,7},{7,6},{8,9},{9,8},{10,11... | collective-permute-start | bytes 1179656 | tf_op jit(solution)/shard_map/ppermute | solution.py:66
  (86 shorter events, 37.4 us)
Async XLA Ops:
  0.0 1.1 copy-start
  6.7 33.1 %all-to-all-start = ((bf16[32,128,128]{2,1,0:T(8,128)(2,1)}), bf16[32,128,128]{2,1,0:T(8,128)(2,1)S(1)}, u32[]{:S(2)}, u32[]{:S(2)}) async-start(bf16[32,128,128]{2,1,0:T(8,128)(2,1)} %gather_fusion), calls=%async_computation | async-start | bytes 2097152 | tf_op jit(solution)/shard_map/all_to_all | solution.py:101
  17.2 20.9 %collective-permute-start = (bf16[2,128,128]{2,1,0:T(8,128)(2,1)S(1)}, bf16[2,128,128]{2,1,0:T(8,128)(2,1)S(1)}, u32[]{:S(2)}, u32[]{:S(2)}) collective-permute-start(bf16[2,128,128]{2,1,0:T(8,128)(2,1)S(1)} %bitcast_bitcast_fusion), channel_id=1, source_target_pairs={{0,16},{16,0},{1,17},{17,1},{2,18},{18,2},{3,19},{19,3},{4,20},{20... | collective-permute-start | bytes 196616 | tf_op jit(solution)/shard_map/ppermute | solution.py:92
  36.3 13.0 %copy-start.6 = (bf16[64,1536]{1,0:T(8,128)(2,1)S(1)}, bf16[64,1536]{1,0:T(8,128)(2,1)}, u32[]{:S(2)}) copy-start(bf16[64,1536]{1,0:T(8,128)(2,1)} %param.14) | copy-start | bytes 589828
  39.7 11.0 %copy-start.5 = (bf16[1536,64]{0,1:T(8,128)(2,1)S(1)}, bf16[1536,64]{0,1:T(8,128)(2,1)}, u32[]{:S(2)}) copy-start(bf16[1536,64]{0,1:T(8,128)(2,1)} %param.11) | copy-start | bytes 589828
  39.7 33.4 %all-to-all-start.1 = ((bf16[32,128,128]{2,1,0:T(8,128)(2,1)}), bf16[32,128,128]{2,1,0:T(8,128)(2,1)S(1)}, u32[]{:S(2)}, u32[]{:S(2)}) async-start(bf16[32,128,128]{2,1,0:T(8,128)(2,1)} %gather_fusion.2), calls=%async_computation.1 | async-start | bytes 2097152 | tf_op jit(solution)/shard_map/all_to_all | solution.py:102
  79.4 1.0 copy-start.1
  84.5 30.3 %all-to-all-start.3 = ((bf16[32,128,128]{2,1,0:T(8,128)(2,1)}), bf16[32,128,128]{2,1,0:T(8,128)(2,1)}, u32[]{:S(2)}, u32[]{:S(2)}) async-start(bf16[32,128,128]{2,1,0:T(8,128)(2,1)} %broadcast_select_fusion), calls=%async_computation.3 | async-start | bytes 2097152 | tf_op jit(solution)/shard_map/all_to_all | solution.py:131
  96.0 51.7 %copy-start.2 = (bf16[2,128,16,128]{1,3,2,0:T(8,128)(2,1)S(1)}, bf16[2,128,16,128]{1,3,2,0:T(8,128)(2,1)}, u32[]{:S(2)}) copy-start(bf16[2,128,16,128]{1,3,2,0:T(8,128)(2,1)} %copy-done.1) | copy-start | bytes 3145732
  114.8 33.3 %all-to-all-start.2 = ((bf16[32,128,128]{2,1,0:T(8,128)(2,1)}), bf16[32,128,128]{2,1,0:T(8,128)(2,1)}, u32[]{:S(2)}, u32[]{:S(2)}) async-start(bf16[32,128,128]{2,1,0:T(8,128)(2,1)} %broadcast_select_fusion.1), calls=%async_computation.2 | async-start | bytes 2097152 | tf_op jit(solution)/shard_map/all_to_all | solution.py:142
  121.6 30.9 %copy-start.3 = (bf16[1536,64]{0,1:T(8,128)(2,1)S(1)}, bf16[1536,64]{0,1:T(8,128)(2,1)}, u32[]{:S(2)}) copy-start(bf16[1536,64]{0,1:T(8,128)(2,1)} %param.12) | copy-start | bytes 589828
  124.2 28.7 %copy-start.4 = (bf16[1536,64]{0,1:T(8,128)(2,1)S(1)}, bf16[1536,64]{0,1:T(8,128)(2,1)}, u32[]{:S(2)}) copy-start(bf16[1536,64]{0,1:T(8,128)(2,1)} %param.13) | copy-start | bytes 589828
  124.2 26.4 %collective-permute-start.1 = (f32[2,128,128]{2,0,1:T(2,128)}, f32[2,128,128]{2,0,1:T(2,128)}, u32[]{:S(2)}, u32[]{:S(2)}) collective-permute-start(f32[2,128,128]{2,0,1:T(2,128)} %fusion.10), channel_id=1, source_target_pairs={{0,16},{16,0},{1,17},{17,1},{2,18},{18,2},{3,19},{19,3},{4,20},{20... | collective-permute-start | bytes 393224 | tf_op jit(solution)/shard_map/ppermute | solution.py:141
  153.8 6.7 %collective-permute-start.2 = (bf16[128,1536]{1,0:T(8,128)(2,1)S(1)}, bf16[128,1536]{1,0:T(8,128)(2,1)S(1)}, u32[]{:S(2)}, u32[]{:S(2)}) collective-permute-start(bf16[128,1536]{1,0:T(8,128)(2,1)S(1)} %select_convert_fusion), channel_id=1, source_target_pairs={{0,1},{1,0},{2,3},{3,2},{4,5},{5,4},{6,7},{7,6},{8,9},{9,8},{10,11... | collective-permute-start | bytes 1179656 | tf_op jit(solution)/shard_map/ppermute | solution.py:59
  160.7 14.7 %collective-permute-start.3 = (bf16[64,1536]{1,0:T(8,128)(2,1)S(1)}, bf16[64,1536]{1,0:T(8,128)(2,1)S(1)}, u32[]{:S(2)}, u32[]{:S(2)}) collective-permute-start(bf16[64,1536]{1,0:T(8,128)(2,1)S(1)} %select_convert_fusion.1), channel_id=1, source_target_pairs={{0,2},{1,3},{2,0},{3,1},{4,6},{5,7},{6,4},{7,5},{8,10},{9,11},{10,... | collective-permute-start | bytes 589832 | tf_op jit(solution)/shard_map/ppermute | solution.py:59
  175.4 7.7 %collective-permute-start.4 = (bf16[32,1536]{1,0:T(8,128)(2,1)S(1)}, bf16[32,1536]{1,0:T(8,128)(2,1)S(1)}, u32[]{:S(2)}, u32[]{:S(2)}) collective-permute-start(bf16[32,1536]{1,0:T(8,128)(2,1)S(1)} %select_convert_fusion.2), channel_id=1, source_target_pairs={{0,4},{1,5},{2,6},{3,7},{4,0},{5,1},{6,2},{7,3},{8,12},{9,13},{10,... | collective-permute-start | bytes 294920 | tf_op jit(solution)/shard_map/ppermute | solution.py:59
  183.1 8.8 %collective-permute-start.5 = (bf16[16,1536]{1,0:T(8,128)(2,1)S(1)}, bf16[16,1536]{1,0:T(8,128)(2,1)S(1)}, u32[]{:S(2)}, u32[]{:S(2)}) collective-permute-start(bf16[16,1536]{1,0:T(8,128)(2,1)S(1)} %select_convert_fusion.3), channel_id=1, source_target_pairs={{0,8},{1,9},{2,10},{3,11},{4,12},{5,13},{6,14},{7,15},{8,0},{9,1},... | collective-permute-start | bytes 147464 | tf_op jit(solution)/shard_map/ppermute | solution.py:59
  191.9 8.8 %collective-permute-start.6 = (bf16[16,1536]{1,0:T(8,128)(2,1)S(1)}, bf16[16,1536]{1,0:T(8,128)(2,1)S(1)}, u32[]{:S(2)}, u32[]{:S(2)}) collective-permute-start(bf16[16,1536]{1,0:T(8,128)(2,1)S(1)} %add_convert_fusion), channel_id=1, source_target_pairs={{0,8},{1,9},{2,10},{3,11},{4,12},{5,13},{6,14},{7,15},{8,0},{9,1},... | collective-permute-start | bytes 147464 | tf_op jit(solution)/shard_map/ppermute | solution.py:66
  200.7 6.3 %collective-permute-start.7 = (bf16[32,1536]{1,0:T(8,128)(2,1)S(1)}, bf16[32,1536]{1,0:T(8,128)(2,1)S(1)}, u32[]{:S(2)}, u32[]{:S(2)}) collective-permute-start(bf16[32,1536]{1,0:T(8,128)(2,1)S(1)} %maximum_select_fusion.3), channel_id=1, source_target_pairs={{0,4},{1,5},{2,6},{3,7},{4,0},{5,1},{6,2},{7,3},{8,12},{9,13},{10,... | collective-permute-start | bytes 294920 | tf_op jit(solution)/shard_map/ppermute | solution.py:66
  207.0 10.5 %collective-permute-start.8 = (bf16[64,1536]{1,0:T(8,128)(2,1)S(1)}, bf16[64,1536]{1,0:T(8,128)(2,1)S(1)}, u32[]{:S(2)}, u32[]{:S(2)}) collective-permute-start(bf16[64,1536]{1,0:T(8,128)(2,1)S(1)} %maximum_select_fusion.2), channel_id=1, source_target_pairs={{0,2},{1,3},{2,0},{3,1},{4,6},{5,7},{6,4},{7,5},{8,10},{9,11},{10,... | collective-permute-start | bytes 589832 | tf_op jit(solution)/shard_map/ppermute | solution.py:66
  217.5 7.7 %collective-permute-start.9 = (bf16[128,1536]{1,0:T(8,128)(2,1)S(1)}, bf16[128,1536]{1,0:T(8,128)(2,1)S(1)}, u32[]{:S(2)}, u32[]{:S(2)}) collective-permute-start(bf16[128,1536]{1,0:T(8,128)(2,1)S(1)} %maximum_select_fusion.1), channel_id=1, source_target_pairs={{0,1},{1,0},{2,3},{3,2},{4,5},{5,4},{6,7},{7,6},{8,9},{9,8},{10,11... | collective-permute-start | bytes 1179656 | tf_op jit(solution)/shard_map/ppermute | solution.py:66

commit v9 on v8

--- a/solution.py
+++ b/solution.py
@@ -66,6 +66,28 @@
         got = lax.ppermute(cur, "tensor", [(i, i ^ step) for i in range(count)])
         cur = jnp.where(upper, jnp.concatenate([got, cur]), jnp.concatenate([cur, got]))
     return cur.astype(jnp.float32)
+
+
+def relay_pairs(side_count, tensor_count, hop):
+    line = tensor_count // 2
+    ring = side_count * line
+    pairs = []
+    for side in range(side_count):
+        for t in range(tensor_count):
+            z = (side * line + t // 2 + hop) % ring
+            pairs.append((side * tensor_count + t, (z // line) * tensor_count + (z % line) * 2 + t % 2))
+    return pairs
+
+
+def mirror_swap(payload):
+    side_count = lax.axis_size("zh")
+    tensor_count = lax.axis_size("tensor")
+    quarter = tensor_count // 2 * side_count // 4
+    ahead, behind = jnp.split(payload, 2, axis=0)
+    for _ in range(2):
+        ahead = lax.ppermute(ahead, ("zh", "tensor"), relay_pairs(side_count, tensor_count, quarter))
+        behind = lax.ppermute(behind, ("zh", "tensor"), relay_pairs(side_count, tensor_count, -quarter))
+    return jnp.concatenate([ahead, behind], axis=0)
 
 
 def local(normed, grad_out, w_query, w_key, w_value, w_out, key_span):
@@ -138,7 +160,7 @@
         far_back,
         preferred_element_type=jnp.float32,
     )
-    other_back = lax.ppermute(other, "zh", swap)
+    other_back = mirror_swap(other)
     near_back = lax.all_to_all(
         jnp.take(pair_grads, near_pair, axis=0, mode="fill", fill_value=0),
         "tq", split_axis=0, concat_axis=0, tiled=True,

time: 228 us -> 235 us (1.031)
  waiting for transfers between devices: 64.9 us -> 80 us
  starting transfers between devices: 124 us -> 117 us
    ppermute x1 -> x4, starting transfers between devices: 23.4 us -> 33.3 us  [the longest x2 19.9 us: mirror_swap(): lax.ppermute(ahead, ('zh', 'tensor'), relay_pairs(side_count, tensor_coun...]
    ppermute x4, starting transfers between devices: 23.4 us -> 14.3 us  [head_sum(): got = lax.ppermute(cur, 'tensor', [(i, i ^ step) for i in range(count)])]
    ppermute x4, starting transfers between devices: 25.2 us -> 17 us  [head_sum(): lax.ppermute(send.astype(jnp.bfloat16), 'tensor', [(i, i ^ step) for i in...]
    ppermute x4, waiting for transfers between devices: 12.5 us -> 18.5 us  [head_sum(): lax.ppermute(send.astype(jnp.bfloat16), 'tensor', [(i, i ^ step) for i in...]
    ppermute x4, waiting for transfers between devices: 9.71 us -> 15.5 us  [head_sum(): got = lax.ppermute(cur, 'tensor', [(i, i ^ step) for i in range(count)])]
    ppermute x1 -> x4, waiting for transfers between devices: 2.56 us -> 5.92 us  [the longest x2 4.9 us: mirror_swap(): lax.ppermute(behind, ('zh', 'tensor'), relay_pairs(side_count, tensor_cou...]
  transfers between devices with their start and end apart: 14 -> 17, of which waited for: 12 -> 13; matrix products, arithmetic and copies ran while one was open for 6% -> 6% of each run, Pallas kernels for 0% -> 0%
where the time goes in v9:
time: 235 us; the launch traced here: 234 us
  starting transfers between devices  117 us (50%)
  waiting for transfers between devices  80 us (34%)
  local copies, waits for them, and re-layouts  14.1 us (6%)
  matrix products  12.8 us (5%)
  other arithmetic  9.19 us (4%)
    ppermute x2, starting transfers between devices, mirror_swap(): lax.ppermute(ahead, ('zh', 'tensor'), relay_pairs(side_count, tensor_coun...  19.9 us
    all_to_all x1, waiting for transfers between devices, local(): lax.all_to_all(mirror_spans[mirror_slot], 'tq', split_axis=0, concat_axis...  19.5 us
    ppermute x1, starting transfers between devices, local(): mirror_spans = lax.ppermute(paired_spans, 'zh', swap)  19.1 us
    all_to_all x1, waiting for transfers between devices, local(): lax.all_to_all(jnp.take(pair_grads, far_pair, axis=0, mode='fill', fill_v...  18.8 us
    ppermute x4, waiting for transfers between devices, head_sum(): lax.ppermute(send.astype(jnp.bfloat16), 'tensor', [(i, i ^ step) for i in...  18.5 us
    ppermute x4, starting transfers between devices, head_sum(): lax.ppermute(send.astype(jnp.bfloat16), 'tensor', [(i, i ^ step) for i in...  17 us
    ppermute x4, waiting for transfers between devices, head_sum(): got = lax.ppermute(cur, 'tensor', [(i, i ^ step) for i in range(count)])  15.5 us
    ppermute x4, starting transfers between devices, head_sum(): got = lax.ppermute(cur, 'tensor', [(i, i ^ step) for i in range(count)])  14.3 us
  transfers between devices with their start and end apart: 17, of which 13 were waited for; matrix products, arithmetic and copies ran while one was open for 6% of the time, Pallas kernels for 0%

profile of v9, /device:TPU:1, one launch (start us, length us, event | category | flops | bytes accessed | tf_op | source)
XLA Modules:
  0.0 233.6 jit_solution(5116103695347151260)
XLA Ops:
  6.7 10.5 %all-to-all-start = ((bf16[32,128,128]{2,1,0:T(8,128)(2,1)}), bf16[32,128,128]{2,1,0:T(8,128)(2,1)S(1)}, u32[]{:S(2)}, u32[]{:S(2)}) async-start(bf16[32,128,128]{2,1,0:T(8,128)(2,1)} %gather_fusion), calls=%async_computation | async-start | bytes 2097152 | tf_op jit(solution)/shard_map/all_to_all | solution.py:123
  17.2 19.1 %collective-permute-start = (bf16[2,128,128]{2,1,0:T(8,128)(2,1)S(1)}, bf16[2,128,128]{2,1,0:T(8,128)(2,1)S(1)}, u32[]{:S(2)}, u32[]{:S(2)}) collective-permute-start(bf16[2,128,128]{2,1,0:T(8,128)(2,1)S(1)} %bitcast_bitcast_fusion), channel_id=1, source_target_pairs={{0,16},{16,0},{1,17},{17,1},{2,18},{18,2},{3,19},{19,3},{4,20},{20... | collective-permute-start | bytes 196616 | tf_op jit(solution)/shard_map/ppermute | solution.py:114
  39.7 9.5 %all-to-all-start.1 = ((bf16[32,128,128]{2,1,0:T(8,128)(2,1)}), bf16[32,128,128]{2,1,0:T(8,128)(2,1)S(1)}, u32[]{:S(2)}, u32[]{:S(2)}) async-start(bf16[32,128,128]{2,1,0:T(8,128)(2,1)} %gather_fusion.2), calls=%async_computation.1 | async-start | bytes 2097152 | tf_op jit(solution)/shard_map/all_to_all | solution.py:124
  53.5 19.5 %all-to-all-done.1 = bf16[32,128,128]{2,1,0:T(8,128)(2,1)S(1)} async-done(((bf16[32,128,128]{2,1,0:T(8,128)(2,1)}), bf16[32,128,128]{2,1,0:T(8,128)(2,1)S(1)}, u32[]{:S(2)}, u32[]{:S(2)}) %all-to-all-start.1) | async-done | bytes 1048608 | tf_op jit(solution)/shard_map/all_to_all | solution.py:124
  84.5 6.7 %all-to-all-start.3 = ((bf16[32,128,128]{2,1,0:T(8,128)(2,1)}), bf16[32,128,128]{2,1,0:T(8,128)(2,1)}, u32[]{:S(2)}, u32[]{:S(2)}) async-start(bf16[32,128,128]{2,1,0:T(8,128)(2,1)} %broadcast_select_fusion), calls=%async_computation.3 | async-start | bytes 2097152 | tf_op jit(solution)/shard_map/all_to_all | solution.py:153
  96.0 18.8 %all-to-all-done.3 = bf16[32,128,128]{2,1,0:T(8,128)(2,1)} async-done(((bf16[32,128,128]{2,1,0:T(8,128)(2,1)}), bf16[32,128,128]{2,1,0:T(8,128)(2,1)}, u32[]{:S(2)}, u32[]{:S(2)}) %all-to-all-start.3) | async-done | bytes 1048608 | tf_op jit(solution)/shard_map/all_to_all | solution.py:153
  114.8 6.6 %all-to-all-start.2 = ((bf16[32,128,128]{2,1,0:T(8,128)(2,1)}), bf16[32,128,128]{2,1,0:T(8,128)(2,1)}, u32[]{:S(2)}, u32[]{:S(2)}) async-start(bf16[32,128,128]{2,1,0:T(8,128)(2,1)} %broadcast_select_fusion.1), calls=%async_computation.2 | async-start | bytes 2097152 | tf_op jit(solution)/shard_map/all_to_all | solution.py:164
  123.6 14.8 %collective-permute-start.1 = (f32[1,128,128]{2,0,1:T(1,128)S(1)}, f32[1,128,128]{2,0,1:T(1,128)S(1)}, u32[]{:S(2)}, u32[]{:S(2)}) collective-permute-start(f32[1,128,128]{2,0,1:T(1,128)S(1)} %get-tuple-element.11), channel_id=1, source_target_pairs={{0,8},{1,9},{2,10},{3,11},{4,12},{5,13},{6,14},{7,15},{8,16},{9,17... | collective-permute-start | bytes 196616 | tf_op jit(solution)/shard_map/ppermute | solution.py:88
  138.4 9.2 %collective-permute-start.3 = (f32[1,128,128]{2,0,1:T(1,128)S(1)}, f32[1,128,128]{2,0,1:T(1,128)S(1)}, u32[]{:S(2)}, u32[]{:S(2)}) collective-permute-start(f32[1,128,128]{2,0,1:T(1,128)S(1)} %get-tuple-element.12), channel_id=1, source_target_pairs={{0,24},{1,25},{2,26},{3,27},{4,28},{5,29},{6,30},{7,31},{8,0},{9,1... | collective-permute-start | bytes 196616 | tf_op jit(solution)/shard_map/ppermute | solution.py:89
  147.7 5.1 %collective-permute-start.2 = (f32[1,128,128]{2,0,1:T(1,128)S(1)}, f32[1,128,128]{2,0,1:T(1,128)S(1)}, u32[]{:S(2)}, u32[]{:S(2)}) collective-permute-start(f32[1,128,128]{2,0,1:T(1,128)S(1)} %collective-permute-done.1), channel_id=1, source_target_pairs={{0,8},{1,9},{2,10},{3,11},{4,12},{5,13},{6,14},{7,15},{8,16},{9,17... | collective-permute-start | bytes 196616 | tf_op jit(solution)/shard_map/ppermute | solution.py:88
  152.8 4.2 %collective-permute-start.4 = (f32[1,128,128]{2,0,1:T(1,128)S(1)}, f32[1,128,128]{2,0,1:T(1,128)S(1)}, u32[]{:S(2)}, u32[]{:S(2)}) collective-permute-start(f32[1,128,128]{2,0,1:T(1,128)S(1)} %collective-permute-done.3), channel_id=1, source_target_pairs={{0,24},{1,25},{2,26},{3,27},{4,28},{5,29},{6,30},{7,31},{8,0},{9,1... | collective-permute-start | bytes 196616 | tf_op jit(solution)/shard_map/ppermute | solution.py:89
  158.4 4.9 %collective-permute-done.4 = f32[1,128,128]{2,0,1:T(1,128)S(1)} collective-permute-done((f32[1,128,128]{2,0,1:T(1,128)S(1)}, f32[1,128,128]{2,0,1:T(1,128)S(1)}, u32[]{:S(2)}, u32[]{:S(2)}) %collective-permute-start.4) | collective-permute-done | bytes 65568 | tf_op jit(solution)/shard_map/ppermute | solution.py:89
  166.5 6.3 %collective-permute-start.5 = (bf16[128,1536]{1,0:T(8,128)(2,1)S(1)}, bf16[128,1536]{1,0:T(8,128)(2,1)S(1)}, u32[]{:S(2)}, u32[]{:S(2)}) collective-permute-start(bf16[128,1536]{1,0:T(8,128)(2,1)S(1)} %select_convert_fusion), channel_id=1, source_target_pairs={{0,1},{1,0},{2,3},{3,2},{4,5},{5,4},{6,7},{7,6},{8,9},{9,8},{10,11... | collective-permute-start | bytes 1179656 | tf_op jit(solution)/shard_map/ppermute | solution.py:59
  176.2 6.0 %collective-permute-done.6 = bf16[64,1536]{1,0:T(8,128)(2,1)S(1)} collective-permute-done((bf16[64,1536]{1,0:T(8,128)(2,1)S(1)}, bf16[64,1536]{1,0:T(8,128)(2,1)S(1)}, u32[]{:S(2)}, u32[]{:S(2)}) %collective-permute-start.6) | collective-permute-done | bytes 196640 | tf_op jit(solution)/shard_map/ppermute | solution.py:59
  182.3 3.4 %collective-permute-start.7 = (bf16[32,1536]{1,0:T(8,128)(2,1)S(1)}, bf16[32,1536]{1,0:T(8,128)(2,1)S(1)}, u32[]{:S(2)}, u32[]{:S(2)}) collective-permute-start(bf16[32,1536]{1,0:T(8,128)(2,1)S(1)} %select_convert_fusion.2), channel_id=1, source_target_pairs={{0,4},{1,5},{2,6},{3,7},{4,0},{5,1},{6,2},{7,3},{8,12},{9,13},{10,... | collective-permute-start | bytes 294920 | tf_op jit(solution)/shard_map/ppermute | solution.py:59
  185.8 5.8 %collective-permute-done.7 = bf16[32,1536]{1,0:T(8,128)(2,1)S(1)} collective-permute-done((bf16[32,1536]{1,0:T(8,128)(2,1)S(1)}, bf16[32,1536]{1,0:T(8,128)(2,1)S(1)}, u32[]{:S(2)}, u32[]{:S(2)}) %collective-permute-start.7) | collective-permute-done | bytes 98336 | tf_op jit(solution)/shard_map/ppermute | solution.py:59
  191.7 5.3 %collective-permute-start.8 = (bf16[16,1536]{1,0:T(8,128)(2,1)S(1)}, bf16[16,1536]{1,0:T(8,128)(2,1)S(1)}, u32[]{:S(2)}, u32[]{:S(2)}) collective-permute-start(bf16[16,1536]{1,0:T(8,128)(2,1)S(1)} %select_convert_fusion.3), channel_id=1, source_target_pairs={{0,8},{1,9},{2,10},{3,11},{4,12},{5,13},{6,14},{7,15},{8,0},{9,1},... | collective-permute-start | bytes 147464 | tf_op jit(solution)/shard_map/ppermute | solution.py:59
  197.0 5.3 %collective-permute-done.8 = bf16[16,1536]{1,0:T(8,128)(2,1)S(1)} collective-permute-done((bf16[16,1536]{1,0:T(8,128)(2,1)S(1)}, bf16[16,1536]{1,0:T(8,128)(2,1)S(1)}, u32[]{:S(2)}, u32[]{:S(2)}) %collective-permute-start.8) | collective-permute-done | bytes 49184 | tf_op jit(solution)/shard_map/ppermute | solution.py:59
  202.3 3.5 %collective-permute-start.9 = (bf16[16,1536]{1,0:T(8,128)(2,1)S(1)}, bf16[16,1536]{1,0:T(8,128)(2,1)S(1)}, u32[]{:S(2)}, u32[]{:S(2)}) collective-permute-start(bf16[16,1536]{1,0:T(8,128)(2,1)S(1)} %add_convert_fusion), channel_id=1, source_target_pairs={{0,8},{1,9},{2,10},{3,11},{4,12},{5,13},{6,14},{7,15},{8,0},{9,1},... | collective-permute-start | bytes 147464 | tf_op jit(solution)/shard_map/ppermute | solution.py:66
  205.8 5.3 %collective-permute-done.9 = bf16[16,1536]{1,0:T(8,128)(2,1)S(1)} collective-permute-done((bf16[16,1536]{1,0:T(8,128)(2,1)S(1)}, bf16[16,1536]{1,0:T(8,128)(2,1)S(1)}, u32[]{:S(2)}, u32[]{:S(2)}) %collective-permute-start.9) | collective-permute-done | bytes 49184 | tf_op jit(solution)/shard_map/ppermute | solution.py:66
  213.0 5.4 %collective-permute-done.10 = bf16[32,1536]{1,0:T(8,128)(2,1)S(1)} collective-permute-done((bf16[32,1536]{1,0:T(8,128)(2,1)S(1)}, bf16[32,1536]{1,0:T(8,128)(2,1)S(1)}, u32[]{:S(2)}, u32[]{:S(2)}) %collective-permute-start.10) | collective-permute-done | bytes 98336 | tf_op jit(solution)/shard_map/ppermute | solution.py:66
  218.4 2.9 %collective-permute-start.11 = (bf16[64,1536]{1,0:T(8,128)(2,1)S(1)}, bf16[64,1536]{1,0:T(8,128)(2,1)S(1)}, u32[]{:S(2)}, u32[]{:S(2)}) collective-permute-start(bf16[64,1536]{1,0:T(8,128)(2,1)S(1)} %maximum_select_fusion.2), channel_id=1, source_target_pairs={{0,2},{1,3},{2,0},{3,1},{4,6},{5,7},{6,4},{7,5},{8,10},{9,11},{10,... | collective-permute-start | bytes 589832 | tf_op jit(solution)/shard_map/ppermute | solution.py:66
  221.3 3.5 %collective-permute-done.11 = bf16[64,1536]{1,0:T(8,128)(2,1)S(1)} collective-permute-done((bf16[64,1536]{1,0:T(8,128)(2,1)S(1)}, bf16[64,1536]{1,0:T(8,128)(2,1)S(1)}, u32[]{:S(2)}, u32[]{:S(2)}) %collective-permute-start.11) | collective-permute-done | bytes 196640 | tf_op jit(solution)/shard_map/ppermute | solution.py:66
  224.9 6.0 %collective-permute-start.12 = (bf16[128,1536]{1,0:T(8,128)(2,1)S(1)}, bf16[128,1536]{1,0:T(8,128)(2,1)S(1)}, u32[]{:S(2)}, u32[]{:S(2)}) collective-permute-start(bf16[128,1536]{1,0:T(8,128)(2,1)S(1)} %maximum_select_fusion.1), channel_id=1, source_target_pairs={{0,1},{1,0},{2,3},{3,2},{4,5},{5,4},{6,7},{7,6},{8,9},{9,8},{10,11... | collective-permute-start | bytes 1179656 | tf_op jit(solution)/shard_map/ppermute | solution.py:66
  (93 shorter events, 45.4 us)
Async XLA Ops:
  0.0 1.1 copy-start
  6.7 33.1 %all-to-all-start = ((bf16[32,128,128]{2,1,0:T(8,128)(2,1)}), bf16[32,128,128]{2,1,0:T(8,128)(2,1)S(1)}, u32[]{:S(2)}, u32[]{:S(2)}) async-start(bf16[32,128,128]{2,1,0:T(8,128)(2,1)} %gather_fusion), calls=%async_computation | async-start | bytes 2097152 | tf_op jit(solution)/shard_map/all_to_all | solution.py:123
  17.2 20.9 %collective-permute-start = (bf16[2,128,128]{2,1,0:T(8,128)(2,1)S(1)}, bf16[2,128,128]{2,1,0:T(8,128)(2,1)S(1)}, u32[]{:S(2)}, u32[]{:S(2)}) collective-permute-start(bf16[2,128,128]{2,1,0:T(8,128)(2,1)S(1)} %bitcast_bitcast_fusion), channel_id=1, source_target_pairs={{0,16},{16,0},{1,17},{17,1},{2,18},{18,2},{3,19},{19,3},{4,20},{20... | collective-permute-start | bytes 196616 | tf_op jit(solution)/shard_map/ppermute | solution.py:114
  36.3 13.0 %copy-start.6 = (bf16[64,1536]{1,0:T(8,128)(2,1)S(1)}, bf16[64,1536]{1,0:T(8,128)(2,1)}, u32[]{:S(2)}) copy-start(bf16[64,1536]{1,0:T(8,128)(2,1)} %param.14) | copy-start | bytes 589828
  39.7 11.0 %copy-start.5 = (bf16[1536,64]{0,1:T(8,128)(2,1)S(1)}, bf16[1536,64]{0,1:T(8,128)(2,1)}, u32[]{:S(2)}) copy-start(bf16[1536,64]{0,1:T(8,128)(2,1)} %param.11) | copy-start | bytes 589828
  39.7 33.4 %all-to-all-start.1 = ((bf16[32,128,128]{2,1,0:T(8,128)(2,1)}), bf16[32,128,128]{2,1,0:T(8,128)(2,1)S(1)}, u32[]{:S(2)}, u32[]{:S(2)}) async-start(bf16[32,128,128]{2,1,0:T(8,128)(2,1)} %gather_fusion.2), calls=%async_computation.1 | async-start | bytes 2097152 | tf_op jit(solution)/shard_map/all_to_all | solution.py:124
  79.4 1.0 copy-start.1
  84.5 30.3 %all-to-all-start.3 = ((bf16[32,128,128]{2,1,0:T(8,128)(2,1)}), bf16[32,128,128]{2,1,0:T(8,128)(2,1)}, u32[]{:S(2)}, u32[]{:S(2)}) async-start(bf16[32,128,128]{2,1,0:T(8,128)(2,1)} %broadcast_select_fusion), calls=%async_computation.3 | async-start | bytes 2097152 | tf_op jit(solution)/shard_map/all_to_all | solution.py:153
  96.0 61.0 %copy-start.2 = (bf16[2,128,16,128]{1,3,2,0:T(8,128)(2,1)S(1)}, bf16[2,128,16,128]{1,3,2,0:T(8,128)(2,1)}, u32[]{:S(2)}) copy-start(bf16[2,128,16,128]{1,3,2,0:T(8,128)(2,1)} %copy-done.1) | copy-start | bytes 3145732
  114.8 42.6 %all-to-all-start.2 = ((bf16[32,128,128]{2,1,0:T(8,128)(2,1)}), bf16[32,128,128]{2,1,0:T(8,128)(2,1)}, u32[]{:S(2)}, u32[]{:S(2)}) async-start(bf16[32,128,128]{2,1,0:T(8,128)(2,1)} %broadcast_select_fusion.1), calls=%async_computation.2 | async-start | bytes 2097152 | tf_op jit(solution)/shard_map/all_to_all | solution.py:164
  123.5 41.7 %copy-start.3 = (bf16[1536,64]{0,1:T(8,128)(2,1)S(1)}, bf16[1536,64]{0,1:T(8,128)(2,1)}, u32[]{:S(2)}) copy-start(bf16[1536,64]{0,1:T(8,128)(2,1)} %param.12) | copy-start | bytes 589828
  123.6 24.0 %collective-permute-start.1 = (f32[1,128,128]{2,0,1:T(1,128)S(1)}, f32[1,128,128]{2,0,1:T(1,128)S(1)}, u32[]{:S(2)}, u32[]{:S(2)}) collective-permute-start(f32[1,128,128]{2,0,1:T(1,128)S(1)} %get-tuple-element.11), channel_id=1, source_target_pairs={{0,8},{1,9},{2,10},{3,11},{4,12},{5,13},{6,14},{7,15},{8,16},{9,17... | collective-permute-start | bytes 196616 | tf_op jit(solution)/shard_map/ppermute | solution.py:88
  138.4 14.3 %collective-permute-start.3 = (f32[1,128,128]{2,0,1:T(1,128)S(1)}, f32[1,128,128]{2,0,1:T(1,128)S(1)}, u32[]{:S(2)}, u32[]{:S(2)}) collective-permute-start(f32[1,128,128]{2,0,1:T(1,128)S(1)} %get-tuple-element.12), channel_id=1, source_target_pairs={{0,24},{1,25},{2,26},{3,27},{4,28},{5,29},{6,30},{7,31},{8,0},{9,1... | collective-permute-start | bytes 196616 | tf_op jit(solution)/shard_map/ppermute | solution.py:89
  147.7 10.7 %collective-permute-start.2 = (f32[1,128,128]{2,0,1:T(1,128)S(1)}, f32[1,128,128]{2,0,1:T(1,128)S(1)}, u32[]{:S(2)}, u32[]{:S(2)}) collective-permute-start(f32[1,128,128]{2,0,1:T(1,128)S(1)} %collective-permute-done.1), channel_id=1, source_target_pairs={{0,8},{1,9},{2,10},{3,11},{4,12},{5,13},{6,14},{7,15},{8,16},{9,17... | collective-permute-start | bytes 196616 | tf_op jit(solution)/shard_map/ppermute | solution.py:88
  152.8 10.5 %collective-permute-start.4 = (f32[1,128,128]{2,0,1:T(1,128)S(1)}, f32[1,128,128]{2,0,1:T(1,128)S(1)}, u32[]{:S(2)}, u32[]{:S(2)}) collective-permute-start(f32[1,128,128]{2,0,1:T(1,128)S(1)} %collective-permute-done.3), channel_id=1, source_target_pairs={{0,24},{1,25},{2,26},{3,27},{4,28},{5,29},{6,30},{7,31},{8,0},{9,1... | collective-permute-start | bytes 196616 | tf_op jit(solution)/shard_map/ppermute | solution.py:89
  157.3 8.3 %copy-start.4 = (bf16[1536,64]{0,1:T(8,128)(2,1)S(1)}, bf16[1536,64]{0,1:T(8,128)(2,1)}, u32[]{:S(2)}) copy-start(bf16[1536,64]{0,1:T(8,128)(2,1)} %param.13) | copy-start | bytes 589828
  166.5 7.6 %collective-permute-start.5 = (bf16[128,1536]{1,0:T(8,128)(2,1)S(1)}, bf16[128,1536]{1,0:T(8,128)(2,1)S(1)}, u32[]{:S(2)}, u32[]{:S(2)}) collective-permute-start(bf16[128,1536]{1,0:T(8,128)(2,1)S(1)} %select_convert_fusion), channel_id=1, source_target_pairs={{0,1},{1,0},{2,3},{3,2},{4,5},{5,4},{6,7},{7,6},{8,9},{9,8},{10,11... | collective-permute-start | bytes 1179656 | tf_op jit(solution)/shard_map/ppermute | solution.py:59
  174.3 8.0 %collective-permute-start.6 = (bf16[64,1536]{1,0:T(8,128)(2,1)S(1)}, bf16[64,1536]{1,0:T(8,128)(2,1)S(1)}, u32[]{:S(2)}, u32[]{:S(2)}) collective-permute-start(bf16[64,1536]{1,0:T(8,128)(2,1)S(1)} %select_convert_fusion.1), channel_id=1, source_target_pairs={{0,2},{1,3},{2,0},{3,1},{4,6},{5,7},{6,4},{7,5},{8,10},{9,11},{10,... | collective-permute-start | bytes 589832 | tf_op jit(solution)/shard_map/ppermute | solution.py:59
  182.3 9.3 %collective-permute-start.7 = (bf16[32,1536]{1,0:T(8,128)(2,1)S(1)}, bf16[32,1536]{1,0:T(8,128)(2,1)S(1)}, u32[]{:S(2)}, u32[]{:S(2)}) collective-permute-start(bf16[32,1536]{1,0:T(8,128)(2,1)S(1)} %select_convert_fusion.2), channel_id=1, source_target_pairs={{0,4},{1,5},{2,6},{3,7},{4,0},{5,1},{6,2},{7,3},{8,12},{9,13},{10,... | collective-permute-start | bytes 294920 | tf_op jit(solution)/shard_map/ppermute | solution.py:59
  191.7 10.6 %collective-permute-start.8 = (bf16[16,1536]{1,0:T(8,128)(2,1)S(1)}, bf16[16,1536]{1,0:T(8,128)(2,1)S(1)}, u32[]{:S(2)}, u32[]{:S(2)}) collective-permute-start(bf16[16,1536]{1,0:T(8,128)(2,1)S(1)} %select_convert_fusion.3), channel_id=1, source_target_pairs={{0,8},{1,9},{2,10},{3,11},{4,12},{5,13},{6,14},{7,15},{8,0},{9,1},... | collective-permute-start | bytes 147464 | tf_op jit(solution)/shard_map/ppermute | solution.py:59
  202.3 8.7 %collective-permute-start.9 = (bf16[16,1536]{1,0:T(8,128)(2,1)S(1)}, bf16[16,1536]{1,0:T(8,128)(2,1)S(1)}, u32[]{:S(2)}, u32[]{:S(2)}) collective-permute-start(bf16[16,1536]{1,0:T(8,128)(2,1)S(1)} %add_convert_fusion), channel_id=1, source_target_pairs={{0,8},{1,9},{2,10},{3,11},{4,12},{5,13},{6,14},{7,15},{8,0},{9,1},... | collective-permute-start | bytes 147464 | tf_op jit(solution)/shard_map/ppermute | solution.py:66
  211.1 7.3 %collective-permute-start.10 = (bf16[32,1536]{1,0:T(8,128)(2,1)S(1)}, bf16[32,1536]{1,0:T(8,128)(2,1)S(1)}, u32[]{:S(2)}, u32[]{:S(2)}) collective-permute-start(bf16[32,1536]{1,0:T(8,128)(2,1)S(1)} %maximum_select_fusion.3), channel_id=1, source_target_pairs={{0,4},{1,5},{2,6},{3,7},{4,0},{5,1},{6,2},{7,3},{8,12},{9,13},{10,... | collective-permute-start | bytes 294920 | tf_op jit(solution)/shard_map/ppermute | solution.py:66
  218.4 6.4 %collective-permute-start.11 = (bf16[64,1536]{1,0:T(8,128)(2,1)S(1)}, bf16[64,1536]{1,0:T(8,128)(2,1)S(1)}, u32[]{:S(2)}, u32[]{:S(2)}) collective-permute-start(bf16[64,1536]{1,0:T(8,128)(2,1)S(1)} %maximum_select_fusion.2), channel_id=1, source_target_pairs={{0,2},{1,3},{2,0},{3,1},{4,6},{5,7},{6,4},{7,5},{8,10},{9,11},{10,... | collective-permute-start | bytes 589832 | tf_op jit(solution)/shard_map/ppermute | solution.py:66
  224.9 7.3 %collective-permute-start.12 = (bf16[128,1536]{1,0:T(8,128)(2,1)S(1)}, bf16[128,1536]{1,0:T(8,128)(2,1)S(1)}, u32[]{:S(2)}, u32[]{:S(2)}) collective-permute-start(bf16[128,1536]{1,0:T(8,128)(2,1)S(1)} %maximum_select_fusion.1), channel_id=1, source_target_pairs={{0,1},{1,0},{2,3},{3,2},{4,5},{5,4},{6,7},{7,6},{8,9},{9,8},{10,11... | collective-permute-start | bytes 1179656 | tf_op jit(solution)/shard_map/ppermute | solution.py:66

commit v10 on v8

--- a/solution.py
+++ b/solution.py
@@ -138,7 +138,7 @@
         far_back,
         preferred_element_type=jnp.float32,
     )
-    other_back = lax.ppermute(other, "zh", swap)
+    other_back = lax.ppermute(other.astype(jnp.bfloat16), "zh", swap).astype(jnp.float32)
     near_back = lax.all_to_all(
         jnp.take(pair_grads, near_pair, axis=0, mode="fill", fill_value=0),
         "tq", split_axis=0, concat_axis=0, tiled=True,

time: 228 us -> 228 us (level)
  starting transfers between devices: 124 us -> 128 us
  waiting for transfers between devices: 64.9 us -> 62 us
    ppermute x4, starting transfers between devices: 25.2 us -> 28 us  [head_sum(): lax.ppermute(send.astype(jnp.bfloat16), 'tensor', [(i, i ^ step) for i in...]
where the time goes in v10:
time: 228 us; the launch traced here: 227 us
  starting transfers between devices  128 us (56%)
  waiting for transfers between devices  62 us (27%)
  local copies, waits for them, and re-layouts  14 us (6%)
  matrix products  12.8 us (6%)
  other arithmetic  9.17 us (4%)
    ppermute x4, starting transfers between devices, head_sum(): lax.ppermute(send.astype(jnp.bfloat16), 'tensor', [(i, i ^ step) for i in...  28 us
    ppermute x4, starting transfers between devices, head_sum(): got = lax.ppermute(cur, 'tensor', [(i, i ^ step) for i in range(count)])  24.3 us
    ppermute x1, starting transfers between devices, local(): lax.ppermute(other.astype(jnp.bfloat16), 'zh', swap).astype(jnp.float32)  23.4 us
    all_to_all x1, waiting for transfers between devices, local(): lax.all_to_all(mirror_spans[mirror_slot], 'tq', split_axis=0, concat_axis...  19.5 us
    ppermute x1, starting transfers between devices, local(): mirror_spans = lax.ppermute(paired_spans, 'zh', swap)  19.1 us
    all_to_all x1, waiting for transfers between devices, local(): lax.all_to_all(jnp.take(pair_grads, far_pair, axis=0, mode='fill', fill_v...  18.8 us
    ppermute x4, waiting for transfers between devices, head_sum(): lax.ppermute(send.astype(jnp.bfloat16), 'tensor', [(i, i ^ step) for i in...  11.1 us
    all_to_all x1, starting transfers between devices, local(): lax.all_to_all(paired_spans[own_slot], 'tq', split_axis=0, concat_axis=0,...  10.5 us
  transfers between devices with their start and end apart: 14, of which 12 were waited for; matrix products, arithmetic and copies ran while one was open for 6% of the time, Pallas kernels for 0%

profile of v10, /device:TPU:1, one launch (start us, length us, event | category | flops | bytes accessed | tf_op | source)
XLA Modules:
  0.0 226.6 jit_solution(10924492871048369800)
XLA Ops:
  6.7 10.5 %all-to-all-start = ((bf16[32,128,128]{2,1,0:T(8,128)(2,1)}), bf16[32,128,128]{2,1,0:T(8,128)(2,1)S(1)}, u32[]{:S(2)}, u32[]{:S(2)}) async-start(bf16[32,128,128]{2,1,0:T(8,128)(2,1)} %gather_fusion), calls=%async_computation | async-start | bytes 2097152 | tf_op jit(solution)/shard_map/all_to_all | solution.py:101
  17.2 19.1 %collective-permute-start = (bf16[2,128,128]{2,1,0:T(8,128)(2,1)S(1)}, bf16[2,128,128]{2,1,0:T(8,128)(2,1)S(1)}, u32[]{:S(2)}, u32[]{:S(2)}) collective-permute-start(bf16[2,128,128]{2,1,0:T(8,128)(2,1)S(1)} %bitcast_bitcast_fusion), channel_id=1, source_target_pairs={{0,16},{16,0},{1,17},{17,1},{2,18},{18,2},{3,19},{19,3},{4,20},{20... | collective-permute-start | bytes 196616 | tf_op jit(solution)/shard_map/ppermute | solution.py:92
  39.7 9.5 %all-to-all-start.1 = ((bf16[32,128,128]{2,1,0:T(8,128)(2,1)}), bf16[32,128,128]{2,1,0:T(8,128)(2,1)S(1)}, u32[]{:S(2)}, u32[]{:S(2)}) async-start(bf16[32,128,128]{2,1,0:T(8,128)(2,1)} %gather_fusion.2), calls=%async_computation.1 | async-start | bytes 2097152 | tf_op jit(solution)/shard_map/all_to_all | solution.py:102
  53.5 19.5 %all-to-all-done.1 = bf16[32,128,128]{2,1,0:T(8,128)(2,1)S(1)} async-done(((bf16[32,128,128]{2,1,0:T(8,128)(2,1)}), bf16[32,128,128]{2,1,0:T(8,128)(2,1)S(1)}, u32[]{:S(2)}, u32[]{:S(2)}) %all-to-all-start.1) | async-done | bytes 1048608 | tf_op jit(solution)/shard_map/all_to_all | solution.py:102
  82.1 2.3 %broadcast_select_fusion = bf16[32,128,128]{2,1,0:T(8,128)(2,1)} fusion(bf16[32,128,128]{2,1,0:T(8,128)(2,1)} %gather_fusion.5, pred[32]{0:T(512)(128)(4,1)S(1)} %compare_and_fusion.1), kind=kLoop, calls=%fused_computation.35 | loop fusion | flops 524288 | bytes 2097184 | tf_op jit(solution)/shard_map/jit(_take)/select_n | solution.py:132
  84.5 6.7 %all-to-all-start.3 = ((bf16[32,128,128]{2,1,0:T(8,128)(2,1)}), bf16[32,128,128]{2,1,0:T(8,128)(2,1)}, u32[]{:S(2)}, u32[]{:S(2)}) async-start(bf16[32,128,128]{2,1,0:T(8,128)(2,1)} %broadcast_select_fusion), calls=%async_computation.3 | async-start | bytes 2097152 | tf_op jit(solution)/shard_map/all_to_all | solution.py:131
  93.6 2.4 %broadcast_select_fusion.1 = bf16[32,128,128]{2,1,0:T(8,128)(2,1)} fusion(bf16[32,128,128]{2,1,0:T(8,128)(2,1)} %gather_fusion.4, pred[32]{0:T(512)(128)(4,1)S(1)} %compare_and_fusion.2), kind=kLoop, calls=%fused_computation.36 | loop fusion | flops 524288 | bytes 2097184 | tf_op jit(solution)/shard_map/jit(_take)/select_n | solution.py:143
  96.0 18.8 %all-to-all-done.3 = bf16[32,128,128]{2,1,0:T(8,128)(2,1)} async-done(((bf16[32,128,128]{2,1,0:T(8,128)(2,1)}), bf16[32,128,128]{2,1,0:T(8,128)(2,1)}, u32[]{:S(2)}, u32[]{:S(2)}) %all-to-all-start.3) | async-done | bytes 1048608 | tf_op jit(solution)/shard_map/all_to_all | solution.py:131
  114.8 6.6 %all-to-all-start.2 = ((bf16[32,128,128]{2,1,0:T(8,128)(2,1)}), bf16[32,128,128]{2,1,0:T(8,128)(2,1)}, u32[]{:S(2)}, u32[]{:S(2)}) async-start(bf16[32,128,128]{2,1,0:T(8,128)(2,1)} %broadcast_select_fusion.1), calls=%async_computation.2 | async-start | bytes 2097152 | tf_op jit(solution)/shard_map/all_to_all | solution.py:142
  121.6 1.9 convolution_convert_fusion.1
  123.6 23.4 %collective-permute-start.1 = (bf16[2,128,128]{2,0,1:T(2,128)(2,1)S(1)}, bf16[2,128,128]{2,0,1:T(2,128)(2,1)}, u32[]{:S(2)}, u32[]{:S(2)}) collective-permute-start(bf16[2,128,128]{2,0,1:T(2,128)(2,1)S(1)} %convolution_convert_fusion.1), channel_id=1, source_target_pairs={{0,16},{16,0},{1,17},{17,1},{2,18},{18,2},{3,19},{19,3},{4,20},{20... | collective-permute-start | bytes 196616 | tf_op jit(solution)/shard_map/ppermute | solution.py:141
  148.9 1.9 fusion.15
  152.2 5.4 %collective-permute-start.2 = (bf16[128,1536]{1,0:T(8,128)(2,1)S(1)}, bf16[128,1536]{1,0:T(8,128)(2,1)S(1)}, u32[]{:S(2)}, u32[]{:S(2)}) collective-permute-start(bf16[128,1536]{1,0:T(8,128)(2,1)S(1)} %select_convert_fusion), channel_id=1, source_target_pairs={{0,1},{1,0},{2,3},{3,2},{4,5},{5,4},{6,7},{7,6},{8,9},{9,8},{10,11... | collective-permute-start | bytes 1179656 | tf_op jit(solution)/shard_map/ppermute | solution.py:59
  159.1 6.1 %collective-permute-start.3 = (bf16[64,1536]{1,0:T(8,128)(2,1)S(1)}, bf16[64,1536]{1,0:T(8,128)(2,1)S(1)}, u32[]{:S(2)}, u32[]{:S(2)}) collective-permute-start(bf16[64,1536]{1,0:T(8,128)(2,1)S(1)} %select_convert_fusion.1), channel_id=1, source_target_pairs={{0,2},{1,3},{2,0},{3,1},{4,6},{5,7},{6,4},{7,5},{8,10},{9,11},{10,... | collective-permute-start | bytes 589832 | tf_op jit(solution)/shard_map/ppermute | solution.py:59
  165.2 4.9 %collective-permute-done.3 = bf16[64,1536]{1,0:T(8,128)(2,1)S(1)} collective-permute-done((bf16[64,1536]{1,0:T(8,128)(2,1)S(1)}, bf16[64,1536]{1,0:T(8,128)(2,1)S(1)}, u32[]{:S(2)}, u32[]{:S(2)}) %collective-permute-start.3) | collective-permute-done | bytes 196640 | tf_op jit(solution)/shard_map/ppermute | solution.py:59
  170.2 5.9 %collective-permute-start.4 = (bf16[32,1536]{1,0:T(8,128)(2,1)S(1)}, bf16[32,1536]{1,0:T(8,128)(2,1)S(1)}, u32[]{:S(2)}, u32[]{:S(2)}) collective-permute-start(bf16[32,1536]{1,0:T(8,128)(2,1)S(1)} %select_convert_fusion.2), channel_id=1, source_target_pairs={{0,4},{1,5},{2,6},{3,7},{4,0},{5,1},{6,2},{7,3},{8,12},{9,13},{10,... | collective-permute-start | bytes 294920 | tf_op jit(solution)/shard_map/ppermute | solution.py:59
  176.1 3.4 %collective-permute-done.4 = bf16[32,1536]{1,0:T(8,128)(2,1)S(1)} collective-permute-done((bf16[32,1536]{1,0:T(8,128)(2,1)S(1)}, bf16[32,1536]{1,0:T(8,128)(2,1)S(1)}, u32[]{:S(2)}, u32[]{:S(2)}) %collective-permute-start.4) | collective-permute-done | bytes 98336 | tf_op jit(solution)/shard_map/ppermute | solution.py:59
  179.5 10.6 %collective-permute-start.5 = (bf16[16,1536]{1,0:T(8,128)(2,1)S(1)}, bf16[16,1536]{1,0:T(8,128)(2,1)S(1)}, u32[]{:S(2)}, u32[]{:S(2)}) collective-permute-start(bf16[16,1536]{1,0:T(8,128)(2,1)S(1)} %select_convert_fusion.3), channel_id=1, source_target_pairs={{0,8},{1,9},{2,10},{3,11},{4,12},{5,13},{6,14},{7,15},{8,0},{9,1},... | collective-permute-start | bytes 147464 | tf_op jit(solution)/shard_map/ppermute | solution.py:59
  191.6 7.3 %collective-permute-start.6 = (bf16[16,1536]{1,0:T(8,128)(2,1)S(1)}, bf16[16,1536]{1,0:T(8,128)(2,1)S(1)}, u32[]{:S(2)}, u32[]{:S(2)}) collective-permute-start(bf16[16,1536]{1,0:T(8,128)(2,1)S(1)} %add_convert_fusion.1), channel_id=1, source_target_pairs={{0,8},{1,9},{2,10},{3,11},{4,12},{5,13},{6,14},{7,15},{8,0},{9,1},... | collective-permute-start | bytes 147464 | tf_op jit(solution)/shard_map/ppermute | solution.py:66
  200.3 3.0 %collective-permute-start.7 = (bf16[32,1536]{1,0:T(8,128)(2,1)S(1)}, bf16[32,1536]{1,0:T(8,128)(2,1)S(1)}, u32[]{:S(2)}, u32[]{:S(2)}) collective-permute-start(bf16[32,1536]{1,0:T(8,128)(2,1)S(1)} %maximum_select_fusion.3), channel_id=1, source_target_pairs={{0,4},{1,5},{2,6},{3,7},{4,0},{5,1},{6,2},{7,3},{8,12},{9,13},{10,... | collective-permute-start | bytes 294920 | tf_op jit(solution)/shard_map/ppermute | solution.py:66
  203.3 3.4 %collective-permute-done.7 = bf16[32,1536]{1,0:T(8,128)(2,1)S(1)} collective-permute-done((bf16[32,1536]{1,0:T(8,128)(2,1)S(1)}, bf16[32,1536]{1,0:T(8,128)(2,1)S(1)}, u32[]{:S(2)}, u32[]{:S(2)}) %collective-permute-start.7) | collective-permute-done | bytes 98336 | tf_op jit(solution)/shard_map/ppermute | solution.py:66
  206.8 7.7 %collective-permute-start.8 = (bf16[64,1536]{1,0:T(8,128)(2,1)S(1)}, bf16[64,1536]{1,0:T(8,128)(2,1)S(1)}, u32[]{:S(2)}, u32[]{:S(2)}) collective-permute-start(bf16[64,1536]{1,0:T(8,128)(2,1)S(1)} %maximum_select_fusion.2), channel_id=1, source_target_pairs={{0,2},{1,3},{2,0},{3,1},{4,6},{5,7},{6,4},{7,5},{8,10},{9,11},{10,... | collective-permute-start | bytes 589832 | tf_op jit(solution)/shard_map/ppermute | solution.py:66
  214.4 3.0 %collective-permute-done.8 = bf16[64,1536]{1,0:T(8,128)(2,1)S(1)} collective-permute-done((bf16[64,1536]{1,0:T(8,128)(2,1)S(1)}, bf16[64,1536]{1,0:T(8,128)(2,1)S(1)}, u32[]{:S(2)}, u32[]{:S(2)}) %collective-permute-start.8) | collective-permute-done | bytes 196640 | tf_op jit(solution)/shard_map/ppermute | solution.py:66
  217.6 6.4 %collective-permute-start.9 = (bf16[128,1536]{1,0:T(8,128)(2,1)S(1)}, bf16[128,1536]{1,0:T(8,128)(2,1)S(1)}, u32[]{:S(2)}, u32[]{:S(2)}) collective-permute-start(bf16[128,1536]{1,0:T(8,128)(2,1)S(1)} %maximum_select_fusion.1), channel_id=1, source_target_pairs={{0,1},{1,0},{2,3},{3,2},{4,5},{5,4},{6,7},{7,6},{8,9},{9,8},{10,11... | collective-permute-start | bytes 1179656 | tf_op jit(solution)/shard_map/ppermute | solution.py:66
  (86 shorter events, 36.4 us)
Async XLA Ops:
  0.0 1.1 copy-start
  6.7 33.1 %all-to-all-start = ((bf16[32,128,128]{2,1,0:T(8,128)(2,1)}), bf16[32,128,128]{2,1,0:T(8,128)(2,1)S(1)}, u32[]{:S(2)}, u32[]{:S(2)}) async-start(bf16[32,128,128]{2,1,0:T(8,128)(2,1)} %gather_fusion), calls=%async_computation | async-start | bytes 2097152 | tf_op jit(solution)/shard_map/all_to_all | solution.py:101
  17.2 20.9 %collective-permute-start = (bf16[2,128,128]{2,1,0:T(8,128)(2,1)S(1)}, bf16[2,128,128]{2,1,0:T(8,128)(2,1)S(1)}, u32[]{:S(2)}, u32[]{:S(2)}) collective-permute-start(bf16[2,128,128]{2,1,0:T(8,128)(2,1)S(1)} %bitcast_bitcast_fusion), channel_id=1, source_target_pairs={{0,16},{16,0},{1,17},{17,1},{2,18},{18,2},{3,19},{19,3},{4,20},{20... | collective-permute-start | bytes 196616 | tf_op jit(solution)/shard_map/ppermute | solution.py:92
  36.3 13.0 %copy-start.6 = (bf16[64,1536]{1,0:T(8,128)(2,1)S(1)}, bf16[64,1536]{1,0:T(8,128)(2,1)}, u32[]{:S(2)}) copy-start(bf16[64,1536]{1,0:T(8,128)(2,1)} %param.14) | copy-start | bytes 589828
  39.7 11.0 %copy-start.5 = (bf16[1536,64]{0,1:T(8,128)(2,1)S(1)}, bf16[1536,64]{0,1:T(8,128)(2,1)}, u32[]{:S(2)}) copy-start(bf16[1536,64]{0,1:T(8,128)(2,1)} %param.11) | copy-start | bytes 589828
  39.7 33.4 %all-to-all-start.1 = ((bf16[32,128,128]{2,1,0:T(8,128)(2,1)}), bf16[32,128,128]{2,1,0:T(8,128)(2,1)S(1)}, u32[]{:S(2)}, u32[]{:S(2)}) async-start(bf16[32,128,128]{2,1,0:T(8,128)(2,1)} %gather_fusion.2), calls=%async_computation.1 | async-start | bytes 2097152 | tf_op jit(solution)/shard_map/all_to_all | solution.py:102
  79.4 1.0 copy-start.1
  84.5 30.3 %all-to-all-start.3 = ((bf16[32,128,128]{2,1,0:T(8,128)(2,1)}), bf16[32,128,128]{2,1,0:T(8,128)(2,1)}, u32[]{:S(2)}, u32[]{:S(2)}) async-start(bf16[32,128,128]{2,1,0:T(8,128)(2,1)} %broadcast_select_fusion), calls=%async_computation.3 | async-start | bytes 2097152 | tf_op jit(solution)/shard_map/all_to_all | solution.py:131
  96.0 51.0 %copy-start.2 = (bf16[2,128,16,128]{1,3,2,0:T(8,128)(2,1)S(1)}, bf16[2,128,16,128]{1,3,2,0:T(8,128)(2,1)}, u32[]{:S(2)}) copy-start(bf16[2,128,16,128]{1,3,2,0:T(8,128)(2,1)} %copy-done.1) | copy-start | bytes 3145732
  114.8 32.6 %all-to-all-start.2 = ((bf16[32,128,128]{2,1,0:T(8,128)(2,1)}), bf16[32,128,128]{2,1,0:T(8,128)(2,1)}, u32[]{:S(2)}, u32[]{:S(2)}) async-start(bf16[32,128,128]{2,1,0:T(8,128)(2,1)} %broadcast_select_fusion.1), calls=%async_computation.2 | async-start | bytes 2097152 | tf_op jit(solution)/shard_map/all_to_all | solution.py:142
  121.6 29.3 %copy-start.3 = (bf16[1536,64]{0,1:T(8,128)(2,1)S(1)}, bf16[1536,64]{0,1:T(8,128)(2,1)}, u32[]{:S(2)}) copy-start(bf16[1536,64]{0,1:T(8,128)(2,1)} %param.12) | copy-start | bytes 589828
  123.6 27.7 %copy-start.4 = (bf16[1536,64]{0,1:T(8,128)(2,1)S(1)}, bf16[1536,64]{0,1:T(8,128)(2,1)}, u32[]{:S(2)}) copy-start(bf16[1536,64]{0,1:T(8,128)(2,1)} %param.13) | copy-start | bytes 589828
  123.6 25.3 %collective-permute-start.1 = (bf16[2,128,128]{2,0,1:T(2,128)(2,1)S(1)}, bf16[2,128,128]{2,0,1:T(2,128)(2,1)}, u32[]{:S(2)}, u32[]{:S(2)}) collective-permute-start(bf16[2,128,128]{2,0,1:T(2,128)(2,1)S(1)} %convolution_convert_fusion.1), channel_id=1, source_target_pairs={{0,16},{16,0},{1,17},{17,1},{2,18},{18,2},{3,19},{19,3},{4,20},{20... | collective-permute-start | bytes 196616 | tf_op jit(solution)/shard_map/ppermute | solution.py:141
  152.2 6.8 %collective-permute-start.2 = (bf16[128,1536]{1,0:T(8,128)(2,1)S(1)}, bf16[128,1536]{1,0:T(8,128)(2,1)S(1)}, u32[]{:S(2)}, u32[]{:S(2)}) collective-permute-start(bf16[128,1536]{1,0:T(8,128)(2,1)S(1)} %select_convert_fusion), channel_id=1, source_target_pairs={{0,1},{1,0},{2,3},{3,2},{4,5},{5,4},{6,7},{7,6},{8,9},{9,8},{10,11... | collective-permute-start | bytes 1179656 | tf_op jit(solution)/shard_map/ppermute | solution.py:59
  159.1 11.0 %collective-permute-start.3 = (bf16[64,1536]{1,0:T(8,128)(2,1)S(1)}, bf16[64,1536]{1,0:T(8,128)(2,1)S(1)}, u32[]{:S(2)}, u32[]{:S(2)}) collective-permute-start(bf16[64,1536]{1,0:T(8,128)(2,1)S(1)} %select_convert_fusion.1), channel_id=1, source_target_pairs={{0,2},{1,3},{2,0},{3,1},{4,6},{5,7},{6,4},{7,5},{8,10},{9,11},{10,... | collective-permute-start | bytes 589832 | tf_op jit(solution)/shard_map/ppermute | solution.py:59
  170.2 9.3 %collective-permute-start.4 = (bf16[32,1536]{1,0:T(8,128)(2,1)S(1)}, bf16[32,1536]{1,0:T(8,128)(2,1)S(1)}, u32[]{:S(2)}, u32[]{:S(2)}) collective-permute-start(bf16[32,1536]{1,0:T(8,128)(2,1)S(1)} %select_convert_fusion.2), channel_id=1, source_target_pairs={{0,4},{1,5},{2,6},{3,7},{4,0},{5,1},{6,2},{7,3},{8,12},{9,13},{10,... | collective-permute-start | bytes 294920 | tf_op jit(solution)/shard_map/ppermute | solution.py:59
  179.5 12.1 %collective-permute-start.5 = (bf16[16,1536]{1,0:T(8,128)(2,1)S(1)}, bf16[16,1536]{1,0:T(8,128)(2,1)S(1)}, u32[]{:S(2)}, u32[]{:S(2)}) collective-permute-start(bf16[16,1536]{1,0:T(8,128)(2,1)S(1)} %select_convert_fusion.3), channel_id=1, source_target_pairs={{0,8},{1,9},{2,10},{3,11},{4,12},{5,13},{6,14},{7,15},{8,0},{9,1},... | collective-permute-start | bytes 147464 | tf_op jit(solution)/shard_map/ppermute | solution.py:59
  191.6 8.7 %collective-permute-start.6 = (bf16[16,1536]{1,0:T(8,128)(2,1)S(1)}, bf16[16,1536]{1,0:T(8,128)(2,1)S(1)}, u32[]{:S(2)}, u32[]{:S(2)}) collective-permute-start(bf16[16,1536]{1,0:T(8,128)(2,1)S(1)} %add_convert_fusion.1), channel_id=1, source_target_pairs={{0,8},{1,9},{2,10},{3,11},{4,12},{5,13},{6,14},{7,15},{8,0},{9,1},... | collective-permute-start | bytes 147464 | tf_op jit(solution)/shard_map/ppermute | solution.py:66
  200.3 6.4 %collective-permute-start.7 = (bf16[32,1536]{1,0:T(8,128)(2,1)S(1)}, bf16[32,1536]{1,0:T(8,128)(2,1)S(1)}, u32[]{:S(2)}, u32[]{:S(2)}) collective-permute-start(bf16[32,1536]{1,0:T(8,128)(2,1)S(1)} %maximum_select_fusion.3), channel_id=1, source_target_pairs={{0,4},{1,5},{2,6},{3,7},{4,0},{5,1},{6,2},{7,3},{8,12},{9,13},{10,... | collective-permute-start | bytes 294920 | tf_op jit(solution)/shard_map/ppermute | solution.py:66
  206.8 10.7 %collective-permute-start.8 = (bf16[64,1536]{1,0:T(8,128)(2,1)S(1)}, bf16[64,1536]{1,0:T(8,128)(2,1)S(1)}, u32[]{:S(2)}, u32[]{:S(2)}) collective-permute-start(bf16[64,1536]{1,0:T(8,128)(2,1)S(1)} %maximum_select_fusion.2), channel_id=1, source_target_pairs={{0,2},{1,3},{2,0},{3,1},{4,6},{5,7},{6,4},{7,5},{8,10},{9,11},{10,... | collective-permute-start | bytes 589832 | tf_op jit(solution)/shard_map/ppermute | solution.py:66
  217.6 7.7 %collective-permute-start.9 = (bf16[128,1536]{1,0:T(8,128)(2,1)S(1)}, bf16[128,1536]{1,0:T(8,128)(2,1)S(1)}, u32[]{:S(2)}, u32[]{:S(2)}) collective-permute-start(bf16[128,1536]{1,0:T(8,128)(2,1)S(1)} %maximum_select_fusion.1), channel_id=1, source_target_pairs={{0,1},{1,0},{2,3},{3,2},{4,5},{5,4},{6,7},{7,6},{8,9},{9,8},{10,11... | collective-permute-start | bytes 1179656 | tf_op jit(solution)/shard_map/ppermute | solution.py:66

commit v11 on v8

--- a/solution.py
+++ b/solution.py
@@ -129,7 +129,7 @@
         exists[:, :, None] & (slot[:, :, None] == jnp.arange(owned, dtype=jnp.int32)[None, None, :])
     ).astype(jnp.bfloat16)
     far_back = lax.all_to_all(
-        jnp.take(pair_grads, far_pair, axis=0, mode="fill", fill_value=0),
+        jnp.take(pair_grads, far_pair, axis=0, mode="clip"),
         "tq", split_axis=0, concat_axis=0, tiled=True,
     )
     other = jnp.einsum(
@@ -140,7 +140,7 @@
     )
     other_back = lax.ppermute(other, "zh", swap)
     near_back = lax.all_to_all(
-        jnp.take(pair_grads, near_pair, axis=0, mode="fill", fill_value=0),
+        jnp.take(pair_grads, near_pair, axis=0, mode="clip"),
         "tq", split_axis=0, concat_axis=0, tiled=True,
     )
     mine = jnp.einsum(

time: 228 us -> 225 us (0.987)
  other arithmetic: 9.17 us -> 4.45 us
  waiting for transfers between devices: 64.9 us -> 67.3 us
    select_n x4 -> x0, other arithmetic: 4.7 us -> none  [the longest x2 2.37 us: local(): jnp.take(pair_grads, near_pair, axis=0, mode='fill', fill_value=0)]
    all_to_all x2, waiting for transfers between devices: 18.8 us -> 21.2 us  [the longest x1 21.2 us: local(): lax.all_to_all(jnp.take(pair_grads, far_pair, axis=0, mode='clip'), 'tq',...]
  transfers between devices with their start and end apart: 14 -> 14, of which waited for: 12 -> 12; matrix products, arithmetic and copies ran while one was open for 6% -> 5% of each run, Pallas kernels for 0% -> 0%
where the time goes in v11:
time: 225 us; the launch traced here: 224 us
  starting transfers between devices  124 us (55%)
  waiting for transfers between devices  67.3 us (30%)
  local copies, waits for them, and re-layouts  14 us (6%)
  matrix products  13.5 us (6%)
  other arithmetic  4.45 us (2%)
    ppermute x4, starting transfers between devices, head_sum(): lax.ppermute(send.astype(jnp.bfloat16), 'tensor', [(i, i ^ step) for i in...  25.2 us
    ppermute x4, starting transfers between devices, head_sum(): got = lax.ppermute(cur, 'tensor', [(i, i ^ step) for i in range(count)])  23.4 us
    ppermute x1, starting transfers between devices, local(): other_back = lax.ppermute(other, 'zh', swap)  23.4 us
    all_to_all x1, waiting for transfers between devices, local(): lax.all_to_all(jnp.take(pair_grads, far_pair, axis=0, mode='clip'), 'tq',...  21.2 us
    all_to_all x1, waiting for transfers between devices, local(): lax.all_to_all(mirror_spans[mirror_slot], 'tq', split_axis=0, concat_axis...  19.6 us
    ppermute x1, starting transfers between devices, local(): mirror_spans = lax.ppermute(paired_spans, 'zh', swap)  19.1 us
    ppermute x4, waiting for transfers between devices, head_sum(): lax.ppermute(send.astype(jnp.bfloat16), 'tensor', [(i, i ^ step) for i in...  12.5 us
    all_to_all x1, starting transfers between devices, local(): lax.all_to_all(paired_spans[own_slot], 'tq', split_axis=0, concat_axis=0,...  10.5 us
  transfers between devices with their start and end apart: 14, of which 12 were waited for; matrix products, arithmetic and copies ran while one was open for 5% of the time, Pallas kernels for 0%

profile of v11, /device:TPU:1, one launch (start us, length us, event | category | flops | bytes accessed | tf_op | source)
XLA Modules:
  0.0 224.2 jit_solution(1021356666749054161)
XLA Ops:
  6.7 10.5 %all-to-all-start = ((bf16[32,128,128]{2,1,0:T(8,128)(2,1)}), bf16[32,128,128]{2,1,0:T(8,128)(2,1)S(1)}, u32[]{:S(2)}, u32[]{:S(2)}) async-start(bf16[32,128,128]{2,1,0:T(8,128)(2,1)} %gather_fusion), calls=%async_computation | async-start | bytes 2097152 | tf_op jit(solution)/shard_map/all_to_all | solution.py:101
  17.2 19.1 %collective-permute-start = (bf16[2,128,128]{2,1,0:T(8,128)(2,1)S(1)}, bf16[2,128,128]{2,1,0:T(8,128)(2,1)S(1)}, u32[]{:S(2)}, u32[]{:S(2)}) collective-permute-start(bf16[2,128,128]{2,1,0:T(8,128)(2,1)S(1)} %bitcast_bitcast_fusion), channel_id=1, source_target_pairs={{0,16},{16,0},{1,17},{17,1},{2,18},{18,2},{3,19},{19,3},{4,20},{20... | collective-permute-start | bytes 196616 | tf_op jit(solution)/shard_map/ppermute | solution.py:92
  39.7 9.5 %all-to-all-start.1 = ((bf16[32,128,128]{2,1,0:T(8,128)(2,1)}), bf16[32,128,128]{2,1,0:T(8,128)(2,1)S(1)}, u32[]{:S(2)}, u32[]{:S(2)}) async-start(bf16[32,128,128]{2,1,0:T(8,128)(2,1)} %gather_fusion.2), calls=%async_computation.1 | async-start | bytes 2097152 | tf_op jit(solution)/shard_map/all_to_all | solution.py:102
  53.5 19.6 %all-to-all-done.1 = bf16[32,128,128]{2,1,0:T(8,128)(2,1)S(1)} async-done(((bf16[32,128,128]{2,1,0:T(8,128)(2,1)}), bf16[32,128,128]{2,1,0:T(8,128)(2,1)S(1)}, u32[]{:S(2)}, u32[]{:S(2)}) %all-to-all-start.1) | async-done | bytes 1048608 | tf_op jit(solution)/shard_map/all_to_all | solution.py:102
  82.1 6.7 %all-to-all-start.3 = ((bf16[32,128,128]{2,1,0:T(8,128)(2,1)}), bf16[32,128,128]{2,1,0:T(8,128)(2,1)}, u32[]{:S(2)}, u32[]{:S(2)}) async-start(bf16[32,128,128]{2,1,0:T(8,128)(2,1)} %gather_fusion.5), calls=%async_computation.3 | async-start | bytes 2097152 | tf_op jit(solution)/shard_map/all_to_all | solution.py:131
  91.2 21.2 %all-to-all-done.3 = bf16[32,128,128]{2,1,0:T(8,128)(2,1)} async-done(((bf16[32,128,128]{2,1,0:T(8,128)(2,1)}), bf16[32,128,128]{2,1,0:T(8,128)(2,1)}, u32[]{:S(2)}, u32[]{:S(2)}) %all-to-all-start.3) | async-done | bytes 1048608 | tf_op jit(solution)/shard_map/all_to_all | solution.py:131
  112.4 6.6 %all-to-all-start.2 = ((bf16[32,128,128]{2,1,0:T(8,128)(2,1)}), bf16[32,128,128]{2,1,0:T(8,128)(2,1)}, u32[]{:S(2)}, u32[]{:S(2)}) async-start(bf16[32,128,128]{2,1,0:T(8,128)(2,1)} %gather_fusion.4), calls=%async_computation.2 | async-start | bytes 2097152 | tf_op jit(solution)/shard_map/all_to_all | solution.py:142
  119.3 2.6 %fusion.10 = f32[2,128,128]{2,0,1:T(2,128)} fusion(bf16[32,128,128]{2,1,0:T(8,128)(2,1)} %all-to-all-done.3, pred[32,2,2]{0,2,1:T(4,128)(4,1)S(1)} %compare_and_fusion, s32[]{:T(128)S(6)} %select_n.257), kind=kOutput, calls=%fused_computation.33 | convolution fusion | flops 2097152 | bytes 1180164 | tf_op jit(solution)/shard_map/ck,crh->krh/dot_general | solution.py:135
  121.9 23.4 %collective-permute-start.1 = (f32[2,128,128]{2,0,1:T(2,128)}, f32[2,128,128]{2,0,1:T(2,128)}, u32[]{:S(2)}, u32[]{:S(2)}) collective-permute-start(f32[2,128,128]{2,0,1:T(2,128)} %fusion.10), channel_id=1, source_target_pairs={{0,16},{16,0},{1,17},{17,1},{2,18},{18,2},{3,19},{19,3},{4,20},{20... | collective-permute-start | bytes 393224 | tf_op jit(solution)/shard_map/ppermute | solution.py:141
  145.7 2.6 %collective-permute-done.1 = f32[2,128,128]{2,0,1:T(2,128)} collective-permute-done((f32[2,128,128]{2,0,1:T(2,128)}, f32[2,128,128]{2,0,1:T(2,128)}, u32[]{:S(2)}, u32[]{:S(2)}) %collective-permute-start.1) | collective-permute-done | bytes 131104 | tf_op jit(solution)/shard_map/ppermute | solution.py:141
  148.3 1.9 fusion.6
  151.5 5.3 %collective-permute-start.2 = (bf16[128,1536]{1,0:T(8,128)(2,1)S(1)}, bf16[128,1536]{1,0:T(8,128)(2,1)S(1)}, u32[]{:S(2)}, u32[]{:S(2)}) collective-permute-start(bf16[128,1536]{1,0:T(8,128)(2,1)S(1)} %select_convert_fusion), channel_id=1, source_target_pairs={{0,1},{1,0},{2,3},{3,2},{4,5},{5,4},{6,7},{7,6},{8,9},{9,8},{10,11... | collective-permute-start | bytes 1179656 | tf_op jit(solution)/shard_map/ppermute | solution.py:59
  158.3 9.8 %collective-permute-start.3 = (bf16[64,1536]{1,0:T(8,128)(2,1)S(1)}, bf16[64,1536]{1,0:T(8,128)(2,1)S(1)}, u32[]{:S(2)}, u32[]{:S(2)}) collective-permute-start(bf16[64,1536]{1,0:T(8,128)(2,1)S(1)} %select_convert_fusion.1), channel_id=1, source_target_pairs={{0,2},{1,3},{2,0},{3,1},{4,6},{5,7},{6,4},{7,5},{8,10},{9,11},{10,... | collective-permute-start | bytes 589832 | tf_op jit(solution)/shard_map/ppermute | solution.py:59
  168.1 4.9 %collective-permute-done.3 = bf16[64,1536]{1,0:T(8,128)(2,1)S(1)} collective-permute-done((bf16[64,1536]{1,0:T(8,128)(2,1)S(1)}, bf16[64,1536]{1,0:T(8,128)(2,1)S(1)}, u32[]{:S(2)}, u32[]{:S(2)}) %collective-permute-start.3) | collective-permute-done | bytes 196640 | tf_op jit(solution)/shard_map/ppermute | solution.py:59
  173.1 3.2 %collective-permute-start.4 = (bf16[32,1536]{1,0:T(8,128)(2,1)S(1)}, bf16[32,1536]{1,0:T(8,128)(2,1)S(1)}, u32[]{:S(2)}, u32[]{:S(2)}) collective-permute-start(bf16[32,1536]{1,0:T(8,128)(2,1)S(1)} %select_convert_fusion.2), channel_id=1, source_target_pairs={{0,4},{1,5},{2,6},{3,7},{4,0},{5,1},{6,2},{7,3},{8,12},{9,13},{10,... | collective-permute-start | bytes 294920 | tf_op jit(solution)/shard_map/ppermute | solution.py:59
  176.3 4.5 %collective-permute-done.4 = bf16[32,1536]{1,0:T(8,128)(2,1)S(1)} collective-permute-done((bf16[32,1536]{1,0:T(8,128)(2,1)S(1)}, bf16[32,1536]{1,0:T(8,128)(2,1)S(1)}, u32[]{:S(2)}, u32[]{:S(2)}) %collective-permute-start.4) | collective-permute-done | bytes 98336 | tf_op jit(solution)/shard_map/ppermute | solution.py:59
  180.8 7.0 %collective-permute-start.5 = (bf16[16,1536]{1,0:T(8,128)(2,1)S(1)}, bf16[16,1536]{1,0:T(8,128)(2,1)S(1)}, u32[]{:S(2)}, u32[]{:S(2)}) collective-permute-start(bf16[16,1536]{1,0:T(8,128)(2,1)S(1)} %select_convert_fusion.3), channel_id=1, source_target_pairs={{0,8},{1,9},{2,10},{3,11},{4,12},{5,13},{6,14},{7,15},{8,0},{9,1},... | collective-permute-start | bytes 147464 | tf_op jit(solution)/shard_map/ppermute | solution.py:59
  189.6 7.0 %collective-permute-start.6 = (bf16[16,1536]{1,0:T(8,128)(2,1)S(1)}, bf16[16,1536]{1,0:T(8,128)(2,1)S(1)}, u32[]{:S(2)}, u32[]{:S(2)}) collective-permute-start(bf16[16,1536]{1,0:T(8,128)(2,1)S(1)} %add_convert_fusion), channel_id=1, source_target_pairs={{0,8},{1,9},{2,10},{3,11},{4,12},{5,13},{6,14},{7,15},{8,0},{9,1},... | collective-permute-start | bytes 147464 | tf_op jit(solution)/shard_map/ppermute | solution.py:66
  196.5 1.8 collective-permute-done.6
  198.3 2.7 %collective-permute-start.7 = (bf16[32,1536]{1,0:T(8,128)(2,1)S(1)}, bf16[32,1536]{1,0:T(8,128)(2,1)S(1)}, u32[]{:S(2)}, u32[]{:S(2)}) collective-permute-start(bf16[32,1536]{1,0:T(8,128)(2,1)S(1)} %maximum_select_fusion.3), channel_id=1, source_target_pairs={{0,4},{1,5},{2,6},{3,7},{4,0},{5,1},{6,2},{7,3},{8,12},{9,13},{10,... | collective-permute-start | bytes 294920 | tf_op jit(solution)/shard_map/ppermute | solution.py:66
  201.1 3.5 %collective-permute-done.7 = bf16[32,1536]{1,0:T(8,128)(2,1)S(1)} collective-permute-done((bf16[32,1536]{1,0:T(8,128)(2,1)S(1)}, bf16[32,1536]{1,0:T(8,128)(2,1)S(1)}, u32[]{:S(2)}, u32[]{:S(2)}) %collective-permute-start.7) | collective-permute-done | bytes 98336 | tf_op jit(solution)/shard_map/ppermute | solution.py:66
  204.6 7.4 %collective-permute-start.8 = (bf16[64,1536]{1,0:T(8,128)(2,1)S(1)}, bf16[64,1536]{1,0:T(8,128)(2,1)S(1)}, u32[]{:S(2)}, u32[]{:S(2)}) collective-permute-start(bf16[64,1536]{1,0:T(8,128)(2,1)S(1)} %maximum_select_fusion.2), channel_id=1, source_target_pairs={{0,2},{1,3},{2,0},{3,1},{4,6},{5,7},{6,4},{7,5},{8,10},{9,11},{10,... | collective-permute-start | bytes 589832 | tf_op jit(solution)/shard_map/ppermute | solution.py:66
  212.1 3.0 %collective-permute-done.8 = bf16[64,1536]{1,0:T(8,128)(2,1)S(1)} collective-permute-done((bf16[64,1536]{1,0:T(8,128)(2,1)S(1)}, bf16[64,1536]{1,0:T(8,128)(2,1)S(1)}, u32[]{:S(2)}, u32[]{:S(2)}) %collective-permute-start.8) | collective-permute-done | bytes 196640 | tf_op jit(solution)/shard_map/ppermute | solution.py:66
  215.2 6.3 %collective-permute-start.9 = (bf16[128,1536]{1,0:T(8,128)(2,1)S(1)}, bf16[128,1536]{1,0:T(8,128)(2,1)S(1)}, u32[]{:S(2)}, u32[]{:S(2)}) collective-permute-start(bf16[128,1536]{1,0:T(8,128)(2,1)S(1)} %maximum_select_fusion.1), channel_id=1, source_target_pairs={{0,1},{1,0},{2,3},{3,2},{4,5},{5,4},{6,7},{7,6},{8,9},{9,8},{10,11... | collective-permute-start | bytes 1179656 | tf_op jit(solution)/shard_map/ppermute | solution.py:66
  (80 shorter events, 33.6 us)
Async XLA Ops:
  0.0 1.1 copy-start
  6.7 33.1 %all-to-all-start = ((bf16[32,128,128]{2,1,0:T(8,128)(2,1)}), bf16[32,128,128]{2,1,0:T(8,128)(2,1)S(1)}, u32[]{:S(2)}, u32[]{:S(2)}) async-start(bf16[32,128,128]{2,1,0:T(8,128)(2,1)} %gather_fusion), calls=%async_computation | async-start | bytes 2097152 | tf_op jit(solution)/shard_map/all_to_all | solution.py:101
  17.2 20.9 %collective-permute-start = (bf16[2,128,128]{2,1,0:T(8,128)(2,1)S(1)}, bf16[2,128,128]{2,1,0:T(8,128)(2,1)S(1)}, u32[]{:S(2)}, u32[]{:S(2)}) collective-permute-start(bf16[2,128,128]{2,1,0:T(8,128)(2,1)S(1)} %bitcast_bitcast_fusion), channel_id=1, source_target_pairs={{0,16},{16,0},{1,17},{17,1},{2,18},{18,2},{3,19},{19,3},{4,20},{20... | collective-permute-start | bytes 196616 | tf_op jit(solution)/shard_map/ppermute | solution.py:92
  36.3 13.0 %copy-start.6 = (bf16[64,1536]{1,0:T(8,128)(2,1)S(1)}, bf16[64,1536]{1,0:T(8,128)(2,1)}, u32[]{:S(2)}) copy-start(bf16[64,1536]{1,0:T(8,128)(2,1)} %param.12) | copy-start | bytes 589828
  39.7 11.0 %copy-start.5 = (bf16[1536,64]{0,1:T(8,128)(2,1)S(1)}, bf16[1536,64]{0,1:T(8,128)(2,1)}, u32[]{:S(2)}) copy-start(bf16[1536,64]{0,1:T(8,128)(2,1)} %param.9) | copy-start | bytes 589828
  39.7 33.4 %all-to-all-start.1 = ((bf16[32,128,128]{2,1,0:T(8,128)(2,1)}), bf16[32,128,128]{2,1,0:T(8,128)(2,1)S(1)}, u32[]{:S(2)}, u32[]{:S(2)}) async-start(bf16[32,128,128]{2,1,0:T(8,128)(2,1)} %gather_fusion.2), calls=%async_computation.1 | async-start | bytes 2097152 | tf_op jit(solution)/shard_map/all_to_all | solution.py:102
  79.4 1.0 copy-start.1
  82.1 30.3 %all-to-all-start.3 = ((bf16[32,128,128]{2,1,0:T(8,128)(2,1)}), bf16[32,128,128]{2,1,0:T(8,128)(2,1)}, u32[]{:S(2)}, u32[]{:S(2)}) async-start(bf16[32,128,128]{2,1,0:T(8,128)(2,1)} %gather_fusion.5), calls=%async_computation.3 | async-start | bytes 2097152 | tf_op jit(solution)/shard_map/all_to_all | solution.py:131
  91.2 54.1 %copy-start.2 = (bf16[2,128,16,128]{1,3,2,0:T(8,128)(2,1)S(1)}, bf16[2,128,16,128]{1,3,2,0:T(8,128)(2,1)}, u32[]{:S(2)}) copy-start(bf16[2,128,16,128]{1,3,2,0:T(8,128)(2,1)} %copy-done.1) | copy-start | bytes 3145732
  112.4 33.3 %all-to-all-start.2 = ((bf16[32,128,128]{2,1,0:T(8,128)(2,1)}), bf16[32,128,128]{2,1,0:T(8,128)(2,1)}, u32[]{:S(2)}, u32[]{:S(2)}) async-start(bf16[32,128,128]{2,1,0:T(8,128)(2,1)} %gather_fusion.4), calls=%async_computation.2 | async-start | bytes 2097152 | tf_op jit(solution)/shard_map/all_to_all | solution.py:142
  119.3 30.9 %copy-start.3 = (bf16[1536,64]{0,1:T(8,128)(2,1)S(1)}, bf16[1536,64]{0,1:T(8,128)(2,1)}, u32[]{:S(2)}) copy-start(bf16[1536,64]{0,1:T(8,128)(2,1)} %param.10) | copy-start | bytes 589828
  121.9 28.7 %copy-start.4 = (bf16[1536,64]{0,1:T(8,128)(2,1)S(1)}, bf16[1536,64]{0,1:T(8,128)(2,1)}, u32[]{:S(2)}) copy-start(bf16[1536,64]{0,1:T(8,128)(2,1)} %param.11) | copy-start | bytes 589828
  121.9 26.4 %collective-permute-start.1 = (f32[2,128,128]{2,0,1:T(2,128)}, f32[2,128,128]{2,0,1:T(2,128)}, u32[]{:S(2)}, u32[]{:S(2)}) collective-permute-start(f32[2,128,128]{2,0,1:T(2,128)} %fusion.10), channel_id=1, source_target_pairs={{0,16},{16,0},{1,17},{17,1},{2,18},{18,2},{3,19},{19,3},{4,20},{20... | collective-permute-start | bytes 393224 | tf_op jit(solution)/shard_map/ppermute | solution.py:141
  151.5 6.7 %collective-permute-start.2 = (bf16[128,1536]{1,0:T(8,128)(2,1)S(1)}, bf16[128,1536]{1,0:T(8,128)(2,1)S(1)}, u32[]{:S(2)}, u32[]{:S(2)}) collective-permute-start(bf16[128,1536]{1,0:T(8,128)(2,1)S(1)} %select_convert_fusion), channel_id=1, source_target_pairs={{0,1},{1,0},{2,3},{3,2},{4,5},{5,4},{6,7},{7,6},{8,9},{9,8},{10,11... | collective-permute-start | bytes 1179656 | tf_op jit(solution)/shard_map/ppermute | solution.py:59
  158.3 14.7 %collective-permute-start.3 = (bf16[64,1536]{1,0:T(8,128)(2,1)S(1)}, bf16[64,1536]{1,0:T(8,128)(2,1)S(1)}, u32[]{:S(2)}, u32[]{:S(2)}) collective-permute-start(bf16[64,1536]{1,0:T(8,128)(2,1)S(1)} %select_convert_fusion.1), channel_id=1, source_target_pairs={{0,2},{1,3},{2,0},{3,1},{4,6},{5,7},{6,4},{7,5},{8,10},{9,11},{10,... | collective-permute-start | bytes 589832 | tf_op jit(solution)/shard_map/ppermute | solution.py:59
  173.1 7.7 %collective-permute-start.4 = (bf16[32,1536]{1,0:T(8,128)(2,1)S(1)}, bf16[32,1536]{1,0:T(8,128)(2,1)S(1)}, u32[]{:S(2)}, u32[]{:S(2)}) collective-permute-start(bf16[32,1536]{1,0:T(8,128)(2,1)S(1)} %select_convert_fusion.2), channel_id=1, source_target_pairs={{0,4},{1,5},{2,6},{3,7},{4,0},{5,1},{6,2},{7,3},{8,12},{9,13},{10,... | collective-permute-start | bytes 294920 | tf_op jit(solution)/shard_map/ppermute | solution.py:59
  180.8 8.8 %collective-permute-start.5 = (bf16[16,1536]{1,0:T(8,128)(2,1)S(1)}, bf16[16,1536]{1,0:T(8,128)(2,1)S(1)}, u32[]{:S(2)}, u32[]{:S(2)}) collective-permute-start(bf16[16,1536]{1,0:T(8,128)(2,1)S(1)} %select_convert_fusion.3), channel_id=1, source_target_pairs={{0,8},{1,9},{2,10},{3,11},{4,12},{5,13},{6,14},{7,15},{8,0},{9,1},... | collective-permute-start | bytes 147464 | tf_op jit(solution)/shard_map/ppermute | solution.py:59
  189.6 8.8 %collective-permute-start.6 = (bf16[16,1536]{1,0:T(8,128)(2,1)S(1)}, bf16[16,1536]{1,0:T(8,128)(2,1)S(1)}, u32[]{:S(2)}, u32[]{:S(2)}) collective-permute-start(bf16[16,1536]{1,0:T(8,128)(2,1)S(1)} %add_convert_fusion), channel_id=1, source_target_pairs={{0,8},{1,9},{2,10},{3,11},{4,12},{5,13},{6,14},{7,15},{8,0},{9,1},... | collective-permute-start | bytes 147464 | tf_op jit(solution)/shard_map/ppermute | solution.py:66
  198.3 6.3 %collective-permute-start.7 = (bf16[32,1536]{1,0:T(8,128)(2,1)S(1)}, bf16[32,1536]{1,0:T(8,128)(2,1)S(1)}, u32[]{:S(2)}, u32[]{:S(2)}) collective-permute-start(bf16[32,1536]{1,0:T(8,128)(2,1)S(1)} %maximum_select_fusion.3), channel_id=1, source_target_pairs={{0,4},{1,5},{2,6},{3,7},{4,0},{5,1},{6,2},{7,3},{8,12},{9,13},{10,... | collective-permute-start | bytes 294920 | tf_op jit(solution)/shard_map/ppermute | solution.py:66
  204.6 10.5 %collective-permute-start.8 = (bf16[64,1536]{1,0:T(8,128)(2,1)S(1)}, bf16[64,1536]{1,0:T(8,128)(2,1)S(1)}, u32[]{:S(2)}, u32[]{:S(2)}) collective-permute-start(bf16[64,1536]{1,0:T(8,128)(2,1)S(1)} %maximum_select_fusion.2), channel_id=1, source_target_pairs={{0,2},{1,3},{2,0},{3,1},{4,6},{5,7},{6,4},{7,5},{8,10},{9,11},{10,... | collective-permute-start | bytes 589832 | tf_op jit(solution)/shard_map/ppermute | solution.py:66
  215.2 7.7 %collective-permute-start.9 = (bf16[128,1536]{1,0:T(8,128)(2,1)S(1)}, bf16[128,1536]{1,0:T(8,128)(2,1)S(1)}, u32[]{:S(2)}, u32[]{:S(2)}) collective-permute-start(bf16[128,1536]{1,0:T(8,128)(2,1)S(1)} %maximum_select_fusion.1), channel_id=1, source_target_pairs={{0,1},{1,0},{2,3},{3,2},{4,5},{5,4},{6,7},{7,6},{8,9},{9,8},{10,11... | collective-permute-start | bytes 1179656 | tf_op jit(solution)/shard_map/ppermute | solution.py:66

commit v12 on v11

--- a/solution.py
+++ b/solution.py
@@ -23,14 +23,13 @@
         jnp.einsum("chqjk,cjhdk->chdq", dscores_b, key_t, preferred_element_type=jnp.float32)
         * scaling
     ).astype(jnp.bfloat16)
-    grad_key = (
-        jnp.einsum("chqjk,chdq->cjhdk", dscores_b, query_t, preferred_element_type=jnp.float32)
-        * scaling
+    grad_pair = jnp.einsum(
+        "gchqjk,gchdq->cjghdk",
+        jnp.stack([dscores_b, probs_b]),
+        jnp.stack([query_t * scaling, dout_t]),
+        preferred_element_type=jnp.float32,
     ).astype(jnp.bfloat16)
-    grad_value = jnp.einsum(
-        "chqjk,chdq->cjhdk", probs_b, dout_t, preferred_element_type=jnp.float32
-    ).astype(jnp.bfloat16)
-    return (grad_query, grad_key, grad_value)
+    return (grad_query, grad_pair)
 
 
 def project_back(grads_t, weight):
@@ -108,18 +107,12 @@
     fetched = fetched.reshape(owned, per_reader, 2, head_count, HD, SPAN)
     query_rows = jnp.transpose(queries_t.reshape(head_count, HD, owned, SPAN), (2, 0, 1, 3))
     dout_rows = jnp.transpose(dout_t.reshape(head_count, HD, owned, SPAN), (2, 0, 1, 3))
-    grad_query, grad_key, grad_value = attend_grad(
+    grad_query, grad_pair = attend_grad(
         query_rows, fetched[:, :, 0], fetched[:, :, 1], dout_rows
     )
     grad_query_t = jnp.transpose(grad_query, (1, 2, 0, 3)).reshape(col_count, row_count)
     query_term = project_back(grad_query_t, w_query)
-    pair_grads = jnp.concatenate(
-        [
-            grad_key.reshape(owned * per_reader, col_count, SPAN),
-            grad_value.reshape(owned * per_reader, col_count, SPAN),
-        ],
-        axis=1,
-    )
+    pair_grads = grad_pair.reshape(owned * per_reader, 2 * col_count, SPAN)
     pair_count = owned * per_reader
     pair_index = jnp.arange(pair_count, dtype=jnp.int32)
     unused = jnp.full((column_count,), pair_count, jnp.int32)

time: 225 us -> 225 us (level)
  transfers between devices with their start and end apart: 14 -> 14, of which waited for: 12 -> 12; matrix products, arithmetic and copies ran while one was open for 5% -> 6% of each run, Pallas kernels for 0% -> 0%
where the time goes in v12:
time: 225 us; the launch traced here: 223 us
  starting transfers between devices  124 us (55%)
  waiting for transfers between devices  66 us (29%)
  matrix products  14.1 us (6%)
  local copies, waits for them, and re-layouts  13.6 us (6%)
  other arithmetic  4.81 us (2%)
    ppermute x4, starting transfers between devices, head_sum(): lax.ppermute(send.astype(jnp.bfloat16), 'tensor', [(i, i ^ step) for i in...  25.2 us
    ppermute x4, starting transfers between devices, head_sum(): got = lax.ppermute(cur, 'tensor', [(i, i ^ step) for i in range(count)])  23.5 us
    ppermute x1, starting transfers between devices, local(): other_back = lax.ppermute(other, 'zh', swap)  23.4 us
    all_to_all x1, waiting for transfers between devices, local(): lax.all_to_all(jnp.take(pair_grads, far_pair, axis=0, mode='clip'), 'tq',...  21.2 us
    all_to_all x1, waiting for transfers between devices, local(): lax.all_to_all(mirror_spans[mirror_slot], 'tq', split_axis=0, concat_axis...  19.5 us
    ppermute x1, starting transfers between devices, local(): mirror_spans = lax.ppermute(paired_spans, 'zh', swap)  19.1 us
    ppermute x4, waiting for transfers between devices, head_sum(): lax.ppermute(send.astype(jnp.bfloat16), 'tensor', [(i, i ^ step) for i in...  12.5 us
    all_to_all x1, starting transfers between devices, local(): lax.all_to_all(paired_spans[own_slot], 'tq', split_axis=0, concat_axis=0,...  10.5 us
  transfers between devices with their start and end apart: 14, of which 12 were waited for; matrix products, arithmetic and copies ran while one was open for 6% of the time, Pallas kernels for 0%

profile of v12, /device:TPU:1, one launch (start us, length us, event | category | flops | bytes accessed | tf_op | source)
XLA Modules:
  0.0 223.5 jit_solution(4729353725806517597)
XLA Ops:
  6.7 10.5 %all-to-all-start = ((bf16[32,128,128]{2,1,0:T(8,128)(2,1)}), bf16[32,128,128]{2,1,0:T(8,128)(2,1)S(1)}, u32[]{:S(2)}, u32[]{:S(2)}) async-start(bf16[32,128,128]{2,1,0:T(8,128)(2,1)} %gather_fusion), calls=%async_computation | async-start | bytes 2097152 | tf_op jit(solution)/shard_map/all_to_all | solution.py:100
  17.2 19.1 %collective-permute-start = (bf16[2,128,128]{2,1,0:T(8,128)(2,1)S(1)}, bf16[2,128,128]{2,1,0:T(8,128)(2,1)S(1)}, u32[]{:S(2)}, u32[]{:S(2)}) collective-permute-start(bf16[2,128,128]{2,1,0:T(8,128)(2,1)S(1)} %bitcast_bitcast_fusion), channel_id=1, source_target_pairs={{0,16},{16,0},{1,17},{17,1},{2,18},{18,2},{3,19},{19,3},{4,20},{20... | collective-permute-start | bytes 196616 | tf_op jit(solution)/shard_map/ppermute | solution.py:91
  36.3 1.8 collective-permute-done
  39.7 9.5 %all-to-all-start.1 = ((bf16[32,128,128]{2,1,0:T(8,128)(2,1)}), bf16[32,128,128]{2,1,0:T(8,128)(2,1)S(1)}, u32[]{:S(2)}, u32[]{:S(2)}) async-start(bf16[32,128,128]{2,1,0:T(8,128)(2,1)} %gather_fusion.2), calls=%async_computation.1 | async-start | bytes 2097152 | tf_op jit(solution)/shard_map/all_to_all | solution.py:101
  53.5 19.5 %all-to-all-done.1 = bf16[32,128,128]{2,1,0:T(8,128)(2,1)S(1)} async-done(((bf16[32,128,128]{2,1,0:T(8,128)(2,1)}), bf16[32,128,128]{2,1,0:T(8,128)(2,1)S(1)}, u32[]{:S(2)}, u32[]{:S(2)}) %all-to-all-start.1) | async-done | bytes 1048608 | tf_op jit(solution)/shard_map/all_to_all | solution.py:101
  81.9 6.7 %all-to-all-start.3 = ((bf16[32,128,128]{2,1,0:T(8,128)(2,1)}), bf16[32,128,128]{2,1,0:T(8,128)(2,1)}, u32[]{:S(2)}, u32[]{:S(2)}) async-start(bf16[32,128,128]{2,1,0:T(8,128)(2,1)} %gather_fusion.5), calls=%async_computation.3 | async-start | bytes 2097152 | tf_op jit(solution)/shard_map/all_to_all | solution.py:124
  91.0 21.2 %all-to-all-done.3 = bf16[32,128,128]{2,1,0:T(8,128)(2,1)} async-done(((bf16[32,128,128]{2,1,0:T(8,128)(2,1)}), bf16[32,128,128]{2,1,0:T(8,128)(2,1)}, u32[]{:S(2)}, u32[]{:S(2)}) %all-to-all-start.3) | async-done | bytes 1048608 | tf_op jit(solution)/shard_map/all_to_all | solution.py:124
  112.2 6.5 %all-to-all-start.2 = ((bf16[32,128,128]{2,1,0:T(8,128)(2,1)}), bf16[32,128,128]{2,1,0:T(8,128)(2,1)S(1)}, u32[]{:S(2)}, u32[]{:S(2)}) async-start(bf16[32,128,128]{2,1,0:T(8,128)(2,1)} %gather_fusion.4), calls=%async_computation.2 | async-start | bytes 2097152 | tf_op jit(solution)/shard_map/all_to_all | solution.py:135
  118.9 2.6 %fusion.17 = f32[2,128,128]{2,0,1:T(2,128)} fusion(bf16[32,128,128]{2,1,0:T(8,128)(2,1)} %all-to-all-done.3, pred[32,2,2]{0,2,1:T(4,128)(4,1)S(1)} %compare_and_fusion, s32[]{:T(128)S(6)} %select_n.257), kind=kOutput, calls=%fused_computation.34 | convolution fusion | flops 2097152 | bytes 1180164 | tf_op jit(solution)/shard_map/ck,crh->krh/dot_general | solution.py:128
  121.5 23.4 %collective-permute-start.1 = (f32[2,128,128]{2,0,1:T(2,128)}, f32[2,128,128]{2,0,1:T(2,128)}, u32[]{:S(2)}, u32[]{:S(2)}) collective-permute-start(f32[2,128,128]{2,0,1:T(2,128)} %fusion.17), channel_id=1, source_target_pairs={{0,16},{16,0},{1,17},{17,1},{2,18},{18,2},{3,19},{19,3},{4,20},{20... | collective-permute-start | bytes 393224 | tf_op jit(solution)/shard_map/ppermute | solution.py:134
  150.8 5.3 %collective-permute-start.2 = (bf16[128,1536]{1,0:T(8,128)(2,1)S(1)}, bf16[128,1536]{1,0:T(8,128)(2,1)S(1)}, u32[]{:S(2)}, u32[]{:S(2)}) collective-permute-start(bf16[128,1536]{1,0:T(8,128)(2,1)S(1)} %select_convert_fusion), channel_id=1, source_target_pairs={{0,1},{1,0},{2,3},{3,2},{4,5},{5,4},{6,7},{7,6},{8,9},{9,8},{10,11... | collective-permute-start | bytes 1179656 | tf_op jit(solution)/shard_map/ppermute | solution.py:58
  157.6 9.8 %collective-permute-start.3 = (bf16[64,1536]{1,0:T(8,128)(2,1)S(1)}, bf16[64,1536]{1,0:T(8,128)(2,1)S(1)}, u32[]{:S(2)}, u32[]{:S(2)}) collective-permute-start(bf16[64,1536]{1,0:T(8,128)(2,1)S(1)} %select_convert_fusion.1), channel_id=1, source_target_pairs={{0,2},{1,3},{2,0},{3,1},{4,6},{5,7},{6,4},{7,5},{8,10},{9,11},{10,... | collective-permute-start | bytes 589832 | tf_op jit(solution)/shard_map/ppermute | solution.py:58
  167.4 4.9 %collective-permute-done.3 = bf16[64,1536]{1,0:T(8,128)(2,1)S(1)} collective-permute-done((bf16[64,1536]{1,0:T(8,128)(2,1)S(1)}, bf16[64,1536]{1,0:T(8,128)(2,1)S(1)}, u32[]{:S(2)}, u32[]{:S(2)}) %collective-permute-start.3) | collective-permute-done | bytes 196640 | tf_op jit(solution)/shard_map/ppermute | solution.py:58
  172.3 3.2 %collective-permute-start.4 = (bf16[32,1536]{1,0:T(8,128)(2,1)S(1)}, bf16[32,1536]{1,0:T(8,128)(2,1)S(1)}, u32[]{:S(2)}, u32[]{:S(2)}) collective-permute-start(bf16[32,1536]{1,0:T(8,128)(2,1)S(1)} %select_convert_fusion.2), channel_id=1, source_target_pairs={{0,4},{1,5},{2,6},{3,7},{4,0},{5,1},{6,2},{7,3},{8,12},{9,13},{10,... | collective-permute-start | bytes 294920 | tf_op jit(solution)/shard_map/ppermute | solution.py:58
  175.5 4.5 %collective-permute-done.4 = bf16[32,1536]{1,0:T(8,128)(2,1)S(1)} collective-permute-done((bf16[32,1536]{1,0:T(8,128)(2,1)S(1)}, bf16[32,1536]{1,0:T(8,128)(2,1)S(1)}, u32[]{:S(2)}, u32[]{:S(2)}) %collective-permute-start.4) | collective-permute-done | bytes 98336 | tf_op jit(solution)/shard_map/ppermute | solution.py:58
  180.1 7.0 %collective-permute-start.5 = (bf16[16,1536]{1,0:T(8,128)(2,1)S(1)}, bf16[16,1536]{1,0:T(8,128)(2,1)S(1)}, u32[]{:S(2)}, u32[]{:S(2)}) collective-permute-start(bf16[16,1536]{1,0:T(8,128)(2,1)S(1)} %select_convert_fusion.3), channel_id=1, source_target_pairs={{0,8},{1,9},{2,10},{3,11},{4,12},{5,13},{6,14},{7,15},{8,0},{9,1},... | collective-permute-start | bytes 147464 | tf_op jit(solution)/shard_map/ppermute | solution.py:58
  187.1 1.8 collective-permute-done.5
  188.8 7.0 %collective-permute-start.6 = (bf16[16,1536]{1,0:T(8,128)(2,1)S(1)}, bf16[16,1536]{1,0:T(8,128)(2,1)S(1)}, u32[]{:S(2)}, u32[]{:S(2)}) collective-permute-start(bf16[16,1536]{1,0:T(8,128)(2,1)S(1)} %add_convert_fusion), channel_id=1, source_target_pairs={{0,8},{1,9},{2,10},{3,11},{4,12},{5,13},{6,14},{7,15},{8,0},{9,1},... | collective-permute-start | bytes 147464 | tf_op jit(solution)/shard_map/ppermute | solution.py:65
  195.8 1.8 collective-permute-done.6
  197.6 2.7 %collective-permute-start.7 = (bf16[32,1536]{1,0:T(8,128)(2,1)S(1)}, bf16[32,1536]{1,0:T(8,128)(2,1)S(1)}, u32[]{:S(2)}, u32[]{:S(2)}) collective-permute-start(bf16[32,1536]{1,0:T(8,128)(2,1)S(1)} %maximum_select_fusion.3), channel_id=1, source_target_pairs={{0,4},{1,5},{2,6},{3,7},{4,0},{5,1},{6,2},{7,3},{8,12},{9,13},{10,... | collective-permute-start | bytes 294920 | tf_op jit(solution)/shard_map/ppermute | solution.py:65
  200.3 3.5 %collective-permute-done.7 = bf16[32,1536]{1,0:T(8,128)(2,1)S(1)} collective-permute-done((bf16[32,1536]{1,0:T(8,128)(2,1)S(1)}, bf16[32,1536]{1,0:T(8,128)(2,1)S(1)}, u32[]{:S(2)}, u32[]{:S(2)}) %collective-permute-start.7) | collective-permute-done | bytes 98336 | tf_op jit(solution)/shard_map/ppermute | solution.py:65
  203.9 7.4 %collective-permute-start.8 = (bf16[64,1536]{1,0:T(8,128)(2,1)S(1)}, bf16[64,1536]{1,0:T(8,128)(2,1)S(1)}, u32[]{:S(2)}, u32[]{:S(2)}) collective-permute-start(bf16[64,1536]{1,0:T(8,128)(2,1)S(1)} %maximum_select_fusion.2), channel_id=1, source_target_pairs={{0,2},{1,3},{2,0},{3,1},{4,6},{5,7},{6,4},{7,5},{8,10},{9,11},{10,... | collective-permute-start | bytes 589832 | tf_op jit(solution)/shard_map/ppermute | solution.py:65
  211.3 3.0 %collective-permute-done.8 = bf16[64,1536]{1,0:T(8,128)(2,1)S(1)} collective-permute-done((bf16[64,1536]{1,0:T(8,128)(2,1)S(1)}, bf16[64,1536]{1,0:T(8,128)(2,1)S(1)}, u32[]{:S(2)}, u32[]{:S(2)}) %collective-permute-start.8) | collective-permute-done | bytes 196640 | tf_op jit(solution)/shard_map/ppermute | solution.py:65
  214.5 6.4 %collective-permute-start.9 = (bf16[128,1536]{1,0:T(8,128)(2,1)S(1)}, bf16[128,1536]{1,0:T(8,128)(2,1)S(1)}, u32[]{:S(2)}, u32[]{:S(2)}) collective-permute-start(bf16[128,1536]{1,0:T(8,128)(2,1)S(1)} %maximum_select_fusion.1), channel_id=1, source_target_pairs={{0,1},{1,0},{2,3},{3,2},{4,5},{5,4},{6,7},{7,6},{8,9},{9,8},{10,11... | collective-permute-start | bytes 1179656 | tf_op jit(solution)/shard_map/ppermute | solution.py:65
  (80 shorter events, 34.0 us)
Async XLA Ops:
  0.0 1.1 copy-start
  6.7 33.1 %all-to-all-start = ((bf16[32,128,128]{2,1,0:T(8,128)(2,1)}), bf16[32,128,128]{2,1,0:T(8,128)(2,1)S(1)}, u32[]{:S(2)}, u32[]{:S(2)}) async-start(bf16[32,128,128]{2,1,0:T(8,128)(2,1)} %gather_fusion), calls=%async_computation | async-start | bytes 2097152 | tf_op jit(solution)/shard_map/all_to_all | solution.py:100
  17.2 20.9 %collective-permute-start = (bf16[2,128,128]{2,1,0:T(8,128)(2,1)S(1)}, bf16[2,128,128]{2,1,0:T(8,128)(2,1)S(1)}, u32[]{:S(2)}, u32[]{:S(2)}) collective-permute-start(bf16[2,128,128]{2,1,0:T(8,128)(2,1)S(1)} %bitcast_bitcast_fusion), channel_id=1, source_target_pairs={{0,16},{16,0},{1,17},{17,1},{2,18},{18,2},{3,19},{19,3},{4,20},{20... | collective-permute-start | bytes 196616 | tf_op jit(solution)/shard_map/ppermute | solution.py:91
  36.3 13.0 %copy-start.5 = (bf16[64,1536]{1,0:T(8,128)(2,1)S(1)}, bf16[64,1536]{1,0:T(8,128)(2,1)}, u32[]{:S(2)}) copy-start(bf16[64,1536]{1,0:T(8,128)(2,1)} %param.12) | copy-start | bytes 589828
  39.7 11.1 %copy-start.4 = (bf16[1536,64]{0,1:T(8,128)(2,1)S(1)}, bf16[1536,64]{0,1:T(8,128)(2,1)}, u32[]{:S(2)}) copy-start(bf16[1536,64]{0,1:T(8,128)(2,1)} %param.9) | copy-start | bytes 589828
  39.7 33.4 %all-to-all-start.1 = ((bf16[32,128,128]{2,1,0:T(8,128)(2,1)}), bf16[32,128,128]{2,1,0:T(8,128)(2,1)S(1)}, u32[]{:S(2)}, u32[]{:S(2)}) async-start(bf16[32,128,128]{2,1,0:T(8,128)(2,1)} %gather_fusion.2), calls=%async_computation.1 | async-start | bytes 2097152 | tf_op jit(solution)/shard_map/all_to_all | solution.py:101
  79.2 1.0 copy-start.1
  81.9 30.3 %all-to-all-start.3 = ((bf16[32,128,128]{2,1,0:T(8,128)(2,1)}), bf16[32,128,128]{2,1,0:T(8,128)(2,1)}, u32[]{:S(2)}, u32[]{:S(2)}) async-start(bf16[32,128,128]{2,1,0:T(8,128)(2,1)} %gather_fusion.5), calls=%async_computation.3 | async-start | bytes 2097152 | tf_op jit(solution)/shard_map/all_to_all | solution.py:124
  112.2 34.3 %all-to-all-start.2 = ((bf16[32,128,128]{2,1,0:T(8,128)(2,1)}), bf16[32,128,128]{2,1,0:T(8,128)(2,1)S(1)}, u32[]{:S(2)}, u32[]{:S(2)}) async-start(bf16[32,128,128]{2,1,0:T(8,128)(2,1)} %gather_fusion.4), calls=%async_computation.2 | async-start | bytes 2097152 | tf_op jit(solution)/shard_map/all_to_all | solution.py:135
  118.9 30.6 %copy-start.2 = (bf16[1536,64]{0,1:T(8,128)(2,1)S(1)}, bf16[1536,64]{0,1:T(8,128)(2,1)}, u32[]{:S(2)}) copy-start(bf16[1536,64]{0,1:T(8,128)(2,1)} %param.10) | copy-start | bytes 589828
  121.5 28.4 %copy-start.3 = (bf16[1536,64]{0,1:T(8,128)(2,1)S(1)}, bf16[1536,64]{0,1:T(8,128)(2,1)}, u32[]{:S(2)}) copy-start(bf16[1536,64]{0,1:T(8,128)(2,1)} %param.11) | copy-start | bytes 589828
  121.5 26.4 %collective-permute-start.1 = (f32[2,128,128]{2,0,1:T(2,128)}, f32[2,128,128]{2,0,1:T(2,128)}, u32[]{:S(2)}, u32[]{:S(2)}) collective-permute-start(f32[2,128,128]{2,0,1:T(2,128)} %fusion.17), channel_id=1, source_target_pairs={{0,16},{16,0},{1,17},{17,1},{2,18},{18,2},{3,19},{19,3},{4,20},{20... | collective-permute-start | bytes 393224 | tf_op jit(solution)/shard_map/ppermute | solution.py:134
  150.8 6.7 %collective-permute-start.2 = (bf16[128,1536]{1,0:T(8,128)(2,1)S(1)}, bf16[128,1536]{1,0:T(8,128)(2,1)S(1)}, u32[]{:S(2)}, u32[]{:S(2)}) collective-permute-start(bf16[128,1536]{1,0:T(8,128)(2,1)S(1)} %select_convert_fusion), channel_id=1, source_target_pairs={{0,1},{1,0},{2,3},{3,2},{4,5},{5,4},{6,7},{7,6},{8,9},{9,8},{10,11... | collective-permute-start | bytes 1179656 | tf_op jit(solution)/shard_map/ppermute | solution.py:58
  157.6 14.7 %collective-permute-start.3 = (bf16[64,1536]{1,0:T(8,128)(2,1)S(1)}, bf16[64,1536]{1,0:T(8,128)(2,1)S(1)}, u32[]{:S(2)}, u32[]{:S(2)}) collective-permute-start(bf16[64,1536]{1,0:T(8,128)(2,1)S(1)} %select_convert_fusion.1), channel_id=1, source_target_pairs={{0,2},{1,3},{2,0},{3,1},{4,6},{5,7},{6,4},{7,5},{8,10},{9,11},{10,... | collective-permute-start | bytes 589832 | tf_op jit(solution)/shard_map/ppermute | solution.py:58
  172.3 7.7 %collective-permute-start.4 = (bf16[32,1536]{1,0:T(8,128)(2,1)S(1)}, bf16[32,1536]{1,0:T(8,128)(2,1)S(1)}, u32[]{:S(2)}, u32[]{:S(2)}) collective-permute-start(bf16[32,1536]{1,0:T(8,128)(2,1)S(1)} %select_convert_fusion.2), channel_id=1, source_target_pairs={{0,4},{1,5},{2,6},{3,7},{4,0},{5,1},{6,2},{7,3},{8,12},{9,13},{10,... | collective-permute-start | bytes 294920 | tf_op jit(solution)/shard_map/ppermute | solution.py:58
  180.1 8.8 %collective-permute-start.5 = (bf16[16,1536]{1,0:T(8,128)(2,1)S(1)}, bf16[16,1536]{1,0:T(8,128)(2,1)S(1)}, u32[]{:S(2)}, u32[]{:S(2)}) collective-permute-start(bf16[16,1536]{1,0:T(8,128)(2,1)S(1)} %select_convert_fusion.3), channel_id=1, source_target_pairs={{0,8},{1,9},{2,10},{3,11},{4,12},{5,13},{6,14},{7,15},{8,0},{9,1},... | collective-permute-start | bytes 147464 | tf_op jit(solution)/shard_map/ppermute | solution.py:58
  188.8 8.8 %collective-permute-start.6 = (bf16[16,1536]{1,0:T(8,128)(2,1)S(1)}, bf16[16,1536]{1,0:T(8,128)(2,1)S(1)}, u32[]{:S(2)}, u32[]{:S(2)}) collective-permute-start(bf16[16,1536]{1,0:T(8,128)(2,1)S(1)} %add_convert_fusion), channel_id=1, source_target_pairs={{0,8},{1,9},{2,10},{3,11},{4,12},{5,13},{6,14},{7,15},{8,0},{9,1},... | collective-permute-start | bytes 147464 | tf_op jit(solution)/shard_map/ppermute | solution.py:65
  197.6 6.3 %collective-permute-start.7 = (bf16[32,1536]{1,0:T(8,128)(2,1)S(1)}, bf16[32,1536]{1,0:T(8,128)(2,1)S(1)}, u32[]{:S(2)}, u32[]{:S(2)}) collective-permute-start(bf16[32,1536]{1,0:T(8,128)(2,1)S(1)} %maximum_select_fusion.3), channel_id=1, source_target_pairs={{0,4},{1,5},{2,6},{3,7},{4,0},{5,1},{6,2},{7,3},{8,12},{9,13},{10,... | collective-permute-start | bytes 294920 | tf_op jit(solution)/shard_map/ppermute | solution.py:65
  203.9 10.5 %collective-permute-start.8 = (bf16[64,1536]{1,0:T(8,128)(2,1)S(1)}, bf16[64,1536]{1,0:T(8,128)(2,1)S(1)}, u32[]{:S(2)}, u32[]{:S(2)}) collective-permute-start(bf16[64,1536]{1,0:T(8,128)(2,1)S(1)} %maximum_select_fusion.2), channel_id=1, source_target_pairs={{0,2},{1,3},{2,0},{3,1},{4,6},{5,7},{6,4},{7,5},{8,10},{9,11},{10,... | collective-permute-start | bytes 589832 | tf_op jit(solution)/shard_map/ppermute | solution.py:65
  214.5 7.7 %collective-permute-start.9 = (bf16[128,1536]{1,0:T(8,128)(2,1)S(1)}, bf16[128,1536]{1,0:T(8,128)(2,1)S(1)}, u32[]{:S(2)}, u32[]{:S(2)}) collective-permute-start(bf16[128,1536]{1,0:T(8,128)(2,1)S(1)} %maximum_select_fusion.1), channel_id=1, source_target_pairs={{0,1},{1,0},{2,3},{3,2},{4,5},{5,4},{6,7},{7,6},{8,9},{9,8},{10,11... | collective-permute-start | bytes 1179656 | tf_op jit(solution)/shard_map/ppermute | solution.py:65

commit v13 on v12

--- a/solution.py
+++ b/solution.py
@@ -103,7 +103,8 @@
     owner_ids = (own_ids // owned).reshape(-1)
     owner_column = owner_ids // side_count
     from_near = owner_ids % side_count == my_side
-    fetched = jnp.where(from_near[:, None, None], near[owner_column], far[owner_column])
+    near_picked = lax.optimization_barrier(near[owner_column])
+    fetched = jnp.where(from_near[:, None, None], near_picked, far[owner_column])
     fetched = fetched.reshape(owned, per_reader, 2, head_count, HD, SPAN)
     query_rows = jnp.transpose(queries_t.reshape(head_count, HD, owned, SPAN), (2, 0, 1, 3))
     dout_rows = jnp.transpose(dout_t.reshape(head_count, HD, owned, SPAN), (2, 0, 1, 3))

time: 225 us -> 224 us (level)
  no operation moved by 1% of the time
where the time goes in v13:
time: 224 us; the launch traced here: 223 us
  starting transfers between devices  125 us (56%)
  waiting for transfers between devices  65.8 us (29%)
  matrix products  14.1 us (6%)
  local copies, waits for them, and re-layouts  12.8 us (6%)
  other arithmetic  5.57 us (2%)
    ppermute x4, starting transfers between devices, head_sum(): lax.ppermute(send.astype(jnp.bfloat16), 'tensor', [(i, i ^ step) for i in...  25.2 us
    ppermute x4, starting transfers between devices, head_sum(): got = lax.ppermute(cur, 'tensor', [(i, i ^ step) for i in range(count)])  23.7 us
    ppermute x1, starting transfers between devices, local(): other_back = lax.ppermute(other, 'zh', swap)  23.4 us
    all_to_all x1, waiting for transfers between devices, local(): lax.all_to_all(jnp.take(pair_grads, far_pair, axis=0, mode='clip'), 'tq',...  21.2 us
    all_to_all x1, waiting for transfers between devices, local(): lax.all_to_all(mirror_spans[mirror_slot], 'tq', split_axis=0, concat_axis...  19.4 us
    ppermute x1, starting transfers between devices, local(): mirror_spans = lax.ppermute(paired_spans, 'zh', swap)  19.1 us
    ppermute x4, waiting for transfers between devices, head_sum(): lax.ppermute(send.astype(jnp.bfloat16), 'tensor', [(i, i ^ step) for i in...  12.5 us
    all_to_all x1, starting transfers between devices, local(): lax.all_to_all(paired_spans[own_slot], 'tq', split_axis=0, concat_axis=0,...  10.5 us
  transfers between devices with their start and end apart: 14, of which 12 were waited for; matrix products, arithmetic and copies ran while one was open for 6% of the time, Pallas kernels for 0%

profile of v13, /device:TPU:1, one launch (start us, length us, event | category | flops | bytes accessed | tf_op | source)
XLA Modules:
  0.0 223.4 jit_solution(5110754689418546024)
XLA Ops:
  6.5 10.5 %all-to-all-start = ((bf16[32,128,128]{2,1,0:T(8,128)(2,1)}), bf16[32,128,128]{2,1,0:T(8,128)(2,1)S(1)}, u32[]{:S(2)}, u32[]{:S(2)}) async-start(bf16[32,128,128]{2,1,0:T(8,128)(2,1)} %gather_fusion), calls=%async_computation | async-start | bytes 2097152 | tf_op jit(solution)/shard_map/all_to_all | solution.py:100
  17.0 19.1 %collective-permute-start = (bf16[2,128,128]{2,1,0:T(8,128)(2,1)S(1)}, bf16[2,128,128]{2,1,0:T(8,128)(2,1)S(1)}, u32[]{:S(2)}, u32[]{:S(2)}) collective-permute-start(bf16[2,128,128]{2,1,0:T(8,128)(2,1)S(1)} %bitcast_bitcast_fusion), channel_id=1, source_target_pairs={{0,16},{16,0},{1,17},{17,1},{2,18},{18,2},{3,19},{19,3},{4,20},{20... | collective-permute-start | bytes 196616 | tf_op jit(solution)/shard_map/ppermute | solution.py:91
  36.1 1.8 collective-permute-done
  39.5 9.5 %all-to-all-start.1 = ((bf16[32,128,128]{2,1,0:T(8,128)(2,1)}), bf16[32,128,128]{2,1,0:T(8,128)(2,1)S(1)}, u32[]{:S(2)}, u32[]{:S(2)}) async-start(bf16[32,128,128]{2,1,0:T(8,128)(2,1)} %gather_fusion.2), calls=%async_computation.1 | async-start | bytes 2097152 | tf_op jit(solution)/shard_map/all_to_all | solution.py:101
  53.4 19.4 %all-to-all-done.1 = bf16[32,128,128]{2,1,0:T(8,128)(2,1)S(1)} async-done(((bf16[32,128,128]{2,1,0:T(8,128)(2,1)}), bf16[32,128,128]{2,1,0:T(8,128)(2,1)S(1)}, u32[]{:S(2)}, u32[]{:S(2)}) %all-to-all-start.1) | async-done | bytes 1048608 | tf_op jit(solution)/shard_map/all_to_all | solution.py:101
  74.5 1.7 broadcast_select_fusion
  81.7 6.7 %all-to-all-start.3 = ((bf16[32,128,128]{2,1,0:T(8,128)(2,1)}), bf16[32,128,128]{2,1,0:T(8,128)(2,1)}, u32[]{:S(2)}, u32[]{:S(2)}) async-start(bf16[32,128,128]{2,1,0:T(8,128)(2,1)} %gather_fusion.5), calls=%async_computation.3 | async-start | bytes 2097152 | tf_op jit(solution)/shard_map/all_to_all | solution.py:125
  89.1 1.7 gather_fusion.4
  90.8 21.2 %all-to-all-done.3 = bf16[32,128,128]{2,1,0:T(8,128)(2,1)} async-done(((bf16[32,128,128]{2,1,0:T(8,128)(2,1)}), bf16[32,128,128]{2,1,0:T(8,128)(2,1)}, u32[]{:S(2)}, u32[]{:S(2)}) %all-to-all-start.3) | async-done | bytes 1048608 | tf_op jit(solution)/shard_map/all_to_all | solution.py:125
  112.0 6.5 %all-to-all-start.2 = ((bf16[32,128,128]{2,1,0:T(8,128)(2,1)}), bf16[32,128,128]{2,1,0:T(8,128)(2,1)S(1)}, u32[]{:S(2)}, u32[]{:S(2)}) async-start(bf16[32,128,128]{2,1,0:T(8,128)(2,1)} %gather_fusion.4), calls=%async_computation.2 | async-start | bytes 2097152 | tf_op jit(solution)/shard_map/all_to_all | solution.py:136
  118.7 2.6 %fusion.17 = f32[2,128,128]{2,0,1:T(2,128)} fusion(bf16[32,128,128]{2,1,0:T(8,128)(2,1)} %all-to-all-done.3, pred[32,2,2]{0,2,1:T(4,128)(4,1)S(1)} %compare_and_fusion, s32[]{:T(128)S(6)} %select_n.250), kind=kOutput, calls=%fused_computation.34 | convolution fusion | flops 2097152 | bytes 1180164 | tf_op jit(solution)/shard_map/ck,crh->krh/dot_general | solution.py:129
  121.3 23.4 %collective-permute-start.1 = (f32[2,128,128]{2,0,1:T(2,128)}, f32[2,128,128]{2,0,1:T(2,128)}, u32[]{:S(2)}, u32[]{:S(2)}) collective-permute-start(f32[2,128,128]{2,0,1:T(2,128)} %fusion.17), channel_id=1, source_target_pairs={{0,16},{16,0},{1,17},{17,1},{2,18},{18,2},{3,19},{19,3},{4,20},{20... | collective-permute-start | bytes 393224 | tf_op jit(solution)/shard_map/ppermute | solution.py:135
  150.6 5.3 %collective-permute-start.2 = (bf16[128,1536]{1,0:T(8,128)(2,1)S(1)}, bf16[128,1536]{1,0:T(8,128)(2,1)S(1)}, u32[]{:S(2)}, u32[]{:S(2)}) collective-permute-start(bf16[128,1536]{1,0:T(8,128)(2,1)S(1)} %select_convert_fusion), channel_id=1, source_target_pairs={{0,1},{1,0},{2,3},{3,2},{4,5},{5,4},{6,7},{7,6},{8,9},{9,8},{10,11... | collective-permute-start | bytes 1179656 | tf_op jit(solution)/shard_map/ppermute | solution.py:58
  157.4 9.7 %collective-permute-start.3 = (bf16[64,1536]{1,0:T(8,128)(2,1)S(1)}, bf16[64,1536]{1,0:T(8,128)(2,1)S(1)}, u32[]{:S(2)}, u32[]{:S(2)}) collective-permute-start(bf16[64,1536]{1,0:T(8,128)(2,1)S(1)} %select_convert_fusion.1), channel_id=1, source_target_pairs={{0,2},{1,3},{2,0},{3,1},{4,6},{5,7},{6,4},{7,5},{8,10},{9,11},{10,... | collective-permute-start | bytes 589832 | tf_op jit(solution)/shard_map/ppermute | solution.py:58
  167.2 4.9 %collective-permute-done.3 = bf16[64,1536]{1,0:T(8,128)(2,1)S(1)} collective-permute-done((bf16[64,1536]{1,0:T(8,128)(2,1)S(1)}, bf16[64,1536]{1,0:T(8,128)(2,1)S(1)}, u32[]{:S(2)}, u32[]{:S(2)}) %collective-permute-start.3) | collective-permute-done | bytes 196640 | tf_op jit(solution)/shard_map/ppermute | solution.py:58
  172.1 3.1 %collective-permute-start.4 = (bf16[32,1536]{1,0:T(8,128)(2,1)S(1)}, bf16[32,1536]{1,0:T(8,128)(2,1)S(1)}, u32[]{:S(2)}, u32[]{:S(2)}) collective-permute-start(bf16[32,1536]{1,0:T(8,128)(2,1)S(1)} %select_convert_fusion.2), channel_id=1, source_target_pairs={{0,4},{1,5},{2,6},{3,7},{4,0},{5,1},{6,2},{7,3},{8,12},{9,13},{10,... | collective-permute-start | bytes 294920 | tf_op jit(solution)/shard_map/ppermute | solution.py:58
  175.2 4.6 %collective-permute-done.4 = bf16[32,1536]{1,0:T(8,128)(2,1)S(1)} collective-permute-done((bf16[32,1536]{1,0:T(8,128)(2,1)S(1)}, bf16[32,1536]{1,0:T(8,128)(2,1)S(1)}, u32[]{:S(2)}, u32[]{:S(2)}) %collective-permute-start.4) | collective-permute-done | bytes 98336 | tf_op jit(solution)/shard_map/ppermute | solution.py:58
  179.9 7.1 %collective-permute-start.5 = (bf16[16,1536]{1,0:T(8,128)(2,1)S(1)}, bf16[16,1536]{1,0:T(8,128)(2,1)S(1)}, u32[]{:S(2)}, u32[]{:S(2)}) collective-permute-start(bf16[16,1536]{1,0:T(8,128)(2,1)S(1)} %select_convert_fusion.3), channel_id=1, source_target_pairs={{0,8},{1,9},{2,10},{3,11},{4,12},{5,13},{6,14},{7,15},{8,0},{9,1},... | collective-permute-start | bytes 147464 | tf_op jit(solution)/shard_map/ppermute | solution.py:58
  188.6 7.1 %collective-permute-start.6 = (bf16[16,1536]{1,0:T(8,128)(2,1)S(1)}, bf16[16,1536]{1,0:T(8,128)(2,1)S(1)}, u32[]{:S(2)}, u32[]{:S(2)}) collective-permute-start(bf16[16,1536]{1,0:T(8,128)(2,1)S(1)} %add_convert_fusion), channel_id=1, source_target_pairs={{0,8},{1,9},{2,10},{3,11},{4,12},{5,13},{6,14},{7,15},{8,0},{9,1},... | collective-permute-start | bytes 147464 | tf_op jit(solution)/shard_map/ppermute | solution.py:65
  197.4 2.7 %collective-permute-start.7 = (bf16[32,1536]{1,0:T(8,128)(2,1)S(1)}, bf16[32,1536]{1,0:T(8,128)(2,1)S(1)}, u32[]{:S(2)}, u32[]{:S(2)}) collective-permute-start(bf16[32,1536]{1,0:T(8,128)(2,1)S(1)} %maximum_select_fusion.3), channel_id=1, source_target_pairs={{0,4},{1,5},{2,6},{3,7},{4,0},{5,1},{6,2},{7,3},{8,12},{9,13},{10,... | collective-permute-start | bytes 294920 | tf_op jit(solution)/shard_map/ppermute | solution.py:65
  200.1 3.5 %collective-permute-done.7 = bf16[32,1536]{1,0:T(8,128)(2,1)S(1)} collective-permute-done((bf16[32,1536]{1,0:T(8,128)(2,1)S(1)}, bf16[32,1536]{1,0:T(8,128)(2,1)S(1)}, u32[]{:S(2)}, u32[]{:S(2)}) %collective-permute-start.7) | collective-permute-done | bytes 98336 | tf_op jit(solution)/shard_map/ppermute | solution.py:65
  203.7 7.6 %collective-permute-start.8 = (bf16[64,1536]{1,0:T(8,128)(2,1)S(1)}, bf16[64,1536]{1,0:T(8,128)(2,1)S(1)}, u32[]{:S(2)}, u32[]{:S(2)}) collective-permute-start(bf16[64,1536]{1,0:T(8,128)(2,1)S(1)} %maximum_select_fusion.2), channel_id=1, source_target_pairs={{0,2},{1,3},{2,0},{3,1},{4,6},{5,7},{6,4},{7,5},{8,10},{9,11},{10,... | collective-permute-start | bytes 589832 | tf_op jit(solution)/shard_map/ppermute | solution.py:65
  211.3 3.0 %collective-permute-done.8 = bf16[64,1536]{1,0:T(8,128)(2,1)S(1)} collective-permute-done((bf16[64,1536]{1,0:T(8,128)(2,1)S(1)}, bf16[64,1536]{1,0:T(8,128)(2,1)S(1)}, u32[]{:S(2)}, u32[]{:S(2)}) %collective-permute-start.8) | collective-permute-done | bytes 196640 | tf_op jit(solution)/shard_map/ppermute | solution.py:65
  214.4 6.3 %collective-permute-start.9 = (bf16[128,1536]{1,0:T(8,128)(2,1)S(1)}, bf16[128,1536]{1,0:T(8,128)(2,1)S(1)}, u32[]{:S(2)}, u32[]{:S(2)}) collective-permute-start(bf16[128,1536]{1,0:T(8,128)(2,1)S(1)} %maximum_select_fusion.1), channel_id=1, source_target_pairs={{0,1},{1,0},{2,3},{3,2},{4,5},{5,4},{6,7},{7,6},{8,9},{9,8},{10,11... | collective-permute-start | bytes 1179656 | tf_op jit(solution)/shard_map/ppermute | solution.py:65
  (83 shorter events, 33.8 us)
Async XLA Ops:
  0.0 1.8 copy-start
  6.5 33.1 %all-to-all-start = ((bf16[32,128,128]{2,1,0:T(8,128)(2,1)}), bf16[32,128,128]{2,1,0:T(8,128)(2,1)S(1)}, u32[]{:S(2)}, u32[]{:S(2)}) async-start(bf16[32,128,128]{2,1,0:T(8,128)(2,1)} %gather_fusion), calls=%async_computation | async-start | bytes 2097152 | tf_op jit(solution)/shard_map/all_to_all | solution.py:100
  17.0 20.9 %collective-permute-start = (bf16[2,128,128]{2,1,0:T(8,128)(2,1)S(1)}, bf16[2,128,128]{2,1,0:T(8,128)(2,1)S(1)}, u32[]{:S(2)}, u32[]{:S(2)}) collective-permute-start(bf16[2,128,128]{2,1,0:T(8,128)(2,1)S(1)} %bitcast_bitcast_fusion), channel_id=1, source_target_pairs={{0,16},{16,0},{1,17},{17,1},{2,18},{18,2},{3,19},{19,3},{4,20},{20... | collective-permute-start | bytes 196616 | tf_op jit(solution)/shard_map/ppermute | solution.py:91
  36.1 13.1 %copy-start.5 = (bf16[64,1536]{1,0:T(8,128)(2,1)S(1)}, bf16[64,1536]{1,0:T(8,128)(2,1)}, u32[]{:S(2)}) copy-start(bf16[64,1536]{1,0:T(8,128)(2,1)} %param.12) | copy-start | bytes 589828
  39.5 11.1 %copy-start.4 = (bf16[1536,64]{0,1:T(8,128)(2,1)S(1)}, bf16[1536,64]{0,1:T(8,128)(2,1)}, u32[]{:S(2)}) copy-start(bf16[1536,64]{0,1:T(8,128)(2,1)} %param.9) | copy-start | bytes 589828
  39.5 33.4 %all-to-all-start.1 = ((bf16[32,128,128]{2,1,0:T(8,128)(2,1)}), bf16[32,128,128]{2,1,0:T(8,128)(2,1)S(1)}, u32[]{:S(2)}, u32[]{:S(2)}) async-start(bf16[32,128,128]{2,1,0:T(8,128)(2,1)} %gather_fusion.2), calls=%async_computation.1 | async-start | bytes 2097152 | tf_op jit(solution)/shard_map/all_to_all | solution.py:101
  79.0 1.0 copy-start.1
  81.7 30.3 %all-to-all-start.3 = ((bf16[32,128,128]{2,1,0:T(8,128)(2,1)}), bf16[32,128,128]{2,1,0:T(8,128)(2,1)}, u32[]{:S(2)}, u32[]{:S(2)}) async-start(bf16[32,128,128]{2,1,0:T(8,128)(2,1)} %gather_fusion.5), calls=%async_computation.3 | async-start | bytes 2097152 | tf_op jit(solution)/shard_map/all_to_all | solution.py:125
  112.0 34.3 %all-to-all-start.2 = ((bf16[32,128,128]{2,1,0:T(8,128)(2,1)}), bf16[32,128,128]{2,1,0:T(8,128)(2,1)S(1)}, u32[]{:S(2)}, u32[]{:S(2)}) async-start(bf16[32,128,128]{2,1,0:T(8,128)(2,1)} %gather_fusion.4), calls=%async_computation.2 | async-start | bytes 2097152 | tf_op jit(solution)/shard_map/all_to_all | solution.py:136
  118.7 30.6 %copy-start.2 = (bf16[1536,64]{0,1:T(8,128)(2,1)S(1)}, bf16[1536,64]{0,1:T(8,128)(2,1)}, u32[]{:S(2)}) copy-start(bf16[1536,64]{0,1:T(8,128)(2,1)} %param.10) | copy-start | bytes 589828
  121.3 28.4 %copy-start.3 = (bf16[1536,64]{0,1:T(8,128)(2,1)S(1)}, bf16[1536,64]{0,1:T(8,128)(2,1)}, u32[]{:S(2)}) copy-start(bf16[1536,64]{0,1:T(8,128)(2,1)} %param.11) | copy-start | bytes 589828
  121.3 26.4 %collective-permute-start.1 = (f32[2,128,128]{2,0,1:T(2,128)}, f32[2,128,128]{2,0,1:T(2,128)}, u32[]{:S(2)}, u32[]{:S(2)}) collective-permute-start(f32[2,128,128]{2,0,1:T(2,128)} %fusion.17), channel_id=1, source_target_pairs={{0,16},{16,0},{1,17},{17,1},{2,18},{18,2},{3,19},{19,3},{4,20},{20... | collective-permute-start | bytes 393224 | tf_op jit(solution)/shard_map/ppermute | solution.py:135
  150.6 6.7 %collective-permute-start.2 = (bf16[128,1536]{1,0:T(8,128)(2,1)S(1)}, bf16[128,1536]{1,0:T(8,128)(2,1)S(1)}, u32[]{:S(2)}, u32[]{:S(2)}) collective-permute-start(bf16[128,1536]{1,0:T(8,128)(2,1)S(1)} %select_convert_fusion), channel_id=1, source_target_pairs={{0,1},{1,0},{2,3},{3,2},{4,5},{5,4},{6,7},{7,6},{8,9},{9,8},{10,11... | collective-permute-start | bytes 1179656 | tf_op jit(solution)/shard_map/ppermute | solution.py:58
  157.4 14.6 %collective-permute-start.3 = (bf16[64,1536]{1,0:T(8,128)(2,1)S(1)}, bf16[64,1536]{1,0:T(8,128)(2,1)S(1)}, u32[]{:S(2)}, u32[]{:S(2)}) collective-permute-start(bf16[64,1536]{1,0:T(8,128)(2,1)S(1)} %select_convert_fusion.1), channel_id=1, source_target_pairs={{0,2},{1,3},{2,0},{3,1},{4,6},{5,7},{6,4},{7,5},{8,10},{9,11},{10,... | collective-permute-start | bytes 589832 | tf_op jit(solution)/shard_map/ppermute | solution.py:58
  172.1 7.7 %collective-permute-start.4 = (bf16[32,1536]{1,0:T(8,128)(2,1)S(1)}, bf16[32,1536]{1,0:T(8,128)(2,1)S(1)}, u32[]{:S(2)}, u32[]{:S(2)}) collective-permute-start(bf16[32,1536]{1,0:T(8,128)(2,1)S(1)} %select_convert_fusion.2), channel_id=1, source_target_pairs={{0,4},{1,5},{2,6},{3,7},{4,0},{5,1},{6,2},{7,3},{8,12},{9,13},{10,... | collective-permute-start | bytes 294920 | tf_op jit(solution)/shard_map/ppermute | solution.py:58
  179.9 8.7 %collective-permute-start.5 = (bf16[16,1536]{1,0:T(8,128)(2,1)S(1)}, bf16[16,1536]{1,0:T(8,128)(2,1)S(1)}, u32[]{:S(2)}, u32[]{:S(2)}) collective-permute-start(bf16[16,1536]{1,0:T(8,128)(2,1)S(1)} %select_convert_fusion.3), channel_id=1, source_target_pairs={{0,8},{1,9},{2,10},{3,11},{4,12},{5,13},{6,14},{7,15},{8,0},{9,1},... | collective-permute-start | bytes 147464 | tf_op jit(solution)/shard_map/ppermute | solution.py:58
  188.6 8.7 %collective-permute-start.6 = (bf16[16,1536]{1,0:T(8,128)(2,1)S(1)}, bf16[16,1536]{1,0:T(8,128)(2,1)S(1)}, u32[]{:S(2)}, u32[]{:S(2)}) collective-permute-start(bf16[16,1536]{1,0:T(8,128)(2,1)S(1)} %add_convert_fusion), channel_id=1, source_target_pairs={{0,8},{1,9},{2,10},{3,11},{4,12},{5,13},{6,14},{7,15},{8,0},{9,1},... | collective-permute-start | bytes 147464 | tf_op jit(solution)/shard_map/ppermute | solution.py:65
  197.4 6.3 %collective-permute-start.7 = (bf16[32,1536]{1,0:T(8,128)(2,1)S(1)}, bf16[32,1536]{1,0:T(8,128)(2,1)S(1)}, u32[]{:S(2)}, u32[]{:S(2)}) collective-permute-start(bf16[32,1536]{1,0:T(8,128)(2,1)S(1)} %maximum_select_fusion.3), channel_id=1, source_target_pairs={{0,4},{1,5},{2,6},{3,7},{4,0},{5,1},{6,2},{7,3},{8,12},{9,13},{10,... | collective-permute-start | bytes 294920 | tf_op jit(solution)/shard_map/ppermute | solution.py:65
  203.7 10.6 %collective-permute-start.8 = (bf16[64,1536]{1,0:T(8,128)(2,1)S(1)}, bf16[64,1536]{1,0:T(8,128)(2,1)S(1)}, u32[]{:S(2)}, u32[]{:S(2)}) collective-permute-start(bf16[64,1536]{1,0:T(8,128)(2,1)S(1)} %maximum_select_fusion.2), channel_id=1, source_target_pairs={{0,2},{1,3},{2,0},{3,1},{4,6},{5,7},{6,4},{7,5},{8,10},{9,11},{10,... | collective-permute-start | bytes 589832 | tf_op jit(solution)/shard_map/ppermute | solution.py:65
  214.4 7.7 %collective-permute-start.9 = (bf16[128,1536]{1,0:T(8,128)(2,1)S(1)}, bf16[128,1536]{1,0:T(8,128)(2,1)S(1)}, u32[]{:S(2)}, u32[]{:S(2)}) collective-permute-start(bf16[128,1536]{1,0:T(8,128)(2,1)S(1)} %maximum_select_fusion.1), channel_id=1, source_target_pairs={{0,1},{1,0},{2,3},{3,2},{4,5},{5,4},{6,7},{7,6},{8,9},{9,8},{10,11... | collective-permute-start | bytes 1179656 | tf_op jit(solution)/shard_map/ppermute | solution.py:65

commit v14 on v13

--- a/solution.py
+++ b/solution.py
@@ -52,9 +52,8 @@
     while step < count:
         upper = (index & step) != 0
         half = cur.shape[0] // 2
-        low, high = cur[:half], cur[half:]
-        keep = jnp.where(upper, high, low)
-        send = jnp.where(upper, low, high)
+        keep = lax.dynamic_slice_in_dim(cur, upper.astype(jnp.int32) * half, half, 0)
+        send = lax.dynamic_slice_in_dim(cur, (1 - upper.astype(jnp.int32)) * half, half, 0)
         got = lax.ppermute(send.astype(jnp.bfloat16), "tensor", [(i, i ^ step) for i in range(count)])
         cur = keep + got.astype(jnp.float32)
         step *= 2

time: 224 us -> 224 us (level)
  no operation moved by 1% of the time
where the time goes in v14:
time: 224 us; the launch traced here: 223 us
  starting transfers between devices  125 us (56%)
  waiting for transfers between devices  65.8 us (29%)
  matrix products  14.1 us (6%)
  local copies, waits for them, and re-layouts  12.9 us (6%)
  other arithmetic  5.36 us (2%)
    ppermute x4, starting transfers between devices, head_sum(): lax.ppermute(send.astype(jnp.bfloat16), 'tensor', [(i, i ^ step) for i in...  25.2 us
    ppermute x4, starting transfers between devices, head_sum(): got = lax.ppermute(cur, 'tensor', [(i, i ^ step) for i in range(count)])  23.7 us
    ppermute x1, starting transfers between devices, local(): other_back = lax.ppermute(other, 'zh', swap)  23.4 us
    all_to_all x1, waiting for transfers between devices, local(): lax.all_to_all(jnp.take(pair_grads, far_pair, axis=0, mode='clip'), 'tq',...  21.2 us
    all_to_all x1, waiting for transfers between devices, local(): lax.all_to_all(mirror_spans[mirror_slot], 'tq', split_axis=0, concat_axis...  19.4 us
    ppermute x1, starting transfers between devices, local(): mirror_spans = lax.ppermute(paired_spans, 'zh', swap)  19.1 us
    ppermute x4, waiting for transfers between devices, head_sum(): lax.ppermute(send.astype(jnp.bfloat16), 'tensor', [(i, i ^ step) for i in...  12.4 us
    all_to_all x1, starting transfers between devices, local(): lax.all_to_all(paired_spans[own_slot], 'tq', split_axis=0, concat_axis=0,...  10.5 us
  transfers between devices with their start and end apart: 14, of which 12 were waited for; matrix products, arithmetic and copies ran while one was open for 6% of the time, Pallas kernels for 0%

profile of v14, /device:TPU:1, one launch (start us, length us, event | category | flops | bytes accessed | tf_op | source)
XLA Modules:
  0.0 223.3 jit_solution(4771717081711925144)
XLA Ops:
  6.5 10.5 %all-to-all-start = ((bf16[32,128,128]{2,1,0:T(8,128)(2,1)}), bf16[32,128,128]{2,1,0:T(8,128)(2,1)S(1)}, u32[]{:S(2)}, u32[]{:S(2)}) async-start(bf16[32,128,128]{2,1,0:T(8,128)(2,1)} %gather_fusion), calls=%async_computation | async-start | bytes 2097152 | tf_op jit(solution)/shard_map/all_to_all | solution.py:99
  17.0 19.1 %collective-permute-start = (bf16[2,128,128]{2,1,0:T(8,128)(2,1)S(1)}, bf16[2,128,128]{2,1,0:T(8,128)(2,1)S(1)}, u32[]{:S(2)}, u32[]{:S(2)}) collective-permute-start(bf16[2,128,128]{2,1,0:T(8,128)(2,1)S(1)} %bitcast_bitcast_fusion), channel_id=1, source_target_pairs={{0,16},{16,0},{1,17},{17,1},{2,18},{18,2},{3,19},{19,3},{4,20},{20... | collective-permute-start | bytes 196616 | tf_op jit(solution)/shard_map/ppermute | solution.py:90
  36.1 1.8 collective-permute-done
  39.5 9.5 %all-to-all-start.1 = ((bf16[32,128,128]{2,1,0:T(8,128)(2,1)}), bf16[32,128,128]{2,1,0:T(8,128)(2,1)S(1)}, u32[]{:S(2)}, u32[]{:S(2)}) async-start(bf16[32,128,128]{2,1,0:T(8,128)(2,1)} %gather_fusion.2), calls=%async_computation.1 | async-start | bytes 2097152 | tf_op jit(solution)/shard_map/all_to_all | solution.py:100
  53.4 19.4 %all-to-all-done.1 = bf16[32,128,128]{2,1,0:T(8,128)(2,1)S(1)} async-done(((bf16[32,128,128]{2,1,0:T(8,128)(2,1)}), bf16[32,128,128]{2,1,0:T(8,128)(2,1)S(1)}, u32[]{:S(2)}, u32[]{:S(2)}) %all-to-all-start.1) | async-done | bytes 1048608 | tf_op jit(solution)/shard_map/all_to_all | solution.py:100
  74.5 1.7 broadcast_select_fusion
  81.7 6.7 %all-to-all-start.3 = ((bf16[32,128,128]{2,1,0:T(8,128)(2,1)}), bf16[32,128,128]{2,1,0:T(8,128)(2,1)}, u32[]{:S(2)}, u32[]{:S(2)}) async-start(bf16[32,128,128]{2,1,0:T(8,128)(2,1)} %gather_fusion.5), calls=%async_computation.3 | async-start | bytes 2097152 | tf_op jit(solution)/shard_map/all_to_all | solution.py:124
  89.1 1.7 gather_fusion.4
  90.8 21.2 %all-to-all-done.3 = bf16[32,128,128]{2,1,0:T(8,128)(2,1)} async-done(((bf16[32,128,128]{2,1,0:T(8,128)(2,1)}), bf16[32,128,128]{2,1,0:T(8,128)(2,1)}, u32[]{:S(2)}, u32[]{:S(2)}) %all-to-all-start.3) | async-done | bytes 1048608 | tf_op jit(solution)/shard_map/all_to_all | solution.py:124
  112.0 6.5 %all-to-all-start.2 = ((bf16[32,128,128]{2,1,0:T(8,128)(2,1)}), bf16[32,128,128]{2,1,0:T(8,128)(2,1)S(1)}, u32[]{:S(2)}, u32[]{:S(2)}) async-start(bf16[32,128,128]{2,1,0:T(8,128)(2,1)} %gather_fusion.4), calls=%async_computation.2 | async-start | bytes 2097152 | tf_op jit(solution)/shard_map/all_to_all | solution.py:135
  118.7 2.6 %fusion.17 = f32[2,128,128]{2,0,1:T(2,128)} fusion(bf16[32,128,128]{2,1,0:T(8,128)(2,1)} %all-to-all-done.3, pred[32,2,2]{0,2,1:T(4,128)(4,1)S(1)} %compare_and_fusion, s32[]{:T(128)S(6)} %select_n.214), kind=kOutput, calls=%fused_computation.34 | convolution fusion | flops 2097152 | bytes 1180164 | tf_op jit(solution)/shard_map/ck,crh->krh/dot_general | solution.py:128
  121.3 23.4 %collective-permute-start.1 = (f32[2,128,128]{2,0,1:T(2,128)}, f32[2,128,128]{2,0,1:T(2,128)}, u32[]{:S(2)}, u32[]{:S(2)}) collective-permute-start(f32[2,128,128]{2,0,1:T(2,128)} %fusion.17), channel_id=1, source_target_pairs={{0,16},{16,0},{1,17},{17,1},{2,18},{18,2},{3,19},{19,3},{4,20},{20... | collective-permute-start | bytes 393224 | tf_op jit(solution)/shard_map/ppermute | solution.py:134
  150.6 5.3 %collective-permute-start.2 = (bf16[128,1536]{1,0:T(8,128)(2,1)S(1)}, bf16[128,1536]{1,0:T(8,128)(2,1)S(1)}, u32[]{:S(2)}, u32[]{:S(2)}) collective-permute-start(bf16[128,1536]{1,0:T(8,128)(2,1)S(1)} %dynamic-slice_convert_fusion), channel_id=1, source_target_pairs={{0,1},{1,0},{2,3},{3,2},{4,5},{5,4},{6,7},{7,6},{8,9},{9,8},{10,11... | collective-permute-start | bytes 1179656 | tf_op jit(solution)/shard_map/ppermute | solution.py:57
  157.3 9.7 %collective-permute-start.3 = (bf16[64,1536]{1,0:T(8,128)(2,1)S(1)}, bf16[64,1536]{1,0:T(8,128)(2,1)S(1)}, u32[]{:S(2)}, u32[]{:S(2)}) collective-permute-start(bf16[64,1536]{1,0:T(8,128)(2,1)S(1)} %dynamic-slice_convert_fusion.1), channel_id=1, source_target_pairs={{0,2},{1,3},{2,0},{3,1},{4,6},{5,7},{6,4},{7,5},{8,10},{9,11},{10,... | collective-permute-start | bytes 589832 | tf_op jit(solution)/shard_map/ppermute | solution.py:57
  167.1 4.9 %collective-permute-done.3 = bf16[64,1536]{1,0:T(8,128)(2,1)S(1)} collective-permute-done((bf16[64,1536]{1,0:T(8,128)(2,1)S(1)}, bf16[64,1536]{1,0:T(8,128)(2,1)S(1)}, u32[]{:S(2)}, u32[]{:S(2)}) %collective-permute-start.3) | collective-permute-done | bytes 196640 | tf_op jit(solution)/shard_map/ppermute | solution.py:57
  172.1 3.1 %collective-permute-start.4 = (bf16[32,1536]{1,0:T(8,128)(2,1)S(1)}, bf16[32,1536]{1,0:T(8,128)(2,1)S(1)}, u32[]{:S(2)}, u32[]{:S(2)}) collective-permute-start(bf16[32,1536]{1,0:T(8,128)(2,1)S(1)} %dynamic-slice_convert_fusion.2), channel_id=1, source_target_pairs={{0,4},{1,5},{2,6},{3,7},{4,0},{5,1},{6,2},{7,3},{8,12},{9,13},{10,... | collective-permute-start | bytes 294920 | tf_op jit(solution)/shard_map/ppermute | solution.py:57
  175.2 4.6 %collective-permute-done.4 = bf16[32,1536]{1,0:T(8,128)(2,1)S(1)} collective-permute-done((bf16[32,1536]{1,0:T(8,128)(2,1)S(1)}, bf16[32,1536]{1,0:T(8,128)(2,1)S(1)}, u32[]{:S(2)}, u32[]{:S(2)}) %collective-permute-start.4) | collective-permute-done | bytes 98336 | tf_op jit(solution)/shard_map/ppermute | solution.py:57
  179.8 7.1 %collective-permute-start.5 = (bf16[16,1536]{1,0:T(8,128)(2,1)S(1)}, bf16[16,1536]{1,0:T(8,128)(2,1)S(1)}, u32[]{:S(2)}, u32[]{:S(2)}) collective-permute-start(bf16[16,1536]{1,0:T(8,128)(2,1)S(1)} %dynamic-slice_convert_fusion.3), channel_id=1, source_target_pairs={{0,8},{1,9},{2,10},{3,11},{4,12},{5,13},{6,14},{7,15},{8,0},{9,1},... | collective-permute-start | bytes 147464 | tf_op jit(solution)/shard_map/ppermute | solution.py:57
  188.5 7.1 %collective-permute-start.6 = (bf16[16,1536]{1,0:T(8,128)(2,1)S(1)}, bf16[16,1536]{1,0:T(8,128)(2,1)S(1)}, u32[]{:S(2)}, u32[]{:S(2)}) collective-permute-start(bf16[16,1536]{1,0:T(8,128)(2,1)S(1)} %add_convert_fusion), channel_id=1, source_target_pairs={{0,8},{1,9},{2,10},{3,11},{4,12},{5,13},{6,14},{7,15},{8,0},{9,1},... | collective-permute-start | bytes 147464 | tf_op jit(solution)/shard_map/ppermute | solution.py:64
  197.3 2.7 %collective-permute-start.7 = (bf16[32,1536]{1,0:T(8,128)(2,1)S(1)}, bf16[32,1536]{1,0:T(8,128)(2,1)S(1)}, u32[]{:S(2)}, u32[]{:S(2)}) collective-permute-start(bf16[32,1536]{1,0:T(8,128)(2,1)S(1)} %maximum_select_fusion.3), channel_id=1, source_target_pairs={{0,4},{1,5},{2,6},{3,7},{4,0},{5,1},{6,2},{7,3},{8,12},{9,13},{10,... | collective-permute-start | bytes 294920 | tf_op jit(solution)/shard_map/ppermute | solution.py:64
  200.0 3.5 %collective-permute-done.7 = bf16[32,1536]{1,0:T(8,128)(2,1)S(1)} collective-permute-done((bf16[32,1536]{1,0:T(8,128)(2,1)S(1)}, bf16[32,1536]{1,0:T(8,128)(2,1)S(1)}, u32[]{:S(2)}, u32[]{:S(2)}) %collective-permute-start.7) | collective-permute-done | bytes 98336 | tf_op jit(solution)/shard_map/ppermute | solution.py:64
  203.6 7.6 %collective-permute-start.8 = (bf16[64,1536]{1,0:T(8,128)(2,1)S(1)}, bf16[64,1536]{1,0:T(8,128)(2,1)S(1)}, u32[]{:S(2)}, u32[]{:S(2)}) collective-permute-start(bf16[64,1536]{1,0:T(8,128)(2,1)S(1)} %maximum_select_fusion.2), channel_id=1, source_target_pairs={{0,2},{1,3},{2,0},{3,1},{4,6},{5,7},{6,4},{7,5},{8,10},{9,11},{10,... | collective-permute-start | bytes 589832 | tf_op jit(solution)/shard_map/ppermute | solution.py:64
  211.2 3.0 %collective-permute-done.8 = bf16[64,1536]{1,0:T(8,128)(2,1)S(1)} collective-permute-done((bf16[64,1536]{1,0:T(8,128)(2,1)S(1)}, bf16[64,1536]{1,0:T(8,128)(2,1)S(1)}, u32[]{:S(2)}, u32[]{:S(2)}) %collective-permute-start.8) | collective-permute-done | bytes 196640 | tf_op jit(solution)/shard_map/ppermute | solution.py:64
  214.3 6.3 %collective-permute-start.9 = (bf16[128,1536]{1,0:T(8,128)(2,1)S(1)}, bf16[128,1536]{1,0:T(8,128)(2,1)S(1)}, u32[]{:S(2)}, u32[]{:S(2)}) collective-permute-start(bf16[128,1536]{1,0:T(8,128)(2,1)S(1)} %maximum_select_fusion.1), channel_id=1, source_target_pairs={{0,1},{1,0},{2,3},{3,2},{4,5},{5,4},{6,7},{7,6},{8,9},{9,8},{10,11... | collective-permute-start | bytes 1179656 | tf_op jit(solution)/shard_map/ppermute | solution.py:64
  (83 shorter events, 33.7 us)
Async XLA Ops:
  0.0 1.8 copy-start
  6.5 33.1 %all-to-all-start = ((bf16[32,128,128]{2,1,0:T(8,128)(2,1)}), bf16[32,128,128]{2,1,0:T(8,128)(2,1)S(1)}, u32[]{:S(2)}, u32[]{:S(2)}) async-start(bf16[32,128,128]{2,1,0:T(8,128)(2,1)} %gather_fusion), calls=%async_computation | async-start | bytes 2097152 | tf_op jit(solution)/shard_map/all_to_all | solution.py:99
  17.0 20.9 %collective-permute-start = (bf16[2,128,128]{2,1,0:T(8,128)(2,1)S(1)}, bf16[2,128,128]{2,1,0:T(8,128)(2,1)S(1)}, u32[]{:S(2)}, u32[]{:S(2)}) collective-permute-start(bf16[2,128,128]{2,1,0:T(8,128)(2,1)S(1)} %bitcast_bitcast_fusion), channel_id=1, source_target_pairs={{0,16},{16,0},{1,17},{17,1},{2,18},{18,2},{3,19},{19,3},{4,20},{20... | collective-permute-start | bytes 196616 | tf_op jit(solution)/shard_map/ppermute | solution.py:90
  36.1 13.1 %copy-start.5 = (bf16[64,1536]{1,0:T(8,128)(2,1)S(1)}, bf16[64,1536]{1,0:T(8,128)(2,1)}, u32[]{:S(2)}) copy-start(bf16[64,1536]{1,0:T(8,128)(2,1)} %param.12) | copy-start | bytes 589828
  39.5 11.1 %copy-start.4 = (bf16[1536,64]{0,1:T(8,128)(2,1)S(1)}, bf16[1536,64]{0,1:T(8,128)(2,1)}, u32[]{:S(2)}) copy-start(bf16[1536,64]{0,1:T(8,128)(2,1)} %param.9) | copy-start | bytes 589828
  39.5 33.4 %all-to-all-start.1 = ((bf16[32,128,128]{2,1,0:T(8,128)(2,1)}), bf16[32,128,128]{2,1,0:T(8,128)(2,1)S(1)}, u32[]{:S(2)}, u32[]{:S(2)}) async-start(bf16[32,128,128]{2,1,0:T(8,128)(2,1)} %gather_fusion.2), calls=%async_computation.1 | async-start | bytes 2097152 | tf_op jit(solution)/shard_map/all_to_all | solution.py:100
  79.0 1.0 copy-start.1
  81.7 30.3 %all-to-all-start.3 = ((bf16[32,128,128]{2,1,0:T(8,128)(2,1)}), bf16[32,128,128]{2,1,0:T(8,128)(2,1)}, u32[]{:S(2)}, u32[]{:S(2)}) async-start(bf16[32,128,128]{2,1,0:T(8,128)(2,1)} %gather_fusion.5), calls=%async_computation.3 | async-start | bytes 2097152 | tf_op jit(solution)/shard_map/all_to_all | solution.py:124
  112.0 34.3 %all-to-all-start.2 = ((bf16[32,128,128]{2,1,0:T(8,128)(2,1)}), bf16[32,128,128]{2,1,0:T(8,128)(2,1)S(1)}, u32[]{:S(2)}, u32[]{:S(2)}) async-start(bf16[32,128,128]{2,1,0:T(8,128)(2,1)} %gather_fusion.4), calls=%async_computation.2 | async-start | bytes 2097152 | tf_op jit(solution)/shard_map/all_to_all | solution.py:135
  118.7 30.6 %copy-start.2 = (bf16[1536,64]{0,1:T(8,128)(2,1)S(1)}, bf16[1536,64]{0,1:T(8,128)(2,1)}, u32[]{:S(2)}) copy-start(bf16[1536,64]{0,1:T(8,128)(2,1)} %param.10) | copy-start | bytes 589828
  121.3 28.4 %copy-start.3 = (bf16[1536,64]{0,1:T(8,128)(2,1)S(1)}, bf16[1536,64]{0,1:T(8,128)(2,1)}, u32[]{:S(2)}) copy-start(bf16[1536,64]{0,1:T(8,128)(2,1)} %param.11) | copy-start | bytes 589828
  121.3 26.4 %collective-permute-start.1 = (f32[2,128,128]{2,0,1:T(2,128)}, f32[2,128,128]{2,0,1:T(2,128)}, u32[]{:S(2)}, u32[]{:S(2)}) collective-permute-start(f32[2,128,128]{2,0,1:T(2,128)} %fusion.17), channel_id=1, source_target_pairs={{0,16},{16,0},{1,17},{17,1},{2,18},{18,2},{3,19},{19,3},{4,20},{20... | collective-permute-start | bytes 393224 | tf_op jit(solution)/shard_map/ppermute | solution.py:134
  150.6 6.7 %collective-permute-start.2 = (bf16[128,1536]{1,0:T(8,128)(2,1)S(1)}, bf16[128,1536]{1,0:T(8,128)(2,1)S(1)}, u32[]{:S(2)}, u32[]{:S(2)}) collective-permute-start(bf16[128,1536]{1,0:T(8,128)(2,1)S(1)} %dynamic-slice_convert_fusion), channel_id=1, source_target_pairs={{0,1},{1,0},{2,3},{3,2},{4,5},{5,4},{6,7},{7,6},{8,9},{9,8},{10,11... | collective-permute-start | bytes 1179656 | tf_op jit(solution)/shard_map/ppermute | solution.py:57
  157.3 14.6 %collective-permute-start.3 = (bf16[64,1536]{1,0:T(8,128)(2,1)S(1)}, bf16[64,1536]{1,0:T(8,128)(2,1)S(1)}, u32[]{:S(2)}, u32[]{:S(2)}) collective-permute-start(bf16[64,1536]{1,0:T(8,128)(2,1)S(1)} %dynamic-slice_convert_fusion.1), channel_id=1, source_target_pairs={{0,2},{1,3},{2,0},{3,1},{4,6},{5,7},{6,4},{7,5},{8,10},{9,11},{10,... | collective-permute-start | bytes 589832 | tf_op jit(solution)/shard_map/ppermute | solution.py:57
  172.1 7.7 %collective-permute-start.4 = (bf16[32,1536]{1,0:T(8,128)(2,1)S(1)}, bf16[32,1536]{1,0:T(8,128)(2,1)S(1)}, u32[]{:S(2)}, u32[]{:S(2)}) collective-permute-start(bf16[32,1536]{1,0:T(8,128)(2,1)S(1)} %dynamic-slice_convert_fusion.2), channel_id=1, source_target_pairs={{0,4},{1,5},{2,6},{3,7},{4,0},{5,1},{6,2},{7,3},{8,12},{9,13},{10,... | collective-permute-start | bytes 294920 | tf_op jit(solution)/shard_map/ppermute | solution.py:57
  179.8 8.7 %collective-permute-start.5 = (bf16[16,1536]{1,0:T(8,128)(2,1)S(1)}, bf16[16,1536]{1,0:T(8,128)(2,1)S(1)}, u32[]{:S(2)}, u32[]{:S(2)}) collective-permute-start(bf16[16,1536]{1,0:T(8,128)(2,1)S(1)} %dynamic-slice_convert_fusion.3), channel_id=1, source_target_pairs={{0,8},{1,9},{2,10},{3,11},{4,12},{5,13},{6,14},{7,15},{8,0},{9,1},... | collective-permute-start | bytes 147464 | tf_op jit(solution)/shard_map/ppermute | solution.py:57
  188.5 8.7 %collective-permute-start.6 = (bf16[16,1536]{1,0:T(8,128)(2,1)S(1)}, bf16[16,1536]{1,0:T(8,128)(2,1)S(1)}, u32[]{:S(2)}, u32[]{:S(2)}) collective-permute-start(bf16[16,1536]{1,0:T(8,128)(2,1)S(1)} %add_convert_fusion), channel_id=1, source_target_pairs={{0,8},{1,9},{2,10},{3,11},{4,12},{5,13},{6,14},{7,15},{8,0},{9,1},... | collective-permute-start | bytes 147464 | tf_op jit(solution)/shard_map/ppermute | solution.py:64
  197.3 6.3 %collective-permute-start.7 = (bf16[32,1536]{1,0:T(8,128)(2,1)S(1)}, bf16[32,1536]{1,0:T(8,128)(2,1)S(1)}, u32[]{:S(2)}, u32[]{:S(2)}) collective-permute-start(bf16[32,1536]{1,0:T(8,128)(2,1)S(1)} %maximum_select_fusion.3), channel_id=1, source_target_pairs={{0,4},{1,5},{2,6},{3,7},{4,0},{5,1},{6,2},{7,3},{8,12},{9,13},{10,... | collective-permute-start | bytes 294920 | tf_op jit(solution)/shard_map/ppermute | solution.py:64
  203.6 10.6 %collective-permute-start.8 = (bf16[64,1536]{1,0:T(8,128)(2,1)S(1)}, bf16[64,1536]{1,0:T(8,128)(2,1)S(1)}, u32[]{:S(2)}, u32[]{:S(2)}) collective-permute-start(bf16[64,1536]{1,0:T(8,128)(2,1)S(1)} %maximum_select_fusion.2), channel_id=1, source_target_pairs={{0,2},{1,3},{2,0},{3,1},{4,6},{5,7},{6,4},{7,5},{8,10},{9,11},{10,... | collective-permute-start | bytes 589832 | tf_op jit(solution)/shard_map/ppermute | solution.py:64
  214.3 7.7 %collective-permute-start.9 = (bf16[128,1536]{1,0:T(8,128)(2,1)S(1)}, bf16[128,1536]{1,0:T(8,128)(2,1)S(1)}, u32[]{:S(2)}, u32[]{:S(2)}) collective-permute-start(bf16[128,1536]{1,0:T(8,128)(2,1)S(1)} %maximum_select_fusion.1), channel_id=1, source_target_pairs={{0,1},{1,0},{2,3},{3,2},{4,5},{5,4},{6,7},{7,6},{8,9},{9,8},{10,11... | collective-permute-start | bytes 1179656 | tf_op jit(solution)/shard_map/ppermute | solution.py:64
